TPU v7x, 128 devices: a whole 4x4x4 slice. The times are simulated.
128 devices in a mesh: dp: 4 (over y), tensor: 32 (over x, z, core).
Axes of the slice: x: 4, y: 4, z: 4, core: 2. Of those that a mesh axis runs over, the one named last changes fastest.
Arguments:
- page_pool: bfloat16 [768, 1024, 256], P('dp', 'tensor'), may hold values from -5 to 5
- page_table: int32 [16, 64], P('dp'), may hold values from 0 to 191, as said below
- destination: int32 [16], replicated, may hold values from 0 to 15, as said below
- cache_len: int32 [16], replicated, may hold values from 2048 to 4096, as said below
- new_tokens: bfloat16 [16, 8192, 384], P('dp', 'tensor'), may hold values from -32 to 32
- residual_in: bfloat16 [8192, 2048], P(('dp', 'tensor')), may hold values from -48 to 48
- out_weight: bfloat16 [2048, 2048], P('tensor'), may hold values from -0.5 to 0.5
- norm_gain: float32 [2048], replicated, may hold values from 0.5 to 1.5
- routes: int32 [8192, 6], P(('dp', 'tensor')), may hold values from 0 to 63, all different within a row; in each aligned block of 64 rows (0 to 63, 64 to 127, ...) at most 8 rows name the same one
- route_gates: float32 [8192, 6], P(('dp', 'tensor')), may hold values from 0.1 to 1
- expert_gate: bfloat16 [64, 2048, 1408], P('tensor', None, 'dp'), may hold values from -0.125 to 0.125
- expert_up: bfloat16 [64, 2048, 1408], P('tensor', None, 'dp'), may hold values from -0.125 to 0.125
- expert_down: bfloat16 [64, 1408, 2048], P('tensor', 'dp'), may hold values from -0.15625 to 0.15625
Outputs:
- layer_out: float32 [8192, 2048], P(('dp', 'tensor'))
Inputs may be any that keep to these rules, and one draw needn't show every extreme that they name: `page_table`: each request names pages of its own dp index's pool of 192 pages; requests 2m and 2m + 1 of a dp index share the first half of their 64 pages, and no other page is named twice within a dp index. `destination`: A permutation of the serving slots; each dp index sends exactly one of its 4 requests to a slot of each other dp index and keeps the others in their own slots. `cache_len`: some request has exactly 4096 cached positions. `routes`: in the rows of one device (64 tokens) no expert is named more than 8 times.
All inputs are finite; a program needn't handle non-finite values.
Results may differ from a plain program's by a relative error of at most 0.004.
Values may be sent and summed in bfloat16 or wider, within the bound.
No kernel may reach another device: no remote copies, remote signals or barrier semaphores. Data moves between devices by JAX's collectives and lax.ppermute only.
A program may use at most 128 MiB of HBM per device.

v0:
```python
import jax
import jax.numpy as jnp
from jax import lax
from jax.sharding import PartitionSpec as P

HEADS = 16
HD = 128
EXPERTS = 64
TOP = 6
PAGE = 64


def swapped(array, axis, stride):
    return lax.ppermute(array, axis, [(i, i ^ 1 << stride) for i in range(lax.axis_size(axis))])


def local_attention(queries, cached, fresh_rows, length, cache_offset, span_offset):
    head_size = queries.shape[1]
    span_len = queries.shape[0]
    page_count = cached.shape[0]
    page_rows = cached.shape[1]
    scale_factor = 1.0 / head_size**0.5
    cache_scores = jnp.einsum(
        "qd,pjd->qpj", queries, cached[:, :, :head_size], preferred_element_type=jnp.float32
    )
    cache_scores = cache_scores.reshape(span_len, page_count * page_rows) * scale_factor
    page_ids = jnp.arange(page_count, dtype=jnp.int32)[:, None]
    row_ids = jnp.arange(page_rows, dtype=jnp.int32)[None, :]
    positions = (page_ids * PAGE + cache_offset + row_ids).reshape(-1)
    cache_scores = jnp.where(positions[None, :] < length, cache_scores, -1e30)
    new_keys = fresh_rows[:, head_size : 2 * head_size]
    new_values = fresh_rows[:, 2 * head_size :]
    span_scores = jnp.dot(queries, new_keys.T, preferred_element_type=jnp.float32) * scale_factor
    key_pos = span_offset + jnp.arange(fresh_rows.shape[0], dtype=jnp.int32)
    query_pos = jnp.arange(span_len, dtype=jnp.int32)
    span_scores = jnp.where(key_pos[None, :] <= query_pos[:, None], span_scores, -1e30)
    maximum = jnp.maximum(jnp.max(cache_scores, axis=1), jnp.max(span_scores, axis=1))
    cache_weights = jnp.exp(cache_scores - maximum[:, None])
    span_weights = jnp.exp(span_scores - maximum[:, None])
    denominator = jnp.sum(cache_weights, axis=1) + jnp.sum(span_weights, axis=1)
    rounded = cache_weights.astype(jnp.bfloat16).reshape(span_len, page_count, page_rows)
    weighted = jnp.einsum(
        "qpj,pjd->qd", rounded, cached[:, :, head_size:], preferred_element_type=jnp.float32
    )
    weighted = weighted + jnp.dot(
        span_weights.astype(jnp.bfloat16), new_values, preferred_element_type=jnp.float32
    )
    return (weighted, maximum, denominator)


def run_experts(slot_rows, expert_gate, expert_up, expert_down):
    gate_part = jnp.einsum(
        "secd,edf->secf", slot_rows, expert_gate, preferred_element_type=jnp.float32
    )
    up_part = jnp.einsum("secd,edf->secf", slot_rows, expert_up, preferred_element_type=jnp.float32)
    active = (jax.nn.silu(gate_part) * up_part).astype(jnp.bfloat16)
    return jnp.einsum("secf,efd->secd", active, expert_down, preferred_element_type=jnp.float32)


def shards(
    page_pool,
    page_table,
    destination,
    cache_len,
    new_tokens,
    residual_in,
    out_weight,
    norm_gain,
    routes,
    route_gates,
    expert_gate,
    expert_up,
    expert_down,
):
    tensor_size = lax.axis_size("tensor")
    group_count = lax.axis_size("dp")
    split_ways = max(1, tensor_size // HEADS)
    heads_here = max(1, HEADS // tensor_size)
    side_index = lax.axis_index("tensor") % split_ways
    group_index = lax.axis_index("dp")
    requests_here = page_table.shape[0]
    first_home = group_index * requests_here
    home_dest = lax.dynamic_slice_in_dim(destination, first_home, requests_here)
    dest_group = home_dest // requests_here
    group_ids = jnp.arange(group_count, dtype=jnp.int32)
    request_ids = jnp.arange(requests_here, dtype=jnp.int32)
    leaving = dest_group[None, :] == group_ids[:, None]
    chosen = jnp.sum(jnp.where(leaving, request_ids[None, :], 0), axis=1)
    chosen = jnp.where(group_ids == group_index, 0, chosen)
    outgoing = page_pool[page_table[chosen]]
    arrived = lax.all_to_all(outgoing, "dp", split_axis=0, concat_axis=0, tiled=True)
    inverse = (
        jnp.zeros_like(destination)
        .at[destination]
        .set(jnp.arange(destination.shape[0], dtype=jnp.int32))
    )
    served = lax.dynamic_slice_in_dim(inverse, first_home, requests_here)
    source = served // requests_here
    resident = source == group_index
    local_pages = page_pool[page_table[jnp.where(resident, served - first_home, 0)]]
    dense_cache = jnp.where(resident[:, None, None, None], local_pages, arrived[source])
    lengths = cache_len[served]
    fresh_per = new_tokens.shape[1] // heads_here
    span_len = fresh_per * split_ways
    rows_per_head = dense_cache.shape[2] // heads_here
    own_queries = new_tokens[:, :, :HD]
    other_queries = swapped(own_queries, "tensor", 0)
    lower_half = jnp.where(side_index == 0, own_queries, other_queries)
    upper_half = jnp.where(side_index == 0, other_queries, own_queries)
    queries = jnp.concatenate([lower_half, upper_half], axis=1)[:, None]

    def one_request(operands):
        return local_attention(
            operands[0],
            operands[1],
            operands[2],
            operands[3],
            side_index * rows_per_head,
            side_index * fresh_per,
        )

    head_results = lax.map(one_request, (queries[:, 0], dense_cache, new_tokens, lengths))
    weighted, maximum, denominator = head_results
    half_dim = HD // 2
    given_part = lax.dynamic_slice_in_dim(weighted, (1 - side_index) * half_dim, half_dim, 2)
    kept_part = lax.dynamic_slice_in_dim(weighted, side_index * half_dim, half_dim, 2)
    received_part, other_max, other_den = swapped((given_part, maximum, denominator), "tensor", 0)
    joint_max = jnp.maximum(maximum, other_max)
    own_scale = jnp.exp(maximum - joint_max)
    theirs = jnp.exp(other_max - joint_max)
    combined = kept_part * own_scale[..., None] + received_part * theirs[..., None]
    attended = combined / (denominator * own_scale + other_den * theirs)[..., None]
    head_out = attended.astype(jnp.bfloat16).reshape(requests_here * span_len, half_dim)
    tok_rows = residual_in.shape[0]
    projected = lax.psum_scatter(
        jnp.dot(head_out, out_weight, preferred_element_type=jnp.float32),
        "tensor",
        scatter_dimension=0,
        tiled=True,
    )
    hidden = residual_in.astype(jnp.float32) + projected
    normed = (
        hidden * lax.rsqrt(jnp.mean(hidden * hidden, axis=1, keepdims=True) + 1e-06) * norm_gain
    ).astype(jnp.bfloat16)
    capacity = max(2, tok_rows * TOP * 4 // (3 * EXPERTS))
    flat_routes = routes.reshape(-1)
    pair_count = flat_routes.shape[0]
    expert_ids = jnp.arange(EXPERTS, dtype=jnp.int32)
    one_hot = (flat_routes[:, None] == expert_ids[None, :]).astype(jnp.int32)
    earlier = jnp.cumsum(one_hot, axis=0) - one_hot
    rank_in_expert = jnp.sum(earlier * one_hot, axis=1)
    slot_of_pair = flat_routes * capacity + rank_in_expert
    slot_ids = jnp.arange(EXPERTS * capacity, dtype=jnp.int32)
    matches = slot_of_pair[None, :] == slot_ids[:, None]
    source_pair = jnp.sum(
        jnp.where(matches, jnp.arange(pair_count, dtype=jnp.int32)[None, :], 0), axis=1
    )
    filled = jnp.any(matches, axis=1)
    outgoing_rows = jnp.where(
        filled[:, None], normed[source_pair // TOP], jnp.zeros((), jnp.bfloat16)
    )
    experts_here = expert_gate.shape[0]
    width = normed.shape[1]
    outgoing_rows = outgoing_rows.reshape(tensor_size, experts_here, capacity, width)
    fanned = jnp.broadcast_to(outgoing_rows[None], (group_count,) + outgoing_rows.shape)
    fanned = fanned.reshape((group_count * tensor_size,) + outgoing_rows.shape[1:])
    partial_value = run_experts(
        lax.all_to_all(fanned, ("dp", "tensor"), split_axis=0, concat_axis=0, tiled=True),
        expert_gate,
        expert_up,
        expert_down,
    ).astype(jnp.bfloat16)
    returned = lax.all_to_all(
        partial_value, ("dp", "tensor"), split_axis=0, concat_axis=0, tiled=True
    )
    slot_out = jnp.sum(
        returned.reshape(group_count, EXPERTS * capacity, width).astype(jnp.float32), axis=0
    )
    picked = slot_out[slot_of_pair].reshape(tok_rows, TOP, width)
    routed = jnp.sum(picked * route_gates[:, :, None], axis=1)
    return hidden + routed


def solution(mesh):
    return jax.shard_map(
        shards,
        mesh=mesh,
        in_specs=(
            P("dp", "tensor", None),
            P("dp", None),
            P(),
            P(),
            P("dp", "tensor", None),
            P(("dp", "tensor"), None),
            P("tensor", None),
            P(),
            P(("dp", "tensor"), None),
            P(("dp", "tensor"), None),
            P("tensor", None, "dp"),
            P("tensor", None, "dp"),
            P("tensor", "dp", None),
        ),
        out_specs=P(("dp", "tensor"), None),
        check_vma=False,
    )
```

profile of v0, /device:TPU:0, one launch (start us, length us, event | category | flops | bytes accessed | tf_op | source)
XLA Modules:
  0.0 557.0 jit_solution(8694701867707541910)
XLA Ops:
  10.2 2.8 gather_fusion.4
  13.0 5.0 all-to-all-start
  19.9 2.8 gather_fusion.2
  25.3 41.9 %all-to-all-done = bf16[4,64,32,256]{3,2,1,0:T(8,128)(2,1)} async-done(((bf16[4,64,32,256]{3,2,1,0:T(8,128)(2,1)}), bf16[4,64,32,256]{3,2,1,0:T(8,128)(2,1)}, u32[]{:S(2)}, u32[]{:S(2)}) %all-to-all-start) | async-done | bytes 4194336 | tf_op jit(solution)/shard_map/all_to_all | solution.py:91
  67.2 5.0 gather_fusion.5
  72.2 5.9 %broadcast_select_fusion = bf16[4,64,32,256]{3,2,1,0:T(8,128)(2,1)} fusion(bf16[4,64,32,256]{3,2,1,0:T(8,128)(2,1)} %bitcast.137, bf16[4,64,32,256]{3,2,1,0:T(8,128)(2,1)} %gather_fusion.5, pred[4]{0:T(512)(128)(4,1)S(1)} %get-tuple-element.156), kind=kLoop, calls=%fused_computation.47 | loop fusion | flops 2097152 | bytes 12582916 | tf_op jit(solution)/shard_map/jit(_where)/select_n | solution.py:101
  78.1 55.9 %while.16 = (s32[]{:T(128)}, f32[4,512,128]{1,2,0:T(8,128)}, f32[4,512]{1,0:T(4,128)S(1)}, f32[4,512]{1,0:T(4,128)S(1)}, s32[]{:T(128)}, /*index=5*/s32[4]{0:T(1...) while((s32[]{:T(128)}, f32[4,512,128]{1,2,0:T(8,128)}, ...), condition=%wide.region_7.8_spmd, body=%wide.region_2.7_spmd.sunk | while | flops 613485952 | bytes 29409492 | solution.py:122
  86.0 2.5 copy.86
  99.9 2.5 copy.86
  113.9 2.5 copy.86
  127.9 2.5 copy.86
  138.5 9.0 %fusion.52 = f32[2048,2048]{1,0:T(8,128)} fusion(bf16[2048,64]{0,1:T(8,128)(2,1)S(1)} %bitcast.140, bf16[64,2048]{1,0:T(8,128)(2,1)} %param.21), kind=kOutput, calls=%fused_computation.129 | convolution fusion | flops 536870912 | bytes 17301504 | tf_op jit(solution)/shard_map/dot_general | solution.py:136
  150.5 113.3 %reduce-scatter.2.cloned.1.call-done = f32[64,2048]{1,0:T(8,128)} async-done(((f32[2048,2048]{1,0:T(8,128)}), f32[64,2048]{1,0:T(8,128)}) %reduce-scatter.2.cloned.1.call-update) | async-done | bytes 524304 | tf_op jit(solution)/shard_map/reduce_scatter | solution.py:135
  269.9 106.1 %all_to_all.15 = bf16[128,2,8,2048]{3,2,1,0:T(8,128)(2,1)} all-to-all(bf16[128,2,8,2048]{3,2,1,0:T(8,128)(2,1)S(1)} %bitcast.135), channel_id=1, replica_groups=mesh['dp'=4,'tensor'=32] {'dp','tensor'}, dimensions={0} | all-to-all | bytes 16777216 | tf_op jit(solution)/shard_map/all_to_all | solution.py:168
  376.0 10.6 %fusion.19 = f32[2,128,8,352]{3,2,1,0:T(8,128)} fusion(bf16[128,2,8,2048]{3,2,1,0:T(8,128)(2,1)} %all_to_all.15, bf16[2,2048,352]{1,2,0:T(8,128)(2,1)} %param.26), kind=kOutput, calls=%fused_computation.42 | convolution fusion | flops 2952790016 | bytes 14155776 | tf_op jit(solution)/shard_map/secd,edf->secf/dot_general | solution.py:55
  386.5 9.0 %fusion.23 = bf16[128,2,8,352]{3,2,0,1:T(8,128)(2,1)S(1)} fusion(f32[2,128,8,352]{3,2,1,0:T(8,128)} %fusion.19, bf16[2,2048,352]{1,2,0:T(8,128)(2,1)S(1)} %copy-done.11, bf16[128,2,8,2048]{3,2,1,0:T(8,128)(2,1)} %all_to_all.15), kind=kOutput, calls=%fused_computation.49 | convolution fusion | flops 2957115392 | bytes 15597568 | tf_op jit(solution)/shard_map/secd,edf->secf/dot_general | solution.py:52
  395.5 8.7 %convert_bitcast_fusion = bf16[128,2,8,2048]{3,0,2,1:T(8,128)(2,1)} fusion(bf16[2,352,2048]{2,1,0:T(8,128)(2,1)} %param.27, bf16[128,2,8,352]{3,2,0,1:T(8,128)(2,1)S(1)} %fusion.23), kind=kOutput, calls=%fused_computation.41 | convolution fusion | flops 2956984320 | bytes 12713984 | tf_op jit(solution)/shard_map/secf,efd->secd/dot_general | solution.py:57
  404.2 11.2 %copy.62 = bf16[128,2,8,2048]{3,2,1,0:T(8,128)(2,1)} copy(bf16[128,2,8,2048]{3,0,2,1:T(8,128)(2,1)} %convert_bitcast_fusion) | data formatting | bytes 16777216 | tf_op jit(solution)/shard_map/convert_element_type | solution.py:172
  415.5 9.7 %all-to-all-start.2 = ((bf16[128,2,8,2048]{3,2,1,0:T(8,128)(2,1)}), bf16[128,2,8,2048]{3,2,1,0:T(8,128)(2,1)}, u32[]{:S(2)}, u32[]{:S(2)}) async-start(bf16[128,2,8,2048]{3,2,1,0:T(8,128)(2,1)} %copy.62), calls=%async_computation.3 | async-start | bytes 16777216 | tf_op jit(solution)/shard_map/all_to_all | solution.py:173
  425.6 99.9 %all-to-all-done.2 = bf16[128,2,8,2048]{3,2,1,0:T(8,128)(2,1)} async-done(((bf16[128,2,8,2048]{3,2,1,0:T(8,128)(2,1)}), bf16[128,2,8,2048]{3,2,1,0:T(8,128)(2,1)}, u32[]{:S(2)}, u32[]{:S(2)}) %all-to-all-start.2) | async-done | bytes 8388640 | tf_op jit(solution)/shard_map/all_to_all | solution.py:173
  525.5 7.6 %convert_reduce_fusion = f32[512,2048]{1,0:T(8,128)} fusion(bf16[4,512,2048]{2,1,0:T(8,128)(2,1)} %bitcast.34), kind=kLoop, calls=%fused_computation.40 | loop fusion | flops 7340032 | bytes 12582912 | tf_op jit(solution)/shard_map/reduce_sum | solution.py:176
  533.1 7.3 %gather_fusion.7 = f32[384,2048]{1,0:T(8,128)} fusion(f32[512,2048]{1,0:T(8,128)} %convert_reduce_fusion, s32[1024]{0:T(1024)S(1)} %pad_clamp_fusion), kind=kCustom, calls=%fused_computation.7 | custom fusion | bytes 6292992 | tf_op jit(solution)/shard_map/gather | solution.py:179
  540.4 4.8 reshape.277
  545.2 3.8 multiply_reduce_fusion
  (185 shorter events, 68.2 us)
Async XLA Ops:
  6.5 3.7 copy-start
  13.0 6.2 %copy-start.7 = (s32[4,64]{1,0:T(4,128)S(1)}, s32[4,64]{1,0:T(4,128)}, u32[]{:S(2)}) copy-start(s32[4,64]{1,0:T(4,128)} %param.16) | copy-start | bytes 3076
  13.0 54.2 %all-to-all-start = ((bf16[4,64,32,256]{3,2,1,0:T(8,128)(2,1)}), bf16[4,64,32,256]{3,2,1,0:T(8,128)(2,1)}, u32[]{:S(2)}, u32[]{:S(2)}) async-start(bf16[4,64,32,256]{3,2,1,0:T(8,128)(2,1)} %bitcast.136), calls=%async_computation | async-start | bytes 8388608 | tf_op jit(solution)/shard_map/all_to_all | solution.py:91
  18.0 245.7 %reduce-scatter.2.cloned.1.call-start = ((), (), s32[]{:S(2)}) async-start(), calls=%async_computation.4 | async-start | bytes 17301504 | tf_op jit(solution)/shard_map/reduce_scatter | solution.py:135
  19.0 4.3 collective-permute-start
  19.9 2.8 copy-start.2
  84.7 1.1 copy-start.3
  88.5 2.4 copy-start.4
  98.7 1.1 copy-start.3
  102.5 2.4 copy-start.4
  112.7 1.1 copy-start.3
  116.4 2.4 copy-start.4
  126.7 1.1 copy-start.3
  130.4 2.4 copy-start.4
  135.1 2.2 collective-permute-start.2
  135.2 1.9 collective-permute-start.1
  135.7 1.6 collective-permute-start.3
  147.6 116.1 %copy-start.6 = (bf16[64,2048]{1,0:T(8,128)(2,1)S(1)}, bf16[64,2048]{1,0:T(8,128)(2,1)}, u32[]{:S(2)}) copy-start(bf16[64,2048]{1,0:T(8,128)(2,1)} %param.20) | copy-start | bytes 786436
  147.6 117.4 %copy-start.9 = (f32[2048]{0:T(1024)S(1)}, f32[2048]{0:T(1024)}, u32[]{:S(2)}) copy-start(f32[2048]{0:T(1024)} %param.22) | copy-start | bytes 24580
  376.0 10.6 %copy-start.11 = (bf16[2,2048,352]{1,2,0:T(8,128)(2,1)S(1)}, bf16[2,2048,352]{1,2,0:T(8,128)(2,1)}, u32[]{:S(2)}) copy-start(bf16[2,2048,352]{1,2,0:T(8,128)(2,1)} %param.25) | copy-start | bytes 8650756
  415.5 10.0 %copy-start.10 = (f32[64,6]{0,1:T(8,128)S(1)}, f32[64,6]{0,1:T(8,128)}, u32[]{:S(2)}) copy-start(f32[64,6]{0,1:T(8,128)} %param.24) | copy-start | bytes 4612
  415.5 110.0 %all-to-all-start.2 = ((bf16[128,2,8,2048]{3,2,1,0:T(8,128)(2,1)}), bf16[128,2,8,2048]{3,2,1,0:T(8,128)(2,1)}, u32[]{:S(2)}, u32[]{:S(2)}) async-start(bf16[128,2,8,2048]{3,2,1,0:T(8,128)(2,1)} %copy.62), calls=%async_computation.3 | async-start | bytes 16777216 | tf_op jit(solution)/shard_map/all_to_all | solution.py:173
  540.4 9.5 %copy-start.1 = (bf16[192,32,256]{2,1,0:T(8,128)(2,1)S(1)}, bf16[192,32,256]{2,1,0:T(8,128)(2,1)}, u32[]{:S(2)}) copy-start(bf16[192,32,256]{2,1,0:T(8,128)(2,1)} %param.15) | copy-start | bytes 9437188
  545.2 3.8 copy-start.5
  (1 other events, 0.7 us)
Sparse Core Ops, SparseCore 0:
  147.7 115.9 reduce-scatter.1
where the time goes:
time: 567 us; the launch traced here: 557 us
  waiting for transfers between devices  256 us (45%)
  blocking collectives  106 us (19%)
  local copies, waits for them, and re-layouts  70.5 us (12%)
  matrix products  59.6 us (11%)
  other arithmetic  34.4 us (6%)
  starting transfers between devices  15.9 us (3%)
  between operations  13.9 us (2%)
    reduce_scatter x1, waiting for transfers between devices, shards(): lax.psum_scatter(jnp.dot(head_out, out_weight, preferred_element_type=jnp...  113 us
    all_to_all x1, blocking collectives, shards(): lax.all_to_all(fanned, ('dp', 'tensor'), split_axis=0, concat_axis=0, til...  106 us
    all_to_all x1, waiting for transfers between devices, shards(): lax.all_to_all(partial_value, ('dp', 'tensor'), split_axis=0, concat_axis...  99.9 us
    all_to_all x1, waiting for transfers between devices, shards(): lax.all_to_all(outgoing, 'dp', split_axis=0, concat_axis=0, tiled=True)  41.9 us
  transfers between devices with their start and end apart: 7, of which 5 were waited for; matrix products, arithmetic and copies ran while one was open for 2% of the time, Pallas kernels for 0%

commit v1 on v0

--- a/solution.py
+++ b/solution.py
@@ -130,14 +130,12 @@
     theirs = jnp.exp(other_max - joint_max)
     combined = kept_part * own_scale[..., None] + received_part * theirs[..., None]
     attended = combined / (denominator * own_scale + other_den * theirs)[..., None]
-    head_out = attended.astype(jnp.bfloat16).reshape(requests_here * span_len, half_dim)
     tok_rows = residual_in.shape[0]
-    projected = lax.psum_scatter(
-        jnp.dot(head_out, out_weight, preferred_element_type=jnp.float32),
-        "tensor",
-        scatter_dimension=0,
-        tiled=True,
-    )
+    head_out = attended.astype(jnp.bfloat16).reshape(tensor_size, tok_rows, half_dim)
+    owned = lax.all_to_all(head_out, "tensor", split_axis=0, concat_axis=0, tiled=True)
+    owned = owned.transpose(1, 0, 2).reshape(tok_rows, tensor_size * half_dim)
+    full_weight = lax.all_gather(out_weight, "tensor", axis=0, tiled=True)
+    projected = jnp.dot(owned, full_weight, preferred_element_type=jnp.float32)
     hidden = residual_in.astype(jnp.float32) + projected
     normed = (
         hidden * lax.rsqrt(jnp.mean(hidden * hidden, axis=1, keepdims=True) + 1e-06) * norm_gain

time: 567 us -> 457 us (0.81)
  waiting for transfers between devices: 256 us -> 150 us
  starting transfers between devices: 15.9 us -> 24.3 us
    reduce_scatter x1 -> x0, waiting for transfers between devices: 113 us -> none  [shards(): lax.psum_scatter(jnp.dot(head_out, out_weight, preferred_element_type=jnp...]
    all_to_all x0 -> x1, waiting for transfers between devices: none -> 8.7 us  [shards(): lax.all_to_all(head_out, 'tensor', split_axis=0, concat_axis=0, tiled=True)]
    all_to_all x0 -> x1, starting transfers between devices: none -> 8.48 us  [shards(): lax.all_to_all(head_out, 'tensor', split_axis=0, concat_axis=0, tiled=True)]
  transfers between devices with their start and end apart: 7 -> 8, of which waited for: 5 -> 4; matrix products, arithmetic and copies ran while one was open for 2% -> 20% of each run, Pallas kernels for 0% -> 0%
where the time goes in v1:
time: 457 us; the launch traced here: 452 us
  waiting for transfers between devices  150 us (33%)
  blocking collectives  103 us (23%)
  local copies, waits for them, and re-layouts  74.2 us (16%)
  matrix products  54.6 us (12%)
  other arithmetic  32.4 us (7%)
  starting transfers between devices  24.3 us (5%)
  between operations  13.8 us (3%)
    all_to_all x1, blocking collectives, shards(): lax.all_to_all(fanned, ('dp', 'tensor'), split_axis=0, concat_axis=0, til...  103 us
    all_to_all x1, waiting for transfers between devices, shards(): lax.all_to_all(partial_value, ('dp', 'tensor'), split_axis=0, concat_axis...  99.9 us
    all_to_all x1, waiting for transfers between devices, shards(): lax.all_to_all(outgoing, 'dp', split_axis=0, concat_axis=0, tiled=True)  39.4 us
    convert_element_type x1, local copies, waits for them, and re-layouts, shards(): partial_value = run_experts(lax.all_to_all(fanned, ('dp', 'tensor'), spli...  11.2 us
    dot_general x1, matrix products, run_experts(): jnp.einsum('secd,edf->secf', slot_rows, expert_gate, preferred_element_ty...  10.3 us
    convert_element_type x4, local copies, waits for them, and re-layouts, local_attention(): cache_weights.astype(jnp.bfloat16).reshape(span_len, page_count, page_rows)  10.2 us
    all_to_all x1, starting transfers between devices, shards(): lax.all_to_all(partial_value, ('dp', 'tensor'), split_axis=0, concat_axis...  10 us
    dot_general x4, matrix products, local_attention(): jnp.einsum('qpj,pjd->qd', rounded, cached[:, :, head_size:], preferred_el...  9.56 us
  transfers between devices with their start and end apart: 8, of which 4 were waited for; matrix products, arithmetic and copies ran while one was open for 20% of the time, Pallas kernels for 0%

profile of v1, /device:TPU:0, one launch (start us, length us, event | category | flops | bytes accessed | tf_op | source)
XLA Modules:
  0.0 452.1 jit_solution(15619407457804660873)
XLA Ops:
  11.0 2.7 gather_fusion.4
  13.8 5.1 %all-to-all-start = ((bf16[4,64,32,256]{3,2,1,0:T(8,128)(2,1)}), bf16[4,64,32,256]{3,2,1,0:T(8,128)(2,1)}, u32[]{:S(2)}, u32[]{:S(2)}) async-start(bf16[4,64,32,256]{3,2,1,0:T(8,128)(2,1)} %bitcast.135), calls=%async_computation | async-start | bytes 8388608 | tf_op jit(solution)/shard_map/all_to_all | solution.py:91
  23.2 2.8 gather_fusion.2
  28.5 39.4 %all-to-all-done = bf16[4,64,32,256]{3,2,1,0:T(8,128)(2,1)} async-done(((bf16[4,64,32,256]{3,2,1,0:T(8,128)(2,1)}), bf16[4,64,32,256]{3,2,1,0:T(8,128)(2,1)}, u32[]{:S(2)}, u32[]{:S(2)}) %all-to-all-start) | async-done | bytes 4194336 | tf_op jit(solution)/shard_map/all_to_all | solution.py:91
  67.9 4.9 %gather_fusion.5 = bf16[4,64,32,256]{3,2,1,0:T(8,128)(2,1)} fusion(bf16[4,64,32,256]{3,2,1,0:T(8,128)(2,1)} %all-to-all-done, s32[1024]{0:T(1024)S(1)} %pad_clamp_fusion.2), kind=kCustom, calls=%fused_computation.5 | custom fusion | bytes 8388624 | tf_op jit(solution)/shard_map/gather | solution.py:101
  72.9 5.9 %broadcast_select_fusion = bf16[4,64,32,256]{3,2,1,0:T(8,128)(2,1)} fusion(bf16[4,64,32,256]{3,2,1,0:T(8,128)(2,1)} %bitcast.136, bf16[4,64,32,256]{3,2,1,0:T(8,128)(2,1)} %gather_fusion.5, pred[4]{0:T(512)(128)(4,1)S(1)} %get-tuple-element.156), kind=kLoop, calls=%fused_computation.47 | loop fusion | flops 2097152 | bytes 12582916 | tf_op jit(solution)/shard_map/jit(_where)/select_n | solution.py:101
  78.8 56.5 %while.16 = (s32[]{:T(128)}, f32[4,512,128]{1,2,0:T(8,128)}, f32[4,512]{1,0:T(4,128)S(1)}, f32[4,512]{1,0:T(4,128)S(1)}, s32[]{:T(128)}, /*index=5*/s32[4]{0:T(1...) while((s32[]{:T(128)}, f32[4,512,128]{1,2,0:T(8,128)}, ...), condition=%wide.region_7.8_spmd, body=%wide.region_2.7_spmd.sunk | while | flops 613485952 | bytes 29409492 | solution.py:122
  86.7 2.6 copy.93
  100.8 2.6 copy.93
  115.0 2.6 copy.93
  141.1 8.5 %all-to-all-start.1 = ((bf16[32,2,2048]{2,1,0:T(2,128)(2,1)}), bf16[32,2,2048]{2,1,0:T(2,128)(2,1)S(1)}, u32[]{:S(2)}, u32[]{:S(2)}) async-start(bf16[32,2,2048]{2,1,0:T(2,128)(2,1)} %reshape.369), calls=%async_computation.1 | async-start | bytes 524288 | tf_op jit(solution)/shard_map/all_to_all | solution.py:135
  149.6 8.7 %all-to-all-done.1 = bf16[32,2,2048]{2,1,0:T(2,128)(2,1)S(1)} async-done(((bf16[32,2,2048]{2,1,0:T(2,128)(2,1)}), bf16[32,2,2048]{2,1,0:T(2,128)(2,1)S(1)}, u32[]{:S(2)}, u32[]{:S(2)}) %all-to-all-start.1) | async-done | bytes 262176 | tf_op jit(solution)/shard_map/all_to_all | solution.py:135
  159.5 5.1 %multiply_reduce_fusion.1 = (f32[64]{0:T(128)S(1)}, f32[64,2048]{1,0:T(8,128)S(1)}) fusion(bf16[64,2048]{1,0:T(8,128)(2,1)S(1)} %reshape.277, bf16[2048,2048]{1,0:T(8,128)(2,1)} %all-gather.2.cloned.1.call-done, bf16[64,2048]{1,0:T(8,128)(2,1)S(1)} %copy-done.8), kind=kOutput, calls=%fused_computation.66 | convolution fusion | flops 537395136 | bytes 9437440 | tf_op jit(solution)/shard_map/dot_general | solution.py:138
  169.3 102.7 %all_to_all.20 = bf16[128,2,8,2048]{3,2,1,0:T(8,128)(2,1)} all-to-all(bf16[128,2,8,2048]{3,2,1,0:T(8,128)(2,1)S(1)} %bitcast.134), channel_id=1, replica_groups=mesh['dp'=4,'tensor'=32] {'dp','tensor'}, dimensions={0} | all-to-all | bytes 16777216 | tf_op jit(solution)/shard_map/all_to_all | solution.py:166
  272.0 8.8 %fusion.19 = f32[2,128,8,352]{3,2,1,0:T(8,128)} fusion(bf16[128,2,8,2048]{3,2,1,0:T(8,128)(2,1)} %all_to_all.20, bf16[2,2048,352]{1,2,0:T(8,128)(2,1)S(1)} %copy-done.12), kind=kOutput, calls=%fused_computation.42 | convolution fusion | flops 2952790016 | bytes 14155776 | tf_op jit(solution)/shard_map/secd,edf->secf/dot_general | solution.py:55
  280.8 10.3 %fusion.23 = bf16[128,2,8,352]{3,2,0,1:T(8,128)(2,1)} fusion(f32[2,128,8,352]{3,2,1,0:T(8,128)} %fusion.19, bf16[2,2048,352]{1,2,0:T(8,128)(2,1)S(1)} %copy-done.13, bf16[128,2,8,2048]{3,2,1,0:T(8,128)(2,1)} %all_to_all.20), kind=kOutput, calls=%fused_computation.49 | convolution fusion | flops 2957115392 | bytes 15597568 | tf_op jit(solution)/shard_map/secd,edf->secf/dot_general | solution.py:52
  291.1 8.2 %convert_bitcast_fusion = bf16[128,2,8,2048]{3,0,2,1:T(8,128)(2,1)} fusion(bf16[2,352,2048]{2,1,0:T(8,128)(2,1)S(1)} %copy-done.14, bf16[128,2,8,352]{3,2,0,1:T(8,128)(2,1)} %fusion.23), kind=kOutput, calls=%fused_computation.41 | convolution fusion | flops 2956984320 | bytes 12713984 | tf_op jit(solution)/shard_map/secf,efd->secd/dot_general | solution.py:57
  299.3 11.2 %copy.68 = bf16[128,2,8,2048]{3,2,1,0:T(8,128)(2,1)} copy(bf16[128,2,8,2048]{3,0,2,1:T(8,128)(2,1)} %convert_bitcast_fusion) | data formatting | bytes 16777216 | tf_op jit(solution)/shard_map/convert_element_type | solution.py:170
  310.5 10.0 %all-to-all-start.3 = ((bf16[128,2,8,2048]{3,2,1,0:T(8,128)(2,1)}), bf16[128,2,8,2048]{3,2,1,0:T(8,128)(2,1)}, u32[]{:S(2)}, u32[]{:S(2)}) async-start(bf16[128,2,8,2048]{3,2,1,0:T(8,128)(2,1)} %copy.68), calls=%async_computation.3 | async-start | bytes 16777216 | tf_op jit(solution)/shard_map/all_to_all | solution.py:171
  320.9 99.9 %all-to-all-done.3 = bf16[128,2,8,2048]{3,2,1,0:T(8,128)(2,1)} async-done(((bf16[128,2,8,2048]{3,2,1,0:T(8,128)(2,1)}), bf16[128,2,8,2048]{3,2,1,0:T(8,128)(2,1)}, u32[]{:S(2)}, u32[]{:S(2)}) %all-to-all-start.3) | async-done | bytes 8388640 | tf_op jit(solution)/shard_map/all_to_all | solution.py:171
  420.8 7.6 %convert_reduce_fusion = f32[512,2048]{1,0:T(8,128)} fusion(bf16[4,512,2048]{2,1,0:T(8,128)(2,1)} %bitcast.36), kind=kLoop, calls=%fused_computation.40 | loop fusion | flops 7340032 | bytes 12582912 | tf_op jit(solution)/shard_map/reduce_sum | solution.py:174
  428.5 7.3 %gather_fusion.7 = f32[384,2048]{1,0:T(8,128)} fusion(f32[512,2048]{1,0:T(8,128)} %convert_reduce_fusion, s32[1024]{0:T(1024)S(1)} %pad_clamp_fusion), kind=kCustom, calls=%fused_computation.7 | custom fusion | bytes 6292992 | tf_op jit(solution)/shard_map/gather | solution.py:177
  435.8 4.8 %reshape.281 = f32[64,6,2048]{2,1,0:T(8,128)} reshape(f32[384,2048]{1,0:T(8,128)} %gather_fusion.7) | data formatting | bytes 6291456 | tf_op jit(solution)/shard_map/reshape | solution.py:177
  440.6 3.8 multiply_reduce_fusion
  (196 shorter events, 72.5 us)
Async XLA Ops:
  6.5 4.5 copy-start
  6.5 152.9 %all-gather.2.cloned.1.call-start = ((), (), s32[]{:S(2)}) async-start(), calls=%async_computation.4 | async-start | bytes 8650752 | tf_op jit(solution)/shard_map/all_gather | solution.py:137
  13.8 6.8 %copy-start.9 = (s32[64,6]{0,1:T(8,128)S(1)}, s32[64,6]{0,1:T(8,128)}, u32[]{:S(2)}) copy-start(s32[64,6]{0,1:T(8,128)} %param.23) | copy-start | bytes 4612
  13.8 7.2 %copy-start.7 = (s32[4,64]{1,0:T(4,128)S(1)}, s32[4,64]{1,0:T(4,128)}, u32[]{:S(2)}) copy-start(s32[4,64]{1,0:T(4,128)} %param.16) | copy-start | bytes 3076
  13.8 54.2 %all-to-all-start = ((bf16[4,64,32,256]{3,2,1,0:T(8,128)(2,1)}), bf16[4,64,32,256]{3,2,1,0:T(8,128)(2,1)}, u32[]{:S(2)}, u32[]{:S(2)}) async-start(bf16[4,64,32,256]{3,2,1,0:T(8,128)(2,1)} %bitcast.135), calls=%async_computation | async-start | bytes 8388608 | tf_op jit(solution)/shard_map/all_to_all | solution.py:91
  20.5 6.1 %collective-permute-start = (bf16[4,256,128]{2,1,0:T(8,128)(2,1)}, bf16[4,256,128]{2,1,0:T(8,128)(2,1)}, u32[]{:S(2)}, u32[]{:S(2)}) collective-permute-start(bf16[4,256,128]{2,1,0:T(8,128)(2,1)} %slice.29), channel_id=1, source_target_pairs={{0,1},{1,0},{2,3},{3,2},{4,5},{5,4},{6,7},{7,6},{8,9},{9,8},{10,11... | collective-permute-start | bytes 786440 | tf_op jit(solution)/shard_map/ppermute | solution.py:14
  23.2 2.8 copy-start.2
  89.3 2.4 copy-start.4
  103.4 2.4 copy-start.4
  117.5 2.4 copy-start.4
  131.7 2.4 copy-start.4
  135.3 24.2 %copy-start.8 = (bf16[64,2048]{1,0:T(8,128)(2,1)S(1)}, bf16[64,2048]{1,0:T(8,128)(2,1)}, u32[]{:S(2)}) copy-start(bf16[64,2048]{1,0:T(8,128)(2,1)} %param.20) | copy-start | bytes 786436
  136.4 2.0 collective-permute-start.2
  136.6 1.9 collective-permute-start.1
  137.1 1.3 collective-permute-start.3
  141.1 17.2 %all-to-all-start.1 = ((bf16[32,2,2048]{2,1,0:T(2,128)(2,1)}), bf16[32,2,2048]{2,1,0:T(2,128)(2,1)S(1)}, u32[]{:S(2)}, u32[]{:S(2)}) async-start(bf16[32,2,2048]{2,1,0:T(2,128)(2,1)} %reshape.369), calls=%async_computation.1 | async-start | bytes 524288 | tf_op jit(solution)/shard_map/all_to_all | solution.py:135
  159.4 5.9 %copy-start.10 = (f32[2048]{0:T(1024)S(1)}, f32[2048]{0:T(1024)}, u32[]{:S(2)}) copy-start(f32[2048]{0:T(1024)} %param.22) | copy-start | bytes 24580
  169.3 102.7 %copy-start.12 = (bf16[2,2048,352]{1,2,0:T(8,128)(2,1)S(1)}, bf16[2,2048,352]{1,2,0:T(8,128)(2,1)}, u32[]{:S(2)}) copy-start(bf16[2,2048,352]{1,2,0:T(8,128)(2,1)} %param.26) | copy-start | bytes 8650756
  272.0 8.8 %copy-start.13 = (bf16[2,2048,352]{1,2,0:T(8,128)(2,1)S(1)}, bf16[2,2048,352]{1,2,0:T(8,128)(2,1)}, u32[]{:S(2)}) copy-start(bf16[2,2048,352]{1,2,0:T(8,128)(2,1)} %param.25) | copy-start | bytes 8650756
  280.8 10.3 %copy-start.14 = (bf16[2,352,2048]{2,1,0:T(8,128)(2,1)S(1)}, bf16[2,352,2048]{2,1,0:T(8,128)(2,1)}, u32[]{:S(2)}) copy-start(bf16[2,352,2048]{2,1,0:T(8,128)(2,1)} %param.27) | copy-start | bytes 8650756
  310.5 10.3 %copy-start.11 = (f32[64,6]{0,1:T(8,128)S(1)}, f32[64,6]{0,1:T(8,128)}, u32[]{:S(2)}) copy-start(f32[64,6]{0,1:T(8,128)} %param.24) | copy-start | bytes 4612
  310.5 110.3 %all-to-all-start.3 = ((bf16[128,2,8,2048]{3,2,1,0:T(8,128)(2,1)}), bf16[128,2,8,2048]{3,2,1,0:T(8,128)(2,1)}, u32[]{:S(2)}, u32[]{:S(2)}) async-start(bf16[128,2,8,2048]{3,2,1,0:T(8,128)(2,1)} %copy.68), calls=%async_computation.3 | async-start | bytes 16777216 | tf_op jit(solution)/shard_map/all_to_all | solution.py:171
  435.8 9.5 %copy-start.1 = (bf16[192,32,256]{2,1,0:T(8,128)(2,1)S(1)}, bf16[192,32,256]{2,1,0:T(8,128)(2,1)}, u32[]{:S(2)}) copy-start(bf16[192,32,256]{2,1,0:T(8,128)(2,1)} %param.15) | copy-start | bytes 9437188
  440.6 3.8 copy-start.6
  (5 other events, 5.0 us)
Sparse Core Ops, SparseCore 0:
  9.6 55.3 all-gather.1

commit v2 on v1

--- a/solution.py
+++ b/solution.py
@@ -160,22 +160,28 @@
     experts_here = expert_gate.shape[0]
     width = normed.shape[1]
     outgoing_rows = outgoing_rows.reshape(tensor_size, experts_here, capacity, width)
-    fanned = jnp.broadcast_to(outgoing_rows[None], (group_count,) + outgoing_rows.shape)
-    fanned = fanned.reshape((group_count * tensor_size,) + outgoing_rows.shape[1:])
-    partial_value = run_experts(
-        lax.all_to_all(fanned, ("dp", "tensor"), split_axis=0, concat_axis=0, tiled=True),
-        expert_gate,
-        expert_up,
-        expert_down,
-    ).astype(jnp.bfloat16)
-    returned = lax.all_to_all(
-        partial_value, ("dp", "tensor"), split_axis=0, concat_axis=0, tiled=True
-    )
-    slot_out = jnp.sum(
-        returned.reshape(group_count, EXPERTS * capacity, width).astype(jnp.float32), axis=0
-    )
-    picked = slot_out[slot_of_pair].reshape(tok_rows, TOP, width)
-    routed = jnp.sum(picked * route_gates[:, :, None], axis=1)
+    owner_slot = (flat_routes // experts_here) * capacity + rank_in_expert
+    parity = flat_routes % experts_here
+    routed = jnp.zeros((tok_rows, width), jnp.float32)
+    for k in range(experts_here):
+        fanned = jnp.broadcast_to(outgoing_rows[None, :, k], (group_count,) + outgoing_rows[:, k].shape)
+        fanned = fanned.reshape((group_count * tensor_size, capacity, width))
+        arrived_rows = lax.all_to_all(fanned, ("dp", "tensor"), split_axis=0, concat_axis=0, tiled=True)
+        flat_rows = arrived_rows.reshape(-1, width)
+        gate_part = jnp.dot(flat_rows, expert_gate[k], preferred_element_type=jnp.float32)
+        up_part = jnp.dot(flat_rows, expert_up[k], preferred_element_type=jnp.float32)
+        active = (jax.nn.silu(gate_part) * up_part).astype(jnp.bfloat16)
+        partial_value = jnp.dot(active, expert_down[k], preferred_element_type=jnp.float32)
+        partial_value = partial_value.astype(jnp.bfloat16).reshape(arrived_rows.shape)
+        returned = lax.all_to_all(
+            partial_value, ("dp", "tensor"), split_axis=0, concat_axis=0, tiled=True
+        )
+        slot_out = jnp.sum(
+            returned.reshape(group_count, tensor_size * capacity, width).astype(jnp.float32), axis=0
+        )
+        weight = jnp.where(parity == k, route_gates.reshape(-1), 0.0)
+        picked = slot_out[owner_slot] * weight[:, None]
+        routed = routed + jnp.sum(picked.reshape(tok_rows, TOP, width), axis=1)
     return hidden + routed
 
 

time: 457 us -> 432 us (0.945)
  blocking collectives: 103 us -> 57.6 us
  waiting for transfers between devices: 150 us -> 167 us
  starting transfers between devices: 24.3 us -> 34.3 us
  local copies, waits for them, and re-layouts: 74.2 us -> 68.5 us
    all_to_all x1, blocking collectives: 103 us -> 57.6 us  [shards(): lax.all_to_all(fanned, ('dp', 'tensor'), split_axis=0, concat_axis=0, til...]
    all_to_all x0 -> x1, waiting for transfers between devices: none -> 38.1 us  [shards(): lax.all_to_all(fanned, ('dp', 'tensor'), split_axis=0, concat_axis=0, til...]
    all_to_all x1 -> x2, waiting for transfers between devices: 99.9 us -> 78.9 us  [shards(): lax.all_to_all(partial_value, ('dp', 'tensor'), split_axis=0, concat_axis...]
    convert_element_type x1 -> x0, local copies, waits for them, and re-layouts: 11.2 us -> none  [shards(): partial_value = run_experts(lax.all_to_all(fanned, ('dp', 'tensor'), spli...]
    gather x1 -> x4, local copies, waits for them, and re-layouts: 7.28 us -> 15.7 us  [shards(): picked = slot_out[owner_slot] * weight[:, None]]
    all_to_all x0 -> x1, starting transfers between devices: none -> 6.95 us  [shards(): lax.all_to_all(fanned, ('dp', 'tensor'), split_axis=0, concat_axis=0, til...]
    reshape x1 -> x0, local copies, waits for them, and re-layouts: 4.85 us -> none  [shards(): picked = slot_out[slot_of_pair].reshape(tok_rows, TOP, width)]
    all_to_all x1 -> x2, starting transfers between devices: 10 us -> 13 us  [shards(): lax.all_to_all(partial_value, ('dp', 'tensor'), split_axis=0, concat_axis...]
  transfers between devices with their start and end apart: 8 -> 10, of which waited for: 4 -> 6; matrix products, arithmetic and copies ran while one was open for 20% -> 30% of each run, Pallas kernels for 0% -> 0%
where the time goes in v2:
time: 432 us; the launch traced here: 430 us
  waiting for transfers between devices  167 us (39%)
  local copies, waits for them, and re-layouts  68.5 us (16%)
  blocking collectives  57.6 us (13%)
  matrix products  56.2 us (13%)
  starting transfers between devices  34.3 us (8%)
  other arithmetic  32.8 us (8%)
  between operations  13.8 us (3%)
    all_to_all x2, waiting for transfers between devices, shards(): lax.all_to_all(partial_value, ('dp', 'tensor'), split_axis=0, concat_axis...  78.9 us
    all_to_all x1, blocking collectives, shards(): lax.all_to_all(fanned, ('dp', 'tensor'), split_axis=0, concat_axis=0, til...  57.6 us
    all_to_all x1, waiting for transfers between devices, shards(): lax.all_to_all(outgoing, 'dp', split_axis=0, concat_axis=0, tiled=True)  39.4 us
    all_to_all x1, waiting for transfers between devices, shards(): lax.all_to_all(fanned, ('dp', 'tensor'), split_axis=0, concat_axis=0, til...  38.1 us
    dot_general x2, matrix products, shards(): jnp.dot(active, expert_down[k], preferred_element_type=jnp.float32)  18.8 us
    gather x4, local copies, waits for them, and re-layouts, shards(): picked = slot_out[owner_slot] * weight[:, None]  15.7 us
    all_to_all x2, starting transfers between devices, shards(): lax.all_to_all(partial_value, ('dp', 'tensor'), split_axis=0, concat_axis...  13 us
    convert_element_type x4, local copies, waits for them, and re-layouts, local_attention(): cache_weights.astype(jnp.bfloat16).reshape(span_len, page_count, page_rows)  10.2 us
  transfers between devices with their start and end apart: 10, of which 6 were waited for; matrix products, arithmetic and copies ran while one was open for 30% of the time, Pallas kernels for 0%

profile of v2, /device:TPU:0, one launch (start us, length us, event | category | flops | bytes accessed | tf_op | source)
XLA Modules:
  0.0 430.4 jit_solution(10227005117825747345)
XLA Ops:
  13.8 5.1 %all-to-all-start = ((bf16[4,64,32,256]{3,2,1,0:T(8,128)(2,1)}), bf16[4,64,32,256]{3,2,1,0:T(8,128)(2,1)}, u32[]{:S(2)}, u32[]{:S(2)}) async-start(bf16[4,64,32,256]{3,2,1,0:T(8,128)(2,1)} %bitcast.161), calls=%async_computation | async-start | bytes 8388608 | tf_op jit(solution)/shard_map/all_to_all | solution.py:91
  28.5 39.4 %all-to-all-done = bf16[4,64,32,256]{3,2,1,0:T(8,128)(2,1)} async-done(((bf16[4,64,32,256]{3,2,1,0:T(8,128)(2,1)}), bf16[4,64,32,256]{3,2,1,0:T(8,128)(2,1)}, u32[]{:S(2)}, u32[]{:S(2)}) %all-to-all-start) | async-done | bytes 4194336 | tf_op jit(solution)/shard_map/all_to_all | solution.py:91
  67.9 4.9 %gather_fusion.5 = bf16[4,64,32,256]{3,2,1,0:T(8,128)(2,1)} fusion(bf16[4,64,32,256]{3,2,1,0:T(8,128)(2,1)} %all-to-all-done, s32[1024]{0:T(1024)S(1)} %pad_clamp_fusion.2), kind=kCustom, calls=%fused_computation.5 | custom fusion | bytes 8388624 | tf_op jit(solution)/shard_map/gather | solution.py:101
  72.9 5.9 %broadcast_select_fusion = bf16[4,64,32,256]{3,2,1,0:T(8,128)(2,1)} fusion(bf16[4,64,32,256]{3,2,1,0:T(8,128)(2,1)} %bitcast.162, bf16[4,64,32,256]{3,2,1,0:T(8,128)(2,1)} %gather_fusion.5, pred[4]{0:T(512)(128)(4,1)S(1)} %get-tuple-element.156), kind=kLoop, calls=%fused_computation.55 | loop fusion | flops 2097152 | bytes 12582916 | tf_op jit(solution)/shard_map/jit(_where)/select_n | solution.py:101
  78.8 56.5 %while.16 = (s32[]{:T(128)}, f32[4,512,128]{1,2,0:T(8,128)}, f32[4,512]{1,0:T(4,128)S(1)}, f32[4,512]{1,0:T(4,128)S(1)}, s32[]{:T(128)}, /*index=5*/s32[4]{0:T(1...) while((s32[]{:T(128)}, f32[4,512,128]{1,2,0:T(8,128)}, ...), condition=%wide.region_7.8_spmd, body=%wide.region_2.7_spmd.sunk | while | flops 613485952 | bytes 29409492 | solution.py:122
  141.0 8.5 %all-to-all-start.1 = ((bf16[32,2,2048]{2,1,0:T(2,128)(2,1)}), bf16[32,2,2048]{2,1,0:T(2,128)(2,1)S(1)}, u32[]{:S(2)}, u32[]{:S(2)}) async-start(bf16[32,2,2048]{2,1,0:T(2,128)(2,1)} %reshape.502), calls=%async_computation.1 | async-start | bytes 524288 | tf_op jit(solution)/shard_map/all_to_all | solution.py:135
  149.5 8.7 %all-to-all-done.1 = bf16[32,2,2048]{2,1,0:T(2,128)(2,1)S(1)} async-done(((bf16[32,2,2048]{2,1,0:T(2,128)(2,1)}), bf16[32,2,2048]{2,1,0:T(2,128)(2,1)S(1)}, u32[]{:S(2)}, u32[]{:S(2)}) %all-to-all-start.1) | async-done | bytes 262176 | tf_op jit(solution)/shard_map/all_to_all | solution.py:135
  159.4 5.1 %multiply_reduce_fusion.2 = (f32[64]{0:T(128)S(1)}, f32[64,2048]{1,0:T(8,128)S(1)}) fusion(bf16[64,2048]{1,0:T(8,128)(2,1)S(1)} %reshape.399, bf16[2048,2048]{1,0:T(8,128)(2,1)} %all-gather.2.cloned.1.call-done, bf16[64,2048]{1,0:T(8,128)(2,1)S(1)} %copy-done.9), kind=kOutput, calls=%fused_computation.84 | convolution fusion | flops 537395136 | bytes 9437440 | tf_op jit(solution)/shard_map/dot_general | solution.py:138
  168.8 57.6 %all_to_all.30 = bf16[128,8,2048]{2,1,0:T(8,128)(2,1)} all-to-all(bf16[128,8,2048]{2,1,0:T(8,128)(2,1)S(1)} %bitcast.164), channel_id=1, replica_groups=mesh['dp'=4,'tensor'=32] {'dp','tensor'}, dimensions={0} | all-to-all | bytes 8388608 | tf_op jit(solution)/shard_map/all_to_all | solution.py:169
  228.9 7.0 %all-to-all-start.2 = ((bf16[128,8,2048]{2,1,0:T(8,128)(2,1)}), bf16[128,8,2048]{2,1,0:T(8,128)(2,1)}, u32[]{:S(2)}, u32[]{:S(2)}) async-start(bf16[128,8,2048]{2,1,0:T(8,128)(2,1)} %bitcast.163), calls=%async_computation.2 | async-start | bytes 8388608 | tf_op jit(solution)/shard_map/all_to_all | solution.py:169
  235.9 5.0 %fusion.21 = f32[1024,352]{0,1:T(8,128)} fusion(bf16[128,8,2048]{2,1,0:T(8,128)(2,1)} %all_to_all.30, bf16[2,2048,352]{1,2,0:T(8,128)(2,1)S(1)} %copy-done.13), kind=kOutput, calls=%fused_computation.45 | convolution fusion | flops 1476395008 | bytes 7077888 | tf_op jit(solution)/shard_map/dot_general | solution.py:171
  240.9 9.4 %convert_bitcast_fusion = bf16[128,8,2048]{2,1,0:T(8,128)(2,1)} fusion(bf16[2,352,2048]{2,1,0:T(8,128)(2,1)} %param.27, bf16[2,2048,352]{1,2,0:T(8,128)(2,1)} %param.26, bf16[128,8,2048]{2,1,0:T(8,128)(2,1)} %all_to_all.30, f32[1024,352]{0,1:T(8,128)} %fusion.21), kind=kOutput, calls=%fused_computation.52 | convolution fusion | flops 2957049856 | bytes 12713984 | tf_op jit(solution)/shard_map/dot_general | solution.py:174
  250.3 38.1 %all-to-all-done.2 = bf16[128,8,2048]{2,1,0:T(8,128)(2,1)} async-done(((bf16[128,8,2048]{2,1,0:T(8,128)(2,1)}), bf16[128,8,2048]{2,1,0:T(8,128)(2,1)}, u32[]{:S(2)}, u32[]{:S(2)}) %all-to-all-start.2) | async-done | bytes 4194336 | tf_op jit(solution)/shard_map/all_to_all | solution.py:169
  288.4 6.0 %all-to-all-start.5 = ((bf16[128,8,2048]{2,1,0:T(8,128)(2,1)}), bf16[128,8,2048]{2,1,0:T(8,128)(2,1)}, u32[]{:S(2)}, u32[]{:S(2)}) async-start(bf16[128,8,2048]{2,1,0:T(8,128)(2,1)} %convert_bitcast_fusion), calls=%async_computation.5 | async-start | bytes 8388608 | tf_op jit(solution)/shard_map/all_to_all | solution.py:176
  294.4 5.0 %fusion.25 = f32[1024,352]{0,1:T(8,128)} fusion(bf16[128,8,2048]{2,1,0:T(8,128)(2,1)} %all-to-all-done.2, bf16[2,2048,352]{1,2,0:T(8,128)(2,1)S(1)} %copy-done.13), kind=kOutput, calls=%fused_computation.49 | convolution fusion | flops 1476395008 | bytes 7077888 | tf_op jit(solution)/shard_map/dot_general | solution.py:171
  299.4 9.4 %convert_bitcast_fusion.1 = bf16[128,8,2048]{2,1,0:T(8,128)(2,1)} fusion(bf16[2,352,2048]{2,1,0:T(8,128)(2,1)} %param.27, bf16[2,2048,352]{1,2,0:T(8,128)(2,1)} %param.26, bf16[128,8,2048]{2,1,0:T(8,128)(2,1)} %all-to-all-done.2, f32[1024,352]{0,1:T(8,128)} %fusion.25), kind=kOutput, calls=%fused_computation.54 | convolution fusion | flops 2957049856 | bytes 12713984 | tf_op jit(solution)/shard_map/dot_general | solution.py:174
  308.8 37.9 %all-to-all-done.5 = bf16[128,8,2048]{2,1,0:T(8,128)(2,1)} async-done(((bf16[128,8,2048]{2,1,0:T(8,128)(2,1)}), bf16[128,8,2048]{2,1,0:T(8,128)(2,1)}, u32[]{:S(2)}, u32[]{:S(2)}) %all-to-all-start.5) | async-done | bytes 4194336 | tf_op jit(solution)/shard_map/all_to_all | solution.py:176
  346.7 7.0 %all-to-all-start.3 = ((bf16[128,8,2048]{2,1,0:T(8,128)(2,1)}), bf16[128,8,2048]{2,1,0:T(8,128)(2,1)}, u32[]{:S(2)}, u32[]{:S(2)}) async-start(bf16[128,8,2048]{2,1,0:T(8,128)(2,1)} %convert_bitcast_fusion.1), calls=%async_computation.3 | async-start | bytes 8388608 | tf_op jit(solution)/shard_map/all_to_all | solution.py:176
  357.3 3.3 gather_fusion.8
  360.5 4.6 %gather.50 = f32[64,6,2048]{2,1,0:T(8,128)} reshape(f32[384,2048]{1,0:T(8,128)} %gather_fusion.8) | data formatting | bytes 6291456 | tf_op jit(solution)/shard_map/gather | solution.py:183
  365.1 41.1 %all-to-all-done.3 = bf16[128,8,2048]{2,1,0:T(8,128)(2,1)} async-done(((bf16[128,8,2048]{2,1,0:T(8,128)(2,1)}), bf16[128,8,2048]{2,1,0:T(8,128)(2,1)}, u32[]{:S(2)}, u32[]{:S(2)}) %all-to-all-start.3) | async-done | bytes 4194336 | tf_op jit(solution)/shard_map/all_to_all | solution.py:176
  409.4 3.3 gather_fusion.7
  412.6 4.6 %gather.48 = f32[64,6,2048]{2,1,0:T(8,128)} reshape(f32[384,2048]{1,0:T(8,128)} %gather_fusion.7) | data formatting | bytes 6291456 | tf_op jit(solution)/shard_map/gather | solution.py:183
  417.2 3.9 multiply_reduce_fusion
  (204 shorter events, 95.7 us)
Async XLA Ops:
  6.5 4.5 %copy-start = (bf16[192,32,256]{2,1,0:T(8,128)(2,1)S(1)}, bf16[192,32,256]{2,1,0:T(8,128)(2,1)}, u32[]{:S(2)}) copy-start(bf16[192,32,256]{2,1,0:T(8,128)(2,1)} %param.15) | copy-start | bytes 9437188
  6.5 152.9 %all-gather.2.cloned.1.call-start = ((), (), s32[]{:S(2)}) async-start(), calls=%async_computation.6 | async-start | bytes 8650752 | tf_op jit(solution)/shard_map/all_gather | solution.py:137
  13.8 6.8 %copy-start.10 = (s32[64,6]{0,1:T(8,128)S(1)}, s32[64,6]{0,1:T(8,128)}, u32[]{:S(2)}) copy-start(s32[64,6]{0,1:T(8,128)} %param.23) | copy-start | bytes 4612
  13.8 7.2 %copy-start.8 = (s32[4,64]{1,0:T(4,128)S(1)}, s32[4,64]{1,0:T(4,128)}, u32[]{:S(2)}) copy-start(s32[4,64]{1,0:T(4,128)} %param.16) | copy-start | bytes 3076
  13.8 54.2 %all-to-all-start = ((bf16[4,64,32,256]{3,2,1,0:T(8,128)(2,1)}), bf16[4,64,32,256]{3,2,1,0:T(8,128)(2,1)}, u32[]{:S(2)}, u32[]{:S(2)}) async-start(bf16[4,64,32,256]{3,2,1,0:T(8,128)(2,1)} %bitcast.161), calls=%async_computation | async-start | bytes 8388608 | tf_op jit(solution)/shard_map/all_to_all | solution.py:91
  20.5 6.1 %collective-permute-start = (bf16[4,256,128]{2,1,0:T(8,128)(2,1)}, bf16[4,256,128]{2,1,0:T(8,128)(2,1)}, u32[]{:S(2)}, u32[]{:S(2)}) collective-permute-start(bf16[4,256,128]{2,1,0:T(8,128)(2,1)} %slice.53), channel_id=1, source_target_pairs={{0,1},{1,0},{2,3},{3,2},{4,5},{5,4},{6,7},{7,6},{8,9},{9,8},{10,11... | collective-permute-start | bytes 786440 | tf_op jit(solution)/shard_map/ppermute | solution.py:14
  23.2 2.8 copy-start.2
  89.3 2.4 copy-start.4
  103.4 2.4 copy-start.4
  117.5 2.4 copy-start.4
  131.7 2.4 copy-start.4
  136.4 23.0 %copy-start.9 = (bf16[64,2048]{1,0:T(8,128)(2,1)S(1)}, bf16[64,2048]{1,0:T(8,128)(2,1)}, u32[]{:S(2)}) copy-start(bf16[64,2048]{1,0:T(8,128)(2,1)} %param.20) | copy-start | bytes 786436
  136.4 2.0 collective-permute-start.2
  136.5 1.9 collective-permute-start.1
  137.1 1.3 collective-permute-start.3
  141.0 17.2 %all-to-all-start.1 = ((bf16[32,2,2048]{2,1,0:T(2,128)(2,1)}), bf16[32,2,2048]{2,1,0:T(2,128)(2,1)S(1)}, u32[]{:S(2)}, u32[]{:S(2)}) async-start(bf16[32,2,2048]{2,1,0:T(2,128)(2,1)} %reshape.502), calls=%async_computation.1 | async-start | bytes 524288 | tf_op jit(solution)/shard_map/all_to_all | solution.py:135
  159.4 5.9 %copy-start.11 = (f32[2048]{0:T(1024)S(1)}, f32[2048]{0:T(1024)}, u32[]{:S(2)}) copy-start(f32[2048]{0:T(1024)} %param.22) | copy-start | bytes 24580
  228.9 7.0 %copy-start.13 = (bf16[2,2048,352]{1,2,0:T(8,128)(2,1)S(1)}, bf16[2,2048,352]{1,2,0:T(8,128)(2,1)}, u32[]{:S(2)}) copy-start(bf16[2,2048,352]{1,2,0:T(8,128)(2,1)} %param.25) | copy-start | bytes 8650756
  228.9 59.5 %all-to-all-start.2 = ((bf16[128,8,2048]{2,1,0:T(8,128)(2,1)}), bf16[128,8,2048]{2,1,0:T(8,128)(2,1)}, u32[]{:S(2)}, u32[]{:S(2)}) async-start(bf16[128,8,2048]{2,1,0:T(8,128)(2,1)} %bitcast.163), calls=%async_computation.2 | async-start | bytes 8388608 | tf_op jit(solution)/shard_map/all_to_all | solution.py:169
  288.4 58.3 %all-to-all-start.5 = ((bf16[128,8,2048]{2,1,0:T(8,128)(2,1)}), bf16[128,8,2048]{2,1,0:T(8,128)(2,1)}, u32[]{:S(2)}, u32[]{:S(2)}) async-start(bf16[128,8,2048]{2,1,0:T(8,128)(2,1)} %convert_bitcast_fusion), calls=%async_computation.5 | async-start | bytes 8388608 | tf_op jit(solution)/shard_map/all_to_all | solution.py:176
  308.8 45.0 %copy-start.12 = (f32[64,6]{0,1:T(8,128)S(1)}, f32[64,6]{0,1:T(8,128)}, u32[]{:S(2)}) copy-start(f32[64,6]{0,1:T(8,128)} %param.24) | copy-start | bytes 4612
  346.7 59.5 %all-to-all-start.3 = ((bf16[128,8,2048]{2,1,0:T(8,128)(2,1)}), bf16[128,8,2048]{2,1,0:T(8,128)(2,1)}, u32[]{:S(2)}, u32[]{:S(2)}) async-start(bf16[128,8,2048]{2,1,0:T(8,128)(2,1)} %convert_bitcast_fusion.1), calls=%async_computation.3 | async-start | bytes 8388608 | tf_op jit(solution)/shard_map/all_to_all | solution.py:176
  417.2 3.9 copy-start.5
  417.2 6.3 %copy-start.1 = (bf16[192,32,256]{2,1,0:T(8,128)(2,1)S(1)}, bf16[192,32,256]{2,1,0:T(8,128)(2,1)}, u32[]{:S(2)}) copy-start(bf16[192,32,256]{2,1,0:T(8,128)(2,1)} %param.15) | copy-start | bytes 9437188
  (6 other events, 6.6 us)
Sparse Core Ops, SparseCore 0:
  9.6 55.3 all-gather.1

commit v3 on v2

--- a/solution.py
+++ b/solution.py
@@ -82,13 +82,16 @@
     first_home = group_index * requests_here
     home_dest = lax.dynamic_slice_in_dim(destination, first_home, requests_here)
     dest_group = home_dest // requests_here
-    group_ids = jnp.arange(group_count, dtype=jnp.int32)
     request_ids = jnp.arange(requests_here, dtype=jnp.int32)
-    leaving = dest_group[None, :] == group_ids[:, None]
-    chosen = jnp.sum(jnp.where(leaving, request_ids[None, :], 0), axis=1)
-    chosen = jnp.where(group_ids == group_index, 0, chosen)
-    outgoing = page_pool[page_table[chosen]]
-    arrived = lax.all_to_all(outgoing, "dp", split_axis=0, concat_axis=0, tiled=True)
+    shifts = jnp.arange(group_count, dtype=jnp.int32)
+    work_req = jnp.sum(
+        jnp.where(
+            dest_group[None, :] == (group_index + shifts[:, None]) % group_count,
+            request_ids[None, :],
+            0,
+        ),
+        axis=1,
+    )
     inverse = (
         jnp.zeros_like(destination)
         .at[destination]
@@ -96,10 +99,25 @@
     )
     served = lax.dynamic_slice_in_dim(inverse, first_home, requests_here)
     source = served // requests_here
-    resident = source == group_index
-    local_pages = page_pool[page_table[jnp.where(resident, served - first_home, 0)]]
-    dense_cache = jnp.where(resident[:, None, None, None], local_pages, arrived[source])
-    lengths = cache_len[served]
+    send_slot = jnp.sum(
+        jnp.where(
+            source[None, :] == (group_index - shifts[:, None]) % group_count,
+            request_ids[None, :],
+            0,
+        ),
+        axis=1,
+    )
+    outgoing_tokens = new_tokens[send_slot]
+    fresh = [outgoing_tokens[0]]
+    for j in range(1, group_count):
+        fresh.append(
+            lax.ppermute(
+                outgoing_tokens[j], "dp", [(i, (i - j) % group_count) for i in range(group_count)]
+            )
+        )
+    new_tokens = jnp.stack(fresh)
+    dense_cache = page_pool[page_table[work_req]]
+    lengths = cache_len[first_home + work_req]
     fresh_per = new_tokens.shape[1] // heads_here
     span_len = fresh_per * split_ways
     rows_per_head = dense_cache.shape[2] // heads_here
@@ -130,8 +148,15 @@
     theirs = jnp.exp(other_max - joint_max)
     combined = kept_part * own_scale[..., None] + received_part * theirs[..., None]
     attended = combined / (denominator * own_scale + other_den * theirs)[..., None]
+    attended = attended.astype(jnp.bfloat16)
+    back = [attended[0]]
+    for j in range(1, group_count):
+        back.append(
+            lax.ppermute(attended[j], "dp", [(i, (i + j) % group_count) for i in range(group_count)])
+        )
+    attended = jnp.stack(back)[(group_index - source) % group_count]
     tok_rows = residual_in.shape[0]
-    head_out = attended.astype(jnp.bfloat16).reshape(tensor_size, tok_rows, half_dim)
+    head_out = attended.reshape(tensor_size, tok_rows, half_dim)
     owned = lax.all_to_all(head_out, "tensor", split_axis=0, concat_axis=0, tiled=True)
     owned = owned.transpose(1, 0, 2).reshape(tok_rows, tensor_size * half_dim)
     full_weight = lax.all_gather(out_weight, "tensor", axis=0, tiled=True)

time: 432 us -> 412 us (0.954)
  waiting for transfers between devices: 167 us -> 138 us
  starting transfers between devices: 34.3 us -> 47.7 us
  local copies, waits for them, and re-layouts: 68.5 us -> 63.8 us
    all_to_all x1 -> x0, waiting for transfers between devices: 39.4 us -> none  [shards(): lax.all_to_all(outgoing, 'dp', split_axis=0, concat_axis=0, tiled=True)]
    all_to_all x2, starting transfers between devices: 13 us -> 23.6 us  [shards(): lax.all_to_all(partial_value, ('dp', 'tensor'), split_axis=0, concat_axis...]
    ppermute x0 -> x6, waiting for transfers between devices: none -> 10.3 us  [the longest x3 6.14 us: shards(): lax.ppermute(outgoing_tokens[j], 'dp', [(i, (i - j) % group_count) for i...]
    ppermute x0 -> x6, starting transfers between devices: none -> 8.14 us  [the longest x3 4.73 us: shards(): lax.ppermute(outgoing_tokens[j], 'dp', [(i, (i - j) % group_count) for i...]
    select_n x6 -> x5, other arithmetic: 6.73 us -> 0.2 us  [the longest x1 0.1 us: shards(): attended = jnp.stack(back)[(group_index - source) % group_count]]
    gather x6 -> x5, local copies, waits for them, and re-layouts: 12.9 us -> 7.29 us  [the longest x2 3.36 us: shards(): dense_cache = page_pool[page_table[work_req]]]
    all_to_all x1 -> x0, starting transfers between devices: 5.07 us -> none  [shards(): lax.all_to_all(outgoing, 'dp', split_axis=0, concat_axis=0, tiled=True)]
  transfers between devices with their start and end apart: 10 -> 15, of which waited for: 6 -> 10; matrix products, arithmetic and copies ran while one was open for 30% -> 29% of each run, Pallas kernels for 0% -> 0%
where the time goes in v3:
time: 412 us; the launch traced here: 408 us
  waiting for transfers between devices  138 us (33%)
  local copies, waits for them, and re-layouts  63.8 us (15%)
  blocking collectives  58.6 us (14%)
  matrix products  56.3 us (14%)
  starting transfers between devices  47.7 us (12%)
  other arithmetic  29.1 us (7%)
  between operations  14.1 us (3%)
    all_to_all x2, waiting for transfers between devices, shards(): lax.all_to_all(partial_value, ('dp', 'tensor'), split_axis=0, concat_axis...  78.9 us
    all_to_all x1, blocking collectives, shards(): lax.all_to_all(fanned, ('dp', 'tensor'), split_axis=0, concat_axis=0, til...  58.6 us
    all_to_all x1, waiting for transfers between devices, shards(): lax.all_to_all(fanned, ('dp', 'tensor'), split_axis=0, concat_axis=0, til...  38.1 us
    all_to_all x2, starting transfers between devices, shards(): lax.all_to_all(partial_value, ('dp', 'tensor'), split_axis=0, concat_axis...  23.6 us
    dot_general x2, matrix products, shards(): jnp.dot(active, expert_down[k], preferred_element_type=jnp.float32)  18.8 us
    gather x4, local copies, waits for them, and re-layouts, shards(): picked = slot_out[owner_slot] * weight[:, None]  15.7 us
    convert_element_type x4, local copies, waits for them, and re-layouts, local_attention(): cache_weights.astype(jnp.bfloat16).reshape(span_len, page_count, page_rows)  10.2 us
    dot_general x2, matrix products, shards(): jnp.dot(flat_rows, expert_gate[k], preferred_element_type=jnp.float32)  9.99 us
  transfers between devices with their start and end apart: 15, of which 10 were waited for; matrix products, arithmetic and copies ran while one was open for 29% of the time, Pallas kernels for 0%

profile of v3, /device:TPU:0, one launch (start us, length us, event | category | flops | bytes accessed | tf_op | source)
XLA Modules:
  0.0 407.7 jit_solution(7662864671736463131)
XLA Ops:
  13.8 3.1 collective-permute-start
  37.0 55.9 %while.16 = (s32[]{:T(128)}, f32[4,512,128]{1,2,0:T(8,128)}, f32[4,512]{1,0:T(4,128)S(1)}, f32[4,512]{1,0:T(4,128)S(1)}, s32[]{:T(128)}, /*index=5*/s32[4]{0:T(1...) while((s32[]{:T(128)}, f32[4,512,128]{1,2,0:T(8,128)}, ...), condition=%wide.region_8.9_spmd, body=%wide.region_3.8_spmd.sunk | while | flops 613485952 | bytes 29409492 | solution.py:140
  100.8 3.6 collective-permute-done.7
  107.0 8.6 %all-to-all-start = ((bf16[32,2,2048]{2,1,0:T(2,128)(2,1)}), bf16[32,2,2048]{2,1,0:T(2,128)(2,1)S(1)}, u32[]{:S(2)}, u32[]{:S(2)}) async-start(bf16[32,2,2048]{2,1,0:T(2,128)(2,1)} %reshape.541), calls=%async_computation | async-start | bytes 524288 | tf_op jit(solution)/shard_map/all_to_all | solution.py:160
  115.7 8.9 %all-to-all-done = bf16[32,2,2048]{2,1,0:T(2,128)(2,1)S(1)} async-done(((bf16[32,2,2048]{2,1,0:T(2,128)(2,1)}), bf16[32,2,2048]{2,1,0:T(2,128)(2,1)S(1)}, u32[]{:S(2)}, u32[]{:S(2)}) %all-to-all-start) | async-done | bytes 262176 | tf_op jit(solution)/shard_map/all_to_all | solution.py:160
  125.8 5.1 %multiply_reduce_fusion.2 = (f32[64]{0:T(128)S(1)}, f32[64,2048]{1,0:T(8,128)S(1)}) fusion(bf16[64,2048]{1,0:T(8,128)(2,1)S(1)} %reshape.449, bf16[2048,2048]{1,0:T(8,128)(2,1)} %all-gather.2.cloned.1.call-done, bf16[64,2048]{1,0:T(8,128)(2,1)S(1)} %copy-done.9), kind=kOutput, calls=%fused_computation.83 | convolution fusion | flops 537395136 | bytes 9437440 | tf_op jit(solution)/shard_map/dot_general | solution.py:163
  135.1 58.6 %all_to_all.25 = bf16[128,8,2048]{2,1,0:T(8,128)(2,1)} all-to-all(bf16[128,8,2048]{2,1,0:T(8,128)(2,1)S(1)} %bitcast.183), channel_id=1, replica_groups=mesh['dp'=4,'tensor'=32] {'dp','tensor'}, dimensions={0} | all-to-all | bytes 8388608 | tf_op jit(solution)/shard_map/all_to_all | solution.py:194
  196.3 6.1 %all-to-all-start.1 = ((bf16[128,8,2048]{2,1,0:T(8,128)(2,1)}), bf16[128,8,2048]{2,1,0:T(8,128)(2,1)}, u32[]{:S(2)}, u32[]{:S(2)}) async-start(bf16[128,8,2048]{2,1,0:T(8,128)(2,1)} %bitcast.182), calls=%async_computation.1 | async-start | bytes 8388608 | tf_op jit(solution)/shard_map/all_to_all | solution.py:194
  202.3 5.0 %fusion.21 = f32[1024,352]{0,1:T(8,128)} fusion(bf16[128,8,2048]{2,1,0:T(8,128)(2,1)} %all_to_all.25, bf16[2,2048,352]{1,2,0:T(8,128)(2,1)S(1)} %copy-done.15), kind=kOutput, calls=%fused_computation.44 | convolution fusion | flops 1476395008 | bytes 7077888 | tf_op jit(solution)/shard_map/dot_general | solution.py:196
  207.3 9.4 %convert_bitcast_fusion = bf16[128,8,2048]{2,1,0:T(8,128)(2,1)} fusion(bf16[2,352,2048]{2,1,0:T(8,128)(2,1)} %param.27, bf16[2,2048,352]{1,2,0:T(8,128)(2,1)} %param.26, bf16[128,8,2048]{2,1,0:T(8,128)(2,1)} %all_to_all.25, f32[1024,352]{0,1:T(8,128)} %fusion.21), kind=kOutput, calls=%fused_computation.51 | convolution fusion | flops 2957049856 | bytes 12713984 | tf_op jit(solution)/shard_map/dot_general | solution.py:199
  216.8 38.1 %all-to-all-done.1 = bf16[128,8,2048]{2,1,0:T(8,128)(2,1)} async-done(((bf16[128,8,2048]{2,1,0:T(8,128)(2,1)}), bf16[128,8,2048]{2,1,0:T(8,128)(2,1)}, u32[]{:S(2)}, u32[]{:S(2)}) %all-to-all-start.1) | async-done | bytes 4194336 | tf_op jit(solution)/shard_map/all_to_all | solution.py:194
  254.8 16.8 %all-to-all-start.4 = ((bf16[128,8,2048]{2,1,0:T(8,128)(2,1)}), bf16[128,8,2048]{2,1,0:T(8,128)(2,1)}, u32[]{:S(2)}, u32[]{:S(2)}) async-start(bf16[128,8,2048]{2,1,0:T(8,128)(2,1)} %convert_bitcast_fusion), calls=%async_computation.4 | async-start | bytes 8388608 | tf_op jit(solution)/shard_map/all_to_all | solution.py:201
  271.6 5.0 %fusion.25 = f32[1024,352]{0,1:T(8,128)} fusion(bf16[128,8,2048]{2,1,0:T(8,128)(2,1)} %all-to-all-done.1, bf16[2,2048,352]{1,2,0:T(8,128)(2,1)S(1)} %copy-done.15), kind=kOutput, calls=%fused_computation.48 | convolution fusion | flops 1476395008 | bytes 7077888 | tf_op jit(solution)/shard_map/dot_general | solution.py:196
  276.6 9.4 %convert_bitcast_fusion.1 = bf16[128,8,2048]{2,1,0:T(8,128)(2,1)} fusion(bf16[2,352,2048]{2,1,0:T(8,128)(2,1)} %param.27, bf16[2,2048,352]{1,2,0:T(8,128)(2,1)} %param.26, bf16[128,8,2048]{2,1,0:T(8,128)(2,1)} %all-to-all-done.1, f32[1024,352]{0,1:T(8,128)} %fusion.25), kind=kOutput, calls=%fused_computation.53 | convolution fusion | flops 2957049856 | bytes 12713984 | tf_op jit(solution)/shard_map/dot_general | solution.py:199
  286.0 37.9 %all-to-all-done.4 = bf16[128,8,2048]{2,1,0:T(8,128)(2,1)} async-done(((bf16[128,8,2048]{2,1,0:T(8,128)(2,1)}), bf16[128,8,2048]{2,1,0:T(8,128)(2,1)}, u32[]{:S(2)}, u32[]{:S(2)}) %all-to-all-start.4) | async-done | bytes 4194336 | tf_op jit(solution)/shard_map/all_to_all | solution.py:201
  323.9 6.9 %all-to-all-start.2 = ((bf16[128,8,2048]{2,1,0:T(8,128)(2,1)}), bf16[128,8,2048]{2,1,0:T(8,128)(2,1)}, u32[]{:S(2)}, u32[]{:S(2)}) async-start(bf16[128,8,2048]{2,1,0:T(8,128)(2,1)} %convert_bitcast_fusion.1), calls=%async_computation.2 | async-start | bytes 8388608 | tf_op jit(solution)/shard_map/all_to_all | solution.py:201
  331.2 3.2 convert_reduce_fusion
  334.4 3.3 gather_fusion.7
  337.6 4.6 %gather.43 = f32[64,6,2048]{2,1,0:T(8,128)} reshape(f32[384,2048]{1,0:T(8,128)} %gather_fusion.7) | data formatting | bytes 6291456 | tf_op jit(solution)/shard_map/gather | solution.py:208
  342.2 41.1 %all-to-all-done.2 = bf16[128,8,2048]{2,1,0:T(8,128)(2,1)} async-done(((bf16[128,8,2048]{2,1,0:T(8,128)(2,1)}), bf16[128,8,2048]{2,1,0:T(8,128)(2,1)}, u32[]{:S(2)}, u32[]{:S(2)}) %all-to-all-start.2) | async-done | bytes 4194336 | tf_op jit(solution)/shard_map/all_to_all | solution.py:201
  383.3 3.2 convert_reduce_fusion.1
  386.5 3.3 gather_fusion.6
  389.7 4.6 %gather.41 = f32[64,6,2048]{2,1,0:T(8,128)} reshape(f32[384,2048]{1,0:T(8,128)} %gather_fusion.6) | data formatting | bytes 6291456 | tf_op jit(solution)/shard_map/gather | solution.py:208
  394.3 3.9 multiply_reduce_fusion
  (219 shorter events, 103.8 us)
Async XLA Ops:
  6.5 25.1 %copy-start = (bf16[192,32,256]{2,1,0:T(8,128)(2,1)S(1)}, bf16[192,32,256]{2,1,0:T(8,128)(2,1)}, u32[]{:S(2)}) copy-start(bf16[192,32,256]{2,1,0:T(8,128)(2,1)} %param.15) | copy-start | bytes 9437188
  6.5 12.3 %copy-start.14 = (s32[16]{0:T(128)S(1)}, s32[16]{0:T(128)}, u32[]{:S(2)}) copy-start(s32[16]{0:T(128)} %param.17) | copy-start | bytes 196
  6.5 11.9 %copy-start.11 = (s32[64,6]{0,1:T(8,128)S(1)}, s32[64,6]{0,1:T(8,128)}, u32[]{:S(2)}) copy-start(s32[64,6]{0,1:T(8,128)} %param.23) | copy-start | bytes 4612
  6.5 12.6 %copy-start.10 = (s32[4,64]{1,0:T(4,128)S(1)}, s32[4,64]{1,0:T(4,128)}, u32[]{:S(2)}) copy-start(s32[4,64]{1,0:T(4,128)} %param.16) | copy-start | bytes 3076
  6.5 119.2 %all-gather.2.cloned.1.call-start = ((), (), s32[]{:S(2)}) async-start(), calls=%async_computation.5 | async-start | bytes 8650752 | tf_op jit(solution)/shard_map/all_gather | solution.py:162
  13.8 11.8 %collective-permute-start = (bf16[256,384]{1,0:T(8,128)(2,1)}, bf16[256,384]{1,0:T(8,128)(2,1)}, u32[]{:S(2)}, u32[]{:S(2)}) collective-permute-start(bf16[256,384]{1,0:T(8,128)(2,1)} %get-tuple-element.167), channel_id=1, source_target_pairs={{0,96},{32,0},{64,32},{96,64},{1,97},{33,1},{65,33},{97,65},{2,98}... | collective-permute-start | bytes 589832 | tf_op jit(solution)/shard_map/ppermute | solution.py:114
  16.9 9.6 %collective-permute-start.1 = (bf16[256,384]{1,0:T(8,128)(2,1)}, bf16[256,384]{1,0:T(8,128)(2,1)}, u32[]{:S(2)}, u32[]{:S(2)}) collective-permute-start(bf16[256,384]{1,0:T(8,128)(2,1)} %get-tuple-element.166), channel_id=1, source_target_pairs={{0,64},{32,96},{64,0},{96,32},{1,65},{33,97},{65,1},{97,33},{2,66}... | collective-permute-start | bytes 589832 | tf_op jit(solution)/shard_map/ppermute | solution.py:114
  17.5 11.8 %collective-permute-start.2 = (bf16[256,384]{1,0:T(8,128)(2,1)}, bf16[256,384]{1,0:T(8,128)(2,1)}, u32[]{:S(2)}, u32[]{:S(2)}) collective-permute-start(bf16[256,384]{1,0:T(8,128)(2,1)} %get-tuple-element.168), channel_id=1, source_target_pairs={{0,32},{32,64},{64,96},{96,0},{1,33},{33,65},{65,97},{97,1},{2,34}... | collective-permute-start | bytes 589832 | tf_op jit(solution)/shard_map/ppermute | solution.py:114
  31.5 3.6 collective-permute-start.3
  94.0 2.1 collective-permute-start.5
  94.6 1.5 collective-permute-start.4
  94.7 1.4 collective-permute-start.6
  97.4 7.1 %collective-permute-start.7 = (bf16[512,64]{0,1:T(8,128)(2,1)S(1)}, bf16[512,64]{0,1:T(8,128)(2,1)S(1)}, u32[]{:S(2)}, u32[]{:S(2)}) collective-permute-start(bf16[512,64]{0,1:T(8,128)(2,1)S(1)} %get-tuple-element.172), channel_id=1, source_target_pairs={{0,32},{32,64},{64,96},{96,0},{1,33},{33,65},{65,97},{97,1},{2,34}... | collective-permute-start | bytes 196616 | tf_op jit(solution)/shard_map/ppermute | solution.py:155
  97.5 7.0 %collective-permute-start.8 = (bf16[512,64]{0,1:T(8,128)(2,1)S(1)}, bf16[512,64]{0,1:T(8,128)(2,1)S(1)}, u32[]{:S(2)}, u32[]{:S(2)}) collective-permute-start(bf16[512,64]{0,1:T(8,128)(2,1)S(1)} %get-tuple-element.171), channel_id=1, source_target_pairs={{0,64},{32,96},{64,0},{96,32},{1,65},{33,97},{65,1},{97,33},{2,66}... | collective-permute-start | bytes 196616 | tf_op jit(solution)/shard_map/ppermute | solution.py:155
  99.7 5.3 %collective-permute-start.9 = (bf16[512,64]{0,1:T(8,128)(2,1)S(1)}, bf16[512,64]{0,1:T(8,128)(2,1)S(1)}, u32[]{:S(2)}, u32[]{:S(2)}) collective-permute-start(bf16[512,64]{0,1:T(8,128)(2,1)S(1)} %get-tuple-element.170), channel_id=1, source_target_pairs={{0,96},{32,0},{64,32},{96,64},{1,97},{33,1},{65,33},{97,65},{2,98}... | collective-permute-start | bytes 196616 | tf_op jit(solution)/shard_map/ppermute | solution.py:155
  105.1 20.7 %copy-start.9 = (bf16[64,2048]{1,0:T(8,128)(2,1)S(1)}, bf16[64,2048]{1,0:T(8,128)(2,1)}, u32[]{:S(2)}) copy-start(bf16[64,2048]{1,0:T(8,128)(2,1)} %param.20) | copy-start | bytes 786436
  107.0 17.5 %all-to-all-start = ((bf16[32,2,2048]{2,1,0:T(2,128)(2,1)}), bf16[32,2,2048]{2,1,0:T(2,128)(2,1)S(1)}, u32[]{:S(2)}, u32[]{:S(2)}) async-start(bf16[32,2,2048]{2,1,0:T(2,128)(2,1)} %reshape.541), calls=%async_computation | async-start | bytes 524288 | tf_op jit(solution)/shard_map/all_to_all | solution.py:160
  125.7 5.9 %copy-start.12 = (f32[2048]{0:T(1024)S(1)}, f32[2048]{0:T(1024)}, u32[]{:S(2)}) copy-start(f32[2048]{0:T(1024)} %param.22) | copy-start | bytes 24580
  196.3 6.1 %copy-start.15 = (bf16[2,2048,352]{1,2,0:T(8,128)(2,1)S(1)}, bf16[2,2048,352]{1,2,0:T(8,128)(2,1)}, u32[]{:S(2)}) copy-start(bf16[2,2048,352]{1,2,0:T(8,128)(2,1)} %param.25) | copy-start | bytes 8650756
  196.3 58.6 %all-to-all-start.1 = ((bf16[128,8,2048]{2,1,0:T(8,128)(2,1)}), bf16[128,8,2048]{2,1,0:T(8,128)(2,1)}, u32[]{:S(2)}, u32[]{:S(2)}) async-start(bf16[128,8,2048]{2,1,0:T(8,128)(2,1)} %bitcast.182), calls=%async_computation.1 | async-start | bytes 8388608 | tf_op jit(solution)/shard_map/all_to_all | solution.py:194
  254.8 69.1 %all-to-all-start.4 = ((bf16[128,8,2048]{2,1,0:T(8,128)(2,1)}), bf16[128,8,2048]{2,1,0:T(8,128)(2,1)}, u32[]{:S(2)}, u32[]{:S(2)}) async-start(bf16[128,8,2048]{2,1,0:T(8,128)(2,1)} %convert_bitcast_fusion), calls=%async_computation.4 | async-start | bytes 8388608 | tf_op jit(solution)/shard_map/all_to_all | solution.py:201
  286.0 44.9 %copy-start.13 = (f32[64,6]{0,1:T(8,128)S(1)}, f32[64,6]{0,1:T(8,128)}, u32[]{:S(2)}) copy-start(f32[64,6]{0,1:T(8,128)} %param.24) | copy-start | bytes 4612
  323.9 59.4 %all-to-all-start.2 = ((bf16[128,8,2048]{2,1,0:T(8,128)(2,1)}), bf16[128,8,2048]{2,1,0:T(8,128)(2,1)}, u32[]{:S(2)}, u32[]{:S(2)}) async-start(bf16[128,8,2048]{2,1,0:T(8,128)(2,1)} %convert_bitcast_fusion.1), calls=%async_computation.2 | async-start | bytes 8388608 | tf_op jit(solution)/shard_map/all_to_all | solution.py:201
  394.3 6.3 %copy-start.1 = (bf16[192,32,256]{2,1,0:T(8,128)(2,1)S(1)}, bf16[192,32,256]{2,1,0:T(8,128)(2,1)}, u32[]{:S(2)}) copy-start(bf16[192,32,256]{2,1,0:T(8,128)(2,1)} %param.15) | copy-start | bytes 9437188
  (13 other events, 23.8 us)
Sparse Core Ops, SparseCore 0:
  9.6 55.3 all-gather.1

commit v4 on v3

--- a/solution.py
+++ b/solution.py
@@ -1,6 +1,10 @@
+import functools
+
 import jax
 import jax.numpy as jnp
 from jax import lax
+from jax.experimental import pallas as pl
+from jax.experimental.pallas import tpu as pltpu
 from jax.sharding import PartitionSpec as P
 
 HEADS = 16
@@ -14,38 +18,72 @@
     return lax.ppermute(array, axis, [(i, i ^ 1 << stride) for i in range(lax.axis_size(axis))])
 
 
-def local_attention(queries, cached, fresh_rows, length, cache_offset, span_offset):
-    head_size = queries.shape[1]
-    span_len = queries.shape[0]
-    page_count = cached.shape[0]
-    page_rows = cached.shape[1]
-    scale_factor = 1.0 / head_size**0.5
-    cache_scores = jnp.einsum(
-        "qd,pjd->qpj", queries, cached[:, :, :head_size], preferred_element_type=jnp.float32
-    )
-    cache_scores = cache_scores.reshape(span_len, page_count * page_rows) * scale_factor
-    page_ids = jnp.arange(page_count, dtype=jnp.int32)[:, None]
-    row_ids = jnp.arange(page_rows, dtype=jnp.int32)[None, :]
-    positions = (page_ids * PAGE + cache_offset + row_ids).reshape(-1)
-    cache_scores = jnp.where(positions[None, :] < length, cache_scores, -1e30)
-    new_keys = fresh_rows[:, head_size : 2 * head_size]
-    new_values = fresh_rows[:, 2 * head_size :]
-    span_scores = jnp.dot(queries, new_keys.T, preferred_element_type=jnp.float32) * scale_factor
-    key_pos = span_offset + jnp.arange(fresh_rows.shape[0], dtype=jnp.int32)
-    query_pos = jnp.arange(span_len, dtype=jnp.int32)
-    span_scores = jnp.where(key_pos[None, :] <= query_pos[:, None], span_scores, -1e30)
-    maximum = jnp.maximum(jnp.max(cache_scores, axis=1), jnp.max(span_scores, axis=1))
-    cache_weights = jnp.exp(cache_scores - maximum[:, None])
-    span_weights = jnp.exp(span_scores - maximum[:, None])
-    denominator = jnp.sum(cache_weights, axis=1) + jnp.sum(span_weights, axis=1)
-    rounded = cache_weights.astype(jnp.bfloat16).reshape(span_len, page_count, page_rows)
-    weighted = jnp.einsum(
-        "qpj,pjd->qd", rounded, cached[:, :, head_size:], preferred_element_type=jnp.float32
-    )
-    weighted = weighted + jnp.dot(
-        span_weights.astype(jnp.bfloat16), new_values, preferred_element_type=jnp.float32
-    )
-    return (weighted, maximum, denominator)
+def attn_body(scal_ref, q_ref, c_ref, f_ref, w_ref, m_ref, d_ref, *, block_q, page_rows, head):
+    item = pl.program_id(0)
+    qb = pl.program_id(1)
+    length = scal_ref[item]
+    cache_offset = scal_ref[4]
+    span_offset = scal_ref[5]
+    scale = 1.0 / head**0.5
+    q = q_ref[...]
+    cached = c_ref[...]
+    fresh = f_ref[...]
+    dims = (((1,), (1,)), ((), ()))
+    cs = lax.dot_general(q, cached[:, :head], dims, preferred_element_type=jnp.float32) * scale
+    n = lax.broadcasted_iota(jnp.int32, cs.shape, 1)
+    pos = (n // page_rows) * PAGE + cache_offset + n % page_rows
+    cs = jnp.where(pos < length, cs, -1e30)
+    ss = lax.dot_general(q, fresh[:, head:2 * head], dims, preferred_element_type=jnp.float32) * scale
+    kpos = span_offset + lax.broadcasted_iota(jnp.int32, ss.shape, 1)
+    qpos = qb * block_q + lax.broadcasted_iota(jnp.int32, ss.shape, 0)
+    ss = jnp.where(kpos <= qpos, ss, -1e30)
+    mx = jnp.maximum(jnp.max(cs, axis=1, keepdims=True), jnp.max(ss, axis=1, keepdims=True))
+    cw = jnp.exp(cs - mx)
+    sw = jnp.exp(ss - mx)
+    den = jnp.sum(cw, axis=1, keepdims=True) + jnp.sum(sw, axis=1, keepdims=True)
+    acc = jnp.dot(cw.astype(jnp.bfloat16), cached[:, head:], preferred_element_type=jnp.float32)
+    acc = acc + jnp.dot(sw.astype(jnp.bfloat16), fresh[:, 2 * head:], preferred_element_type=jnp.float32)
+    w_ref[...] = acc
+    m_ref[...] = mx
+    d_ref[...] = den
+
+
+def attention_kernel(queries, cached, fresh, lengths, cache_offset, span_offset, interpret=False):
+    items, span, head = queries.shape
+    pages, page_rows = cached.shape[1], cached.shape[2]
+    keys = pages * page_rows
+    cached = cached.reshape(items, keys, cached.shape[3])
+    fresh_rows = fresh.shape[1]
+    block_q = 256
+    scal = jnp.concatenate(
+        [lengths.astype(jnp.int32), jnp.stack([cache_offset, span_offset]).astype(jnp.int32)]
+    )
+    body = functools.partial(attn_body, block_q=block_q, page_rows=page_rows, head=head)
+    grid_spec = pltpu.PrefetchScalarGridSpec(
+        num_scalar_prefetch=1,
+        grid=(items, span // block_q),
+        in_specs=[
+            pl.BlockSpec((None, block_q, head), lambda i, b, s: (i, b, 0)),
+            pl.BlockSpec((None, keys, 2 * head), lambda i, b, s: (i, 0, 0)),
+            pl.BlockSpec((None, fresh_rows, 3 * head), lambda i, b, s: (i, 0, 0)),
+        ],
+        out_specs=[
+            pl.BlockSpec((None, block_q, head), lambda i, b, s: (i, b, 0)),
+            pl.BlockSpec((None, block_q, 1), lambda i, b, s: (i, b, 0)),
+            pl.BlockSpec((None, block_q, 1), lambda i, b, s: (i, b, 0)),
+        ],
+    )
+    weighted, mx, den = pl.pallas_call(
+        body,
+        grid_spec=grid_spec,
+        out_shape=[
+            jax.ShapeDtypeStruct((items, span, head), jnp.float32),
+            jax.ShapeDtypeStruct((items, span, 1), jnp.float32),
+            jax.ShapeDtypeStruct((items, span, 1), jnp.float32),
+        ],
+        interpret=interpret,
+    )(scal, queries, cached, fresh)
+    return weighted, mx[..., 0], den[..., 0]
 
 
 def run_experts(slot_rows, expert_gate, expert_up, expert_down):
@@ -127,17 +165,14 @@
     upper_half = jnp.where(side_index == 0, other_queries, own_queries)
     queries = jnp.concatenate([lower_half, upper_half], axis=1)[:, None]
 
-    def one_request(operands):
-        return local_attention(
-            operands[0],
-            operands[1],
-            operands[2],
-            operands[3],
-            side_index * rows_per_head,
-            side_index * fresh_per,
-        )
-
-    head_results = lax.map(one_request, (queries[:, 0], dense_cache, new_tokens, lengths))
+    head_results = attention_kernel(
+        queries[:, 0],
+        dense_cache,
+        new_tokens,
+        lengths,
+        side_index * rows_per_head,
+        side_index * fresh_per,
+    )
     weighted, maximum, denominator = head_results
     half_dim = HD // 2
     given_part = lax.dynamic_slice_in_dim(weighted, (1 - side_index) * half_dim, half_dim, 2)

time: 412 us -> 362 us (0.88)
  local copies, waits for them, and re-layouts: 63.8 us -> 40.7 us
  matrix products: 56.3 us -> 33.9 us
  Pallas kernels: 0 us -> 13.7 us
  starting transfers between devices: 47.7 us -> 38.3 us
  other arithmetic: 29.1 us -> 24.7 us
    dot_general x16 -> x0, matrix products: 22.4 us -> none  [the longest x4 9.57 us: local_attention(): jnp.einsum('qpj,pjd->qd', rounded, cached[:, :, head_size:], preferred_el...]
    pallas_call x0 -> x1, Pallas kernels: none -> 13.7 us  [attention_kernel(): pl.pallas_call(body, grid_spec=grid_spec, out_shape=[jax.ShapeDtypeStruct...]
    all_to_all x2, starting transfers between devices: 23.6 us -> 13 us  [shards(): lax.all_to_all(partial_value, ('dp', 'tensor'), split_axis=0, concat_axis...]
    convert_element_type x4 -> x0, local copies, waits for them, and re-layouts: 10.2 us -> none  [local_attention(): cache_weights.astype(jnp.bfloat16).reshape(span_len, page_count, page_rows)]
    squeeze x8 -> x0, local copies, waits for them, and re-layouts: 9.04 us -> none  [shards(): lax.map(one_request, (queries[:, 0], dense_cache, new_tokens, lengths))]
    reduce_sum x8 -> x0, other arithmetic: 4.56 us -> none  [local_attention(): denominator = jnp.sum(cache_weights, axis=1) + jnp.sum(span_weights, axis=1)]
  transfers between devices with their start and end apart: 15 -> 15, of which waited for: 10 -> 9; matrix products, arithmetic and copies ran while one was open for 29% -> 19% of each run, Pallas kernels for 0% -> 4%
where the time goes in v4:
time: 362 us; the launch traced here: 361 us
  waiting for transfers between devices  136 us (38%)
  blocking collectives  58.9 us (16%)
  local copies, waits for them, and re-layouts  40.7 us (11%)
  starting transfers between devices  38.3 us (11%)
  matrix products  33.9 us (9%)
  other arithmetic  24.7 us (7%)
  between operations  13.9 us (4%)
  Pallas kernels  13.7 us (4%)
    all_to_all x2, waiting for transfers between devices, shards(): lax.all_to_all(partial_value, ('dp', 'tensor'), split_axis=0, concat_axis...  78.9 us
    all_to_all x1, blocking collectives, shards(): lax.all_to_all(fanned, ('dp', 'tensor'), split_axis=0, concat_axis=0, til...  58.9 us
    all_to_all x1, waiting for transfers between devices, shards(): lax.all_to_all(fanned, ('dp', 'tensor'), split_axis=0, concat_axis=0, til...  38.1 us
    dot_general x2, matrix products, shards(): jnp.dot(active, expert_down[k], preferred_element_type=jnp.float32)  18.8 us
    gather x4, local copies, waits for them, and re-layouts, shards(): picked = slot_out[owner_slot] * weight[:, None]  15.7 us
    pallas_call x1, Pallas kernels, attention_kernel(): pl.pallas_call(body, grid_spec=grid_spec, out_shape=[jax.ShapeDtypeStruct...  13.7 us
    all_to_all x2, starting transfers between devices, shards(): lax.all_to_all(partial_value, ('dp', 'tensor'), split_axis=0, concat_axis...  13 us
    dot_general x2, matrix products, shards(): jnp.dot(flat_rows, expert_gate[k], preferred_element_type=jnp.float32)  9.99 us
  transfers between devices with their start and end apart: 15, of which 9 were waited for; matrix products, arithmetic and copies ran while one was open for 19% of the time, Pallas kernels for 4%

profile of v4, /device:TPU:0, one launch (start us, length us, event | category | flops | bytes accessed | tf_op | source)
XLA Modules:
  0.0 360.6 jit_solution(1931194099837508814)
XLA Ops:
  24.4 3.1 collective-permute-done.1
  35.1 13.7 %shard_map.127 = (f32[4,512,128]{2,1,0:T(8,128)}, f32[4,512,1]{2,1,0:T(8,128)}, f32[4,512,1]{2,1,0:T(8,128)}) custom-call(s32[6]{0:T(128)} %pad_add_fusion.scal_ref, bf16[4,512,128]{2,1,0:T(8,128)(2,1)} %pad_maximum_fusion.1.q_ref, bf16[4,2048,256]{2,1,0:T(8,128)(2,1)} %bitcast.131, bf16[4,256,384]{2,1,0:T(8,128)(2,1)} %copy-done.4), custom_call_target="tpu_custom_call" | custom-call | tf_op jit(solution)/shard_map/pallas_call | solution.py:76
  62.3 3.6 collective-permute-done.7
  70.6 8.6 %all-to-all-start = ((bf16[32,2,2048]{2,1,0:T(2,128)(2,1)}), bf16[32,2,2048]{2,1,0:T(2,128)(2,1)S(1)}, u32[]{:S(2)}, u32[]{:S(2)}) async-start(bf16[32,2,2048]{2,1,0:T(2,128)(2,1)} %reshape.466), calls=%async_computation | async-start | bytes 524288 | tf_op jit(solution)/shard_map/all_to_all | solution.py:195
  79.3 8.7 %all-to-all-done = bf16[32,2,2048]{2,1,0:T(2,128)(2,1)S(1)} async-done(((bf16[32,2,2048]{2,1,0:T(2,128)(2,1)}), bf16[32,2,2048]{2,1,0:T(2,128)(2,1)S(1)}, u32[]{:S(2)}, u32[]{:S(2)}) %all-to-all-start) | async-done | bytes 262176 | tf_op jit(solution)/shard_map/all_to_all | solution.py:195
  89.2 5.1 %multiply_reduce_fusion.2 = (f32[64]{0:T(128)S(1)}, f32[64,2048]{1,0:T(8,128)S(1)}) fusion(bf16[64,2048]{1,0:T(8,128)(2,1)S(1)} %reshape.372, bf16[2048,2048]{1,0:T(8,128)(2,1)} %all-gather.2.cloned.1.call-done, bf16[64,2048]{1,0:T(8,128)(2,1)S(1)} %copy-done.9), kind=kOutput, calls=%fused_computation.54 | convolution fusion | flops 537395136 | bytes 9437440 | tf_op jit(solution)/shard_map/dot_general | solution.py:198
  98.5 58.9 %all_to_all.25 = bf16[128,8,2048]{2,1,0:T(8,128)(2,1)} all-to-all(bf16[128,8,2048]{2,1,0:T(8,128)(2,1)S(1)} %bitcast.133), channel_id=1, replica_groups=mesh['dp'=4,'tensor'=32] {'dp','tensor'}, dimensions={0} | all-to-all | bytes 8388608 | tf_op jit(solution)/shard_map/all_to_all | solution.py:229
  160.0 6.1 %all-to-all-start.1 = ((bf16[128,8,2048]{2,1,0:T(8,128)(2,1)}), bf16[128,8,2048]{2,1,0:T(8,128)(2,1)}, u32[]{:S(2)}, u32[]{:S(2)}) async-start(bf16[128,8,2048]{2,1,0:T(8,128)(2,1)} %bitcast.132), calls=%async_computation.1 | async-start | bytes 8388608 | tf_op jit(solution)/shard_map/all_to_all | solution.py:229
  166.1 5.0 %fusion.2 = f32[1024,352]{0,1:T(8,128)} fusion(bf16[128,8,2048]{2,1,0:T(8,128)(2,1)} %all_to_all.25, bf16[2,2048,352]{1,2,0:T(8,128)(2,1)S(1)} %copy-done.15), kind=kOutput, calls=%fused_computation.13 | convolution fusion | flops 1476395008 | bytes 7077888 | tf_op jit(solution)/shard_map/dot_general | solution.py:231
  171.0 9.4 %convert_bitcast_fusion = bf16[128,8,2048]{2,1,0:T(8,128)(2,1)} fusion(bf16[2,352,2048]{2,1,0:T(8,128)(2,1)} %param.25, bf16[2,2048,352]{1,2,0:T(8,128)(2,1)} %param.24, bf16[128,8,2048]{2,1,0:T(8,128)(2,1)} %all_to_all.25, f32[1024,352]{0,1:T(8,128)} %fusion.2), kind=kOutput, calls=%fused_computation.20 | convolution fusion | flops 2957049856 | bytes 12713984 | tf_op jit(solution)/shard_map/dot_general | solution.py:234
  180.5 38.1 %all-to-all-done.1 = bf16[128,8,2048]{2,1,0:T(8,128)(2,1)} async-done(((bf16[128,8,2048]{2,1,0:T(8,128)(2,1)}), bf16[128,8,2048]{2,1,0:T(8,128)(2,1)}, u32[]{:S(2)}, u32[]{:S(2)}) %all-to-all-start.1) | async-done | bytes 4194336 | tf_op jit(solution)/shard_map/all_to_all | solution.py:229
  218.5 7.2 %all-to-all-start.4 = ((bf16[128,8,2048]{2,1,0:T(8,128)(2,1)}), bf16[128,8,2048]{2,1,0:T(8,128)(2,1)}, u32[]{:S(2)}, u32[]{:S(2)}) async-start(bf16[128,8,2048]{2,1,0:T(8,128)(2,1)} %convert_bitcast_fusion), calls=%async_computation.4 | async-start | bytes 8388608 | tf_op jit(solution)/shard_map/all_to_all | solution.py:236
  225.7 5.0 %fusion.6 = f32[1024,352]{0,1:T(8,128)} fusion(bf16[128,8,2048]{2,1,0:T(8,128)(2,1)} %all-to-all-done.1, bf16[2,2048,352]{1,2,0:T(8,128)(2,1)S(1)} %copy-done.15), kind=kOutput, calls=%fused_computation.17 | convolution fusion | flops 1476395008 | bytes 7077888 | tf_op jit(solution)/shard_map/dot_general | solution.py:231
  230.7 9.4 %convert_bitcast_fusion.1 = bf16[128,8,2048]{2,1,0:T(8,128)(2,1)} fusion(bf16[2,352,2048]{2,1,0:T(8,128)(2,1)} %param.25, bf16[2,2048,352]{1,2,0:T(8,128)(2,1)} %param.24, bf16[128,8,2048]{2,1,0:T(8,128)(2,1)} %all-to-all-done.1, f32[1024,352]{0,1:T(8,128)} %fusion.6), kind=kOutput, calls=%fused_computation.22 | convolution fusion | flops 2957049856 | bytes 12713984 | tf_op jit(solution)/shard_map/dot_general | solution.py:234
  240.1 37.9 %all-to-all-done.4 = bf16[128,8,2048]{2,1,0:T(8,128)(2,1)} async-done(((bf16[128,8,2048]{2,1,0:T(8,128)(2,1)}), bf16[128,8,2048]{2,1,0:T(8,128)(2,1)}, u32[]{:S(2)}, u32[]{:S(2)}) %all-to-all-start.4) | async-done | bytes 4194336 | tf_op jit(solution)/shard_map/all_to_all | solution.py:236
  278.0 5.8 %all-to-all-start.2 = ((bf16[128,8,2048]{2,1,0:T(8,128)(2,1)}), bf16[128,8,2048]{2,1,0:T(8,128)(2,1)}, u32[]{:S(2)}, u32[]{:S(2)}) async-start(bf16[128,8,2048]{2,1,0:T(8,128)(2,1)} %convert_bitcast_fusion.1), calls=%async_computation.2 | async-start | bytes 8388608 | tf_op jit(solution)/shard_map/all_to_all | solution.py:236
  284.2 3.2 convert_reduce_fusion
  287.4 3.3 gather_fusion.7
  290.7 4.6 %gather.43 = f32[64,6,2048]{2,1,0:T(8,128)} reshape(f32[384,2048]{1,0:T(8,128)} %gather_fusion.7) | data formatting | bytes 6291456 | tf_op jit(solution)/shard_map/gather | solution.py:243
  295.3 41.1 %all-to-all-done.2 = bf16[128,8,2048]{2,1,0:T(8,128)(2,1)} async-done(((bf16[128,8,2048]{2,1,0:T(8,128)(2,1)}), bf16[128,8,2048]{2,1,0:T(8,128)(2,1)}, u32[]{:S(2)}, u32[]{:S(2)}) %all-to-all-start.2) | async-done | bytes 4194336 | tf_op jit(solution)/shard_map/all_to_all | solution.py:236
  336.4 3.2 convert_reduce_fusion.1
  339.5 3.3 gather_fusion.6
  342.8 4.6 %gather.41 = f32[64,6,2048]{2,1,0:T(8,128)} reshape(f32[384,2048]{1,0:T(8,128)} %gather_fusion.6) | data formatting | bytes 6291456 | tf_op jit(solution)/shard_map/gather | solution.py:243
  347.4 3.9 %multiply_reduce_fusion = f32[64,2048]{1,0:T(8,128)S(1)} fusion(f32[64,6,2048]{2,1,0:T(8,128)} %gather.43, f32[64,6]{1,0:T(8,128)S(1)} %copy.40), kind=kLoop, calls=%fused_computation.19 | loop fusion | flops 1441792 | bytes 3671552 | tf_op jit(solution)/shard_map/reduce_sum | solution.py:244
  (124 shorter events, 54.2 us)
Async XLA Ops:
  6.5 23.8 %copy-start = (bf16[192,32,256]{2,1,0:T(8,128)(2,1)S(1)}, bf16[192,32,256]{2,1,0:T(8,128)(2,1)}, u32[]{:S(2)}) copy-start(bf16[192,32,256]{2,1,0:T(8,128)(2,1)} %param.13) | copy-start | bytes 9437188
  6.5 12.9 %copy-start.14 = (s32[16]{0:T(128)S(1)}, s32[16]{0:T(128)}, u32[]{:S(2)}) copy-start(s32[16]{0:T(128)} %param.15) | copy-start | bytes 196
  6.5 12.5 %copy-start.11 = (s32[64,6]{0,1:T(8,128)S(1)}, s32[64,6]{0,1:T(8,128)}, u32[]{:S(2)}) copy-start(s32[64,6]{0,1:T(8,128)} %param.21) | copy-start | bytes 4612
  6.5 13.2 %copy-start.10 = (s32[4,64]{1,0:T(4,128)S(1)}, s32[4,64]{1,0:T(4,128)}, u32[]{:S(2)}) copy-start(s32[4,64]{1,0:T(4,128)} %param.14) | copy-start | bytes 3076
  6.5 16.9 %copy-start.2 = (s32[16]{0:T(128)S(1)}, s32[16]{0:T(128)}, u32[]{:S(2)}) copy-start(s32[16]{0:T(128)} %param.16) | copy-start | bytes 196
  6.5 82.6 %all-gather.2.cloned.1.call-start = ((), (), s32[]{:S(2)}) async-start(), calls=%async_computation.5 | async-start | bytes 8650752 | tf_op jit(solution)/shard_map/all_gather | solution.py:197
  13.7 10.6 %collective-permute-start.2 = (bf16[256,384]{1,0:T(8,128)(2,1)}, bf16[256,384]{1,0:T(8,128)(2,1)}, u32[]{:S(2)}, u32[]{:S(2)}) collective-permute-start(bf16[256,384]{1,0:T(8,128)(2,1)} %get-tuple-element.23), channel_id=1, source_target_pairs={{0,32},{32,64},{64,96},{96,0},{1,33},{33,65},{65,97},{97,1},{2,34}... | collective-permute-start | bytes 589832 | tf_op jit(solution)/shard_map/ppermute | solution.py:152
  15.4 9.0 %collective-permute-start = (bf16[256,384]{1,0:T(8,128)(2,1)}, bf16[256,384]{1,0:T(8,128)(2,1)}, u32[]{:S(2)}, u32[]{:S(2)}) collective-permute-start(bf16[256,384]{1,0:T(8,128)(2,1)} %get-tuple-element.22), channel_id=1, source_target_pairs={{0,96},{32,0},{64,32},{96,64},{1,97},{33,1},{65,33},{97,65},{2,98}... | collective-permute-start | bytes 589832 | tf_op jit(solution)/shard_map/ppermute | solution.py:152
  17.0 10.5 %collective-permute-start.1 = (bf16[256,384]{1,0:T(8,128)(2,1)}, bf16[256,384]{1,0:T(8,128)(2,1)}, u32[]{:S(2)}, u32[]{:S(2)}) collective-permute-start(bf16[256,384]{1,0:T(8,128)(2,1)} %get-tuple-element.21), channel_id=1, source_target_pairs={{0,64},{32,96},{64,0},{96,32},{1,65},{33,97},{65,1},{97,33},{2,66}... | collective-permute-start | bytes 589832 | tf_op jit(solution)/shard_map/ppermute | solution.py:152
  29.7 3.5 collective-permute-start.3
  50.5 6.5 %copy-start.7 = (f32[4,512,128]{2,1,0:T(8,128)S(1)}, f32[4,512,128]{2,1,0:T(8,128)}, u32[]{:S(2)}) copy-start(f32[4,512,128]{2,1,0:T(8,128)} %get-tuple-element.8) | copy-start | bytes 3145732
  51.6 4.0 %collective-permute-start.5 = (f32[4,512,64]{1,2,0:T(8,128)}, f32[4,512,64]{1,2,0:T(8,128)}, u32[]{:S(2)}, u32[]{:S(2)}) collective-permute-start(f32[4,512,64]{1,2,0:T(8,128)} %copy.32), channel_id=1, source_target_pairs={{0,1},{1,0},{2,3},{3,2},{4,5},{5,4},{6,7},{7,6},{8,9},{9,8},{10,11... | collective-permute-start | bytes 1572872 | tf_op jit(solution)/shard_map/ppermute | solution.py:18
  53.7 1.3 collective-permute-start.4
  54.2 1.3 collective-permute-start.6
  58.3 7.6 %collective-permute-start.7 = (bf16[512,64]{1,0:T(8,128)(2,1)S(1)}, bf16[512,64]{1,0:T(8,128)(2,1)S(1)}, u32[]{:S(2)}, u32[]{:S(2)}) collective-permute-start(bf16[512,64]{1,0:T(8,128)(2,1)S(1)} %get-tuple-element.27), channel_id=1, source_target_pairs={{0,32},{32,64},{64,96},{96,0},{1,33},{33,65},{65,97},{97,1},{2,34}... | collective-permute-start | bytes 196616 | tf_op jit(solution)/shard_map/ppermute | solution.py:190
  59.5 8.6 %collective-permute-start.8 = (bf16[512,64]{1,0:T(8,128)(2,1)S(1)}, bf16[512,64]{1,0:T(8,128)(2,1)S(1)}, u32[]{:S(2)}, u32[]{:S(2)}) collective-permute-start(bf16[512,64]{1,0:T(8,128)(2,1)S(1)} %get-tuple-element.26), channel_id=1, source_target_pairs={{0,64},{32,96},{64,0},{96,32},{1,65},{33,97},{65,1},{97,33},{2,66}... | collective-permute-start | bytes 196616 | tf_op jit(solution)/shard_map/ppermute | solution.py:190
  61.6 7.1 %collective-permute-start.9 = (bf16[512,64]{1,0:T(8,128)(2,1)S(1)}, bf16[512,64]{1,0:T(8,128)(2,1)S(1)}, u32[]{:S(2)}, u32[]{:S(2)}) collective-permute-start(bf16[512,64]{1,0:T(8,128)(2,1)S(1)} %get-tuple-element.25), channel_id=1, source_target_pairs={{0,96},{32,0},{64,32},{96,64},{1,97},{33,1},{65,33},{97,65},{2,98}... | collective-permute-start | bytes 196616 | tf_op jit(solution)/shard_map/ppermute | solution.py:190
  68.7 20.5 %copy-start.9 = (bf16[64,2048]{1,0:T(8,128)(2,1)S(1)}, bf16[64,2048]{1,0:T(8,128)(2,1)}, u32[]{:S(2)}) copy-start(bf16[64,2048]{1,0:T(8,128)(2,1)} %param.18) | copy-start | bytes 786436
  70.6 17.4 %all-to-all-start = ((bf16[32,2,2048]{2,1,0:T(2,128)(2,1)}), bf16[32,2,2048]{2,1,0:T(2,128)(2,1)S(1)}, u32[]{:S(2)}, u32[]{:S(2)}) async-start(bf16[32,2,2048]{2,1,0:T(2,128)(2,1)} %reshape.466), calls=%async_computation | async-start | bytes 524288 | tf_op jit(solution)/shard_map/all_to_all | solution.py:195
  160.0 58.6 %all-to-all-start.1 = ((bf16[128,8,2048]{2,1,0:T(8,128)(2,1)}), bf16[128,8,2048]{2,1,0:T(8,128)(2,1)}, u32[]{:S(2)}, u32[]{:S(2)}) async-start(bf16[128,8,2048]{2,1,0:T(8,128)(2,1)} %bitcast.132), calls=%async_computation.1 | async-start | bytes 8388608 | tf_op jit(solution)/shard_map/all_to_all | solution.py:229
  218.5 59.5 %all-to-all-start.4 = ((bf16[128,8,2048]{2,1,0:T(8,128)(2,1)}), bf16[128,8,2048]{2,1,0:T(8,128)(2,1)}, u32[]{:S(2)}, u32[]{:S(2)}) async-start(bf16[128,8,2048]{2,1,0:T(8,128)(2,1)} %convert_bitcast_fusion), calls=%async_computation.4 | async-start | bytes 8388608 | tf_op jit(solution)/shard_map/all_to_all | solution.py:236
  240.1 43.9 %copy-start.13 = (f32[64,6]{0,1:T(8,128)S(1)}, f32[64,6]{0,1:T(8,128)}, u32[]{:S(2)}) copy-start(f32[64,6]{0,1:T(8,128)} %param.22) | copy-start | bytes 4612
  278.0 58.3 %all-to-all-start.2 = ((bf16[128,8,2048]{2,1,0:T(8,128)(2,1)}), bf16[128,8,2048]{2,1,0:T(8,128)(2,1)}, u32[]{:S(2)}, u32[]{:S(2)}) async-start(bf16[128,8,2048]{2,1,0:T(8,128)(2,1)} %convert_bitcast_fusion.1), calls=%async_computation.2 | async-start | bytes 8388608 | tf_op jit(solution)/shard_map/all_to_all | solution.py:236
  347.4 6.3 %copy-start.1 = (bf16[192,32,256]{2,1,0:T(8,128)(2,1)S(1)}, bf16[192,32,256]{2,1,0:T(8,128)(2,1)}, u32[]{:S(2)}) copy-start(bf16[192,32,256]{2,1,0:T(8,128)(2,1)} %param.13) | copy-start | bytes 9437188
  (7 other events, 24.3 us)
Sparse Core Ops, SparseCore 0:
  9.6 55.3 all-gather.1

commit v5 on v4

--- a/solution.py
+++ b/solution.py
@@ -184,15 +184,16 @@
     combined = kept_part * own_scale[..., None] + received_part * theirs[..., None]
     attended = combined / (denominator * own_scale + other_den * theirs)[..., None]
     attended = attended.astype(jnp.bfloat16)
-    back = [attended[0]]
-    for j in range(1, group_count):
-        back.append(
-            lax.ppermute(attended[j], "dp", [(i, (i + j) % group_count) for i in range(group_count)])
-        )
-    attended = jnp.stack(back)[(group_index - source) % group_count]
     tok_rows = residual_in.shape[0]
-    head_out = attended.reshape(tensor_size, tok_rows, half_dim)
-    owned = lax.all_to_all(head_out, "tensor", split_axis=0, concat_axis=0, tiled=True)
+    chunks = span_len // tok_rows
+    by_dest = attended[(shifts - group_index) % group_count]
+    by_dest = by_dest.reshape(group_count, 1, chunks, tok_rows, half_dim)
+    send = jnp.broadcast_to(by_dest, (group_count, requests_here, chunks, tok_rows, half_dim))
+    send = send.reshape(group_count * tensor_size, tok_rows, half_dim)
+    received = lax.all_to_all(send, ("dp", "tensor"), split_axis=0, concat_axis=0, tiled=True)
+    received = received.reshape(group_count, tensor_size, tok_rows, half_dim)
+    home_of_slot = source[lax.axis_index("tensor") // chunks]
+    owned = lax.dynamic_index_in_dim(received, home_of_slot, 0, keepdims=False)
     owned = owned.transpose(1, 0, 2).reshape(tok_rows, tensor_size * half_dim)
     full_weight = lax.all_gather(out_weight, "tensor", axis=0, tiled=True)
     projected = jnp.dot(owned, full_weight, preferred_element_type=jnp.float32)

time: 362 us -> 367 us (1.014)
  local copies, waits for them, and re-layouts: 40.7 us -> 44.8 us
    all_to_all x1, waiting for transfers between devices: 8.7 us -> 16 us  [shards(): lax.all_to_all(send, ('dp', 'tensor'), split_axis=0, concat_axis=0, tiled...]
    ppermute x3 -> x0, waiting for transfers between devices: 6.39 us -> none  [shards(): lax.ppermute(attended[j], 'dp', [(i, (i + j) % group_count) for i in rang...]
    ppermute x3 -> x0, starting transfers between devices: 3.99 us -> none  [shards(): lax.ppermute(attended[j], 'dp', [(i, (i + j) % group_count) for i in rang...]
  transfers between devices with their start and end apart: 15 -> 12, of which waited for: 9 -> 8; matrix products, arithmetic and copies ran while one was open for 19% -> 20% of each run, Pallas kernels for 4% -> 4%
where the time goes in v5:
time: 367 us; the launch traced here: 366 us
  waiting for transfers between devices  139 us (38%)
  blocking collectives  57.6 us (16%)
  local copies, waits for them, and re-layouts  44.8 us (12%)
  starting transfers between devices  36.4 us (10%)
  matrix products  33.9 us (9%)
  other arithmetic  24.5 us (7%)
  between operations  15.8 us (4%)
  Pallas kernels  13.9 us (4%)
    all_to_all x2, waiting for transfers between devices, shards(): lax.all_to_all(partial_value, ('dp', 'tensor'), split_axis=0, concat_axis...  78.9 us
    all_to_all x1, blocking collectives, shards(): lax.all_to_all(fanned, ('dp', 'tensor'), split_axis=0, concat_axis=0, til...  57.6 us
    all_to_all x1, waiting for transfers between devices, shards(): lax.all_to_all(fanned, ('dp', 'tensor'), split_axis=0, concat_axis=0, til...  38.1 us
    dot_general x2, matrix products, shards(): jnp.dot(active, expert_down[k], preferred_element_type=jnp.float32)  18.8 us
    all_to_all x1, waiting for transfers between devices, shards(): lax.all_to_all(send, ('dp', 'tensor'), split_axis=0, concat_axis=0, tiled...  16 us
    gather x4, local copies, waits for them, and re-layouts, shards(): picked = slot_out[owner_slot] * weight[:, None]  15.7 us
    pallas_call x1, Pallas kernels, attention_kernel(): pl.pallas_call(body, grid_spec=grid_spec, out_shape=[jax.ShapeDtypeStruct...  13.9 us
    all_to_all x2, starting transfers between devices, shards(): lax.all_to_all(partial_value, ('dp', 'tensor'), split_axis=0, concat_axis...  13.3 us
  transfers between devices with their start and end apart: 12, of which 8 were waited for; matrix products, arithmetic and copies ran while one was open for 20% of the time, Pallas kernels for 4%

profile of v5, /device:TPU:0, one launch (start us, length us, event | category | flops | bytes accessed | tf_op | source)
XLA Modules:
  0.0 366.0 jit_solution(4609933651114688267)
XLA Ops:
  23.5 4.0 %collective-permute-done.1 = bf16[256,384]{1,0:T(8,128)(2,1)} collective-permute-done((bf16[256,384]{1,0:T(8,128)(2,1)}, bf16[256,384]{1,0:T(8,128)(2,1)}, u32[]{:S(2)}, u32[]{:S(2)}) %collective-permute-start.1) | collective-permute-done | bytes 196640 | tf_op jit(solution)/shard_map/ppermute | solution.py:152
  31.4 2.8 gather_fusion.3
  36.6 13.9 %shard_map.127 = (f32[4,512,128]{2,1,0:T(8,128)}, f32[4,512,1]{2,1,0:T(8,128)}, f32[4,512,1]{2,1,0:T(8,128)}) custom-call(s32[6]{0:T(128)} %pad_add_fusion.scal_ref, bf16[4,512,128]{2,1,0:T(8,128)(2,1)} %pad_maximum_fusion.1.q_ref, bf16[4,2048,256]{2,1,0:T(8,128)(2,1)} %bitcast.130, bf16[4,256,384]{2,1,0:T(8,128)(2,1)} %copy-done.4), custom_call_target="tpu_custom_call" | custom-call | tf_op jit(solution)/shard_map/pallas_call | solution.py:76
  63.5 9.9 %all-to-all-start = ((bf16[128,2,2048]{2,1,0:T(2,128)(2,1)}), bf16[128,2,2048]{2,1,0:T(2,128)(2,1)S(1)}, u32[]{:S(2)}, u32[]{:S(2)}) async-start(bf16[128,2,2048]{2,1,0:T(2,128)(2,1)} %reshape.520), calls=%async_computation | async-start | bytes 2097152 | tf_op jit(solution)/shard_map/all_to_all | solution.py:193
  76.5 16.0 %all-to-all-done = bf16[128,2,2048]{2,1,0:T(2,128)(2,1)S(1)} async-done(((bf16[128,2,2048]{2,1,0:T(2,128)(2,1)}), bf16[128,2,2048]{2,1,0:T(2,128)(2,1)S(1)}, u32[]{:S(2)}, u32[]{:S(2)}) %all-to-all-start) | async-done | bytes 1048608 | tf_op jit(solution)/shard_map/all_to_all | solution.py:193
  94.8 5.1 %multiply_reduce_fusion.2 = (f32[64]{0:T(128)S(1)}, f32[64,2048]{1,0:T(8,128)S(1)}) fusion(bf16[64,2048]{1,0:T(8,128)(2,1)S(1)} %reshape.427, bf16[2048,2048]{1,0:T(8,128)(2,1)} %all-gather.2.cloned.1.call-done, bf16[64,2048]{1,0:T(8,128)(2,1)S(1)} %copy-done.9), kind=kOutput, calls=%fused_computation.53 | convolution fusion | flops 537395136 | bytes 9437440 | tf_op jit(solution)/shard_map/dot_general | solution.py:199
  104.1 57.6 %all_to_all.25 = bf16[128,8,2048]{2,1,0:T(8,128)(2,1)} all-to-all(bf16[128,8,2048]{2,1,0:T(8,128)(2,1)S(1)} %bitcast.132), channel_id=1, replica_groups=mesh['dp'=4,'tensor'=32] {'dp','tensor'}, dimensions={0} | all-to-all | bytes 8388608 | tf_op jit(solution)/shard_map/all_to_all | solution.py:230
  164.2 7.0 %all-to-all-start.1 = ((bf16[128,8,2048]{2,1,0:T(8,128)(2,1)}), bf16[128,8,2048]{2,1,0:T(8,128)(2,1)}, u32[]{:S(2)}, u32[]{:S(2)}) async-start(bf16[128,8,2048]{2,1,0:T(8,128)(2,1)} %bitcast.131), calls=%async_computation.1 | async-start | bytes 8388608 | tf_op jit(solution)/shard_map/all_to_all | solution.py:230
  171.2 5.0 %fusion.2 = f32[1024,352]{0,1:T(8,128)} fusion(bf16[128,8,2048]{2,1,0:T(8,128)(2,1)} %all_to_all.25, bf16[2,2048,352]{1,2,0:T(8,128)(2,1)S(1)} %copy-done.15), kind=kOutput, calls=%fused_computation.13 | convolution fusion | flops 1476395008 | bytes 7077888 | tf_op jit(solution)/shard_map/dot_general | solution.py:232
  176.2 9.4 %convert_bitcast_fusion = bf16[128,8,2048]{2,1,0:T(8,128)(2,1)} fusion(bf16[2,352,2048]{2,1,0:T(8,128)(2,1)} %param.25, bf16[2,2048,352]{1,2,0:T(8,128)(2,1)} %param.24, bf16[128,8,2048]{2,1,0:T(8,128)(2,1)} %all_to_all.25, f32[1024,352]{0,1:T(8,128)} %fusion.2), kind=kOutput, calls=%fused_computation.20 | convolution fusion | flops 2957049856 | bytes 12713984 | tf_op jit(solution)/shard_map/dot_general | solution.py:235
  185.6 38.1 %all-to-all-done.1 = bf16[128,8,2048]{2,1,0:T(8,128)(2,1)} async-done(((bf16[128,8,2048]{2,1,0:T(8,128)(2,1)}), bf16[128,8,2048]{2,1,0:T(8,128)(2,1)}, u32[]{:S(2)}, u32[]{:S(2)}) %all-to-all-start.1) | async-done | bytes 4194336 | tf_op jit(solution)/shard_map/all_to_all | solution.py:230
  223.7 6.0 %all-to-all-start.4 = ((bf16[128,8,2048]{2,1,0:T(8,128)(2,1)}), bf16[128,8,2048]{2,1,0:T(8,128)(2,1)}, u32[]{:S(2)}, u32[]{:S(2)}) async-start(bf16[128,8,2048]{2,1,0:T(8,128)(2,1)} %convert_bitcast_fusion), calls=%async_computation.4 | async-start | bytes 8388608 | tf_op jit(solution)/shard_map/all_to_all | solution.py:237
  229.7 5.0 %fusion.6 = f32[1024,352]{0,1:T(8,128)} fusion(bf16[128,8,2048]{2,1,0:T(8,128)(2,1)} %all-to-all-done.1, bf16[2,2048,352]{1,2,0:T(8,128)(2,1)S(1)} %copy-done.15), kind=kOutput, calls=%fused_computation.17 | convolution fusion | flops 1476395008 | bytes 7077888 | tf_op jit(solution)/shard_map/dot_general | solution.py:232
  234.7 9.4 %convert_bitcast_fusion.1 = bf16[128,8,2048]{2,1,0:T(8,128)(2,1)} fusion(bf16[2,352,2048]{2,1,0:T(8,128)(2,1)} %param.25, bf16[2,2048,352]{1,2,0:T(8,128)(2,1)} %param.24, bf16[128,8,2048]{2,1,0:T(8,128)(2,1)} %all-to-all-done.1, f32[1024,352]{0,1:T(8,128)} %fusion.6), kind=kOutput, calls=%fused_computation.22 | convolution fusion | flops 2957049856 | bytes 12713984 | tf_op jit(solution)/shard_map/dot_general | solution.py:235
  244.1 38.1 %all-to-all-done.4 = bf16[128,8,2048]{2,1,0:T(8,128)(2,1)} async-done(((bf16[128,8,2048]{2,1,0:T(8,128)(2,1)}), bf16[128,8,2048]{2,1,0:T(8,128)(2,1)}, u32[]{:S(2)}, u32[]{:S(2)}) %all-to-all-start.4) | async-done | bytes 4194336 | tf_op jit(solution)/shard_map/all_to_all | solution.py:237
  282.2 7.2 %all-to-all-start.2 = ((bf16[128,8,2048]{2,1,0:T(8,128)(2,1)}), bf16[128,8,2048]{2,1,0:T(8,128)(2,1)}, u32[]{:S(2)}, u32[]{:S(2)}) async-start(bf16[128,8,2048]{2,1,0:T(8,128)(2,1)} %convert_bitcast_fusion.1), calls=%async_computation.2 | async-start | bytes 8388608 | tf_op jit(solution)/shard_map/all_to_all | solution.py:237
  289.9 3.2 convert_reduce_fusion
  293.1 3.3 gather_fusion.7
  296.3 4.6 %gather.43 = f32[64,6,2048]{2,1,0:T(8,128)} reshape(f32[384,2048]{1,0:T(8,128)} %gather_fusion.7) | data formatting | bytes 6291456 | tf_op jit(solution)/shard_map/gather | solution.py:244
  300.9 40.8 %all-to-all-done.2 = bf16[128,8,2048]{2,1,0:T(8,128)(2,1)} async-done(((bf16[128,8,2048]{2,1,0:T(8,128)(2,1)}), bf16[128,8,2048]{2,1,0:T(8,128)(2,1)}, u32[]{:S(2)}, u32[]{:S(2)}) %all-to-all-start.2) | async-done | bytes 4194336 | tf_op jit(solution)/shard_map/all_to_all | solution.py:237
  341.7 3.2 convert_reduce_fusion.1
  344.9 3.3 gather_fusion.6
  348.2 4.6 %gather.41 = f32[64,6,2048]{2,1,0:T(8,128)} reshape(f32[384,2048]{1,0:T(8,128)} %gather_fusion.6) | data formatting | bytes 6291456 | tf_op jit(solution)/shard_map/gather | solution.py:244
  352.8 3.9 %multiply_reduce_fusion = f32[64,2048]{1,0:T(8,128)S(1)} fusion(f32[64,6,2048]{2,1,0:T(8,128)} %gather.43, f32[64,6]{1,0:T(8,128)S(1)} %copy.52), kind=kLoop, calls=%fused_computation.19 | loop fusion | flops 1441792 | bytes 3671552 | tf_op jit(solution)/shard_map/reduce_sum | solution.py:245
  (120 shorter events, 48.9 us)
Async XLA Ops:
  6.5 24.8 %copy-start = (bf16[192,32,256]{2,1,0:T(8,128)(2,1)S(1)}, bf16[192,32,256]{2,1,0:T(8,128)(2,1)}, u32[]{:S(2)}) copy-start(bf16[192,32,256]{2,1,0:T(8,128)(2,1)} %param.13) | copy-start | bytes 9437188
  6.5 15.5 %copy-start.14 = (s32[16]{0:T(128)S(1)}, s32[16]{0:T(128)}, u32[]{:S(2)}) copy-start(s32[16]{0:T(128)} %param.15) | copy-start | bytes 196
  6.5 12.6 %copy-start.11 = (s32[64,6]{0,1:T(8,128)S(1)}, s32[64,6]{0,1:T(8,128)}, u32[]{:S(2)}) copy-start(s32[64,6]{0,1:T(8,128)} %param.21) | copy-start | bytes 4612
  6.5 15.8 %copy-start.10 = (s32[4,64]{1,0:T(4,128)S(1)}, s32[4,64]{1,0:T(4,128)}, u32[]{:S(2)}) copy-start(s32[4,64]{1,0:T(4,128)} %param.14) | copy-start | bytes 3076
  6.5 88.2 %all-gather.2.cloned.1.call-start = ((), (), s32[]{:S(2)}) async-start(), calls=%async_computation.5 | async-start | bytes 8650752 | tf_op jit(solution)/shard_map/all_gather | solution.py:198
  9.0 21.7 %copy-start.2 = (s32[16]{0:T(128)S(1)}, s32[16]{0:T(128)}, u32[]{:S(2)}) copy-start(s32[16]{0:T(128)} %param.16) | copy-start | bytes 196
  13.8 9.4 %collective-permute-start.2 = (bf16[256,384]{1,0:T(8,128)(2,1)}, bf16[256,384]{1,0:T(8,128)(2,1)}, u32[]{:S(2)}, u32[]{:S(2)}) collective-permute-start(bf16[256,384]{1,0:T(8,128)(2,1)} %get-tuple-element.21), channel_id=1, source_target_pairs={{0,32},{32,64},{64,96},{96,0},{1,33},{33,65},{65,97},{97,1},{2,34}... | collective-permute-start | bytes 589832 | tf_op jit(solution)/shard_map/ppermute | solution.py:152
  15.4 8.1 %collective-permute-start = (bf16[256,384]{1,0:T(8,128)(2,1)}, bf16[256,384]{1,0:T(8,128)(2,1)}, u32[]{:S(2)}, u32[]{:S(2)}) collective-permute-start(bf16[256,384]{1,0:T(8,128)(2,1)} %get-tuple-element.20), channel_id=1, source_target_pairs={{0,96},{32,0},{64,32},{96,64},{1,97},{33,1},{65,33},{97,65},{2,98}... | collective-permute-start | bytes 589832 | tf_op jit(solution)/shard_map/ppermute | solution.py:152
  17.0 10.5 %collective-permute-start.1 = (bf16[256,384]{1,0:T(8,128)(2,1)}, bf16[256,384]{1,0:T(8,128)(2,1)}, u32[]{:S(2)}, u32[]{:S(2)}) collective-permute-start(bf16[256,384]{1,0:T(8,128)(2,1)} %get-tuple-element.19), channel_id=1, source_target_pairs={{0,64},{32,96},{64,0},{96,32},{1,65},{33,97},{65,1},{97,33},{2,66}... | collective-permute-start | bytes 589832 | tf_op jit(solution)/shard_map/ppermute | solution.py:152
  30.4 4.3 %collective-permute-start.3 = (bf16[4,256,128]{2,1,0:T(8,128)(2,1)}, bf16[4,256,128]{2,1,0:T(8,128)(2,1)}, u32[]{:S(2)}, u32[]{:S(2)}) collective-permute-start(bf16[4,256,128]{2,1,0:T(8,128)(2,1)} %slice.80), channel_id=1, source_target_pairs={{0,1},{1,0},{2,3},{3,2},{4,5},{5,4},{6,7},{7,6},{8,9},{9,8},{10,11... | collective-permute-start | bytes 786440 | tf_op jit(solution)/shard_map/ppermute | solution.py:18
  50.6 5.1 %copy-start.8 = (f32[4,512,1]{2,1,0:T(8,128)S(1)}, f32[4,512,1]{2,1,0:T(8,128)}, u32[]{:S(2)}) copy-start(f32[4,512,1]{2,1,0:T(8,128)} %get-tuple-element.10) | copy-start | bytes 24580
  52.2 6.5 %copy-start.7 = (f32[4,512,128]{2,1,0:T(8,128)S(1)}, f32[4,512,128]{2,1,0:T(8,128)}, u32[]{:S(2)}) copy-start(f32[4,512,128]{2,1,0:T(8,128)} %get-tuple-element.8) | copy-start | bytes 3145732
  53.3 4.0 %collective-permute-start.5 = (f32[4,512,64]{1,2,0:T(8,128)}, f32[4,512,64]{1,2,0:T(8,128)}, u32[]{:S(2)}, u32[]{:S(2)}) collective-permute-start(f32[4,512,64]{1,2,0:T(8,128)} %copy.44), channel_id=1, source_target_pairs={{0,1},{1,0},{2,3},{3,2},{4,5},{5,4},{6,7},{7,6},{8,9},{9,8},{10,11... | collective-permute-start | bytes 1572872 | tf_op jit(solution)/shard_map/ppermute | solution.py:18
  55.3 1.3 collective-permute-start.4
  56.0 1.3 collective-permute-start.6
  63.5 29.0 %all-to-all-start = ((bf16[128,2,2048]{2,1,0:T(2,128)(2,1)}), bf16[128,2,2048]{2,1,0:T(2,128)(2,1)S(1)}, u32[]{:S(2)}, u32[]{:S(2)}) async-start(bf16[128,2,2048]{2,1,0:T(2,128)(2,1)} %reshape.520), calls=%async_computation | async-start | bytes 2097152 | tf_op jit(solution)/shard_map/all_to_all | solution.py:193
  76.5 18.3 %copy-start.9 = (bf16[64,2048]{1,0:T(8,128)(2,1)S(1)}, bf16[64,2048]{1,0:T(8,128)(2,1)}, u32[]{:S(2)}) copy-start(bf16[64,2048]{1,0:T(8,128)(2,1)} %param.18) | copy-start | bytes 786436
  94.7 5.9 %copy-start.12 = (f32[2048]{0:T(1024)S(1)}, f32[2048]{0:T(1024)}, u32[]{:S(2)}) copy-start(f32[2048]{0:T(1024)} %param.20) | copy-start | bytes 24580
  164.2 7.0 %copy-start.15 = (bf16[2,2048,352]{1,2,0:T(8,128)(2,1)S(1)}, bf16[2,2048,352]{1,2,0:T(8,128)(2,1)}, u32[]{:S(2)}) copy-start(bf16[2,2048,352]{1,2,0:T(8,128)(2,1)} %param.23) | copy-start | bytes 8650756
  164.2 59.5 %all-to-all-start.1 = ((bf16[128,8,2048]{2,1,0:T(8,128)(2,1)}), bf16[128,8,2048]{2,1,0:T(8,128)(2,1)}, u32[]{:S(2)}, u32[]{:S(2)}) async-start(bf16[128,8,2048]{2,1,0:T(8,128)(2,1)} %bitcast.131), calls=%async_computation.1 | async-start | bytes 8388608 | tf_op jit(solution)/shard_map/all_to_all | solution.py:230
  223.7 58.6 %all-to-all-start.4 = ((bf16[128,8,2048]{2,1,0:T(8,128)(2,1)}), bf16[128,8,2048]{2,1,0:T(8,128)(2,1)}, u32[]{:S(2)}, u32[]{:S(2)}) async-start(bf16[128,8,2048]{2,1,0:T(8,128)(2,1)} %convert_bitcast_fusion), calls=%async_computation.4 | async-start | bytes 8388608 | tf_op jit(solution)/shard_map/all_to_all | solution.py:237
  244.1 45.5 %copy-start.13 = (f32[64,6]{0,1:T(8,128)S(1)}, f32[64,6]{0,1:T(8,128)}, u32[]{:S(2)}) copy-start(f32[64,6]{0,1:T(8,128)} %param.22) | copy-start | bytes 4612
  282.2 59.5 %all-to-all-start.2 = ((bf16[128,8,2048]{2,1,0:T(8,128)(2,1)}), bf16[128,8,2048]{2,1,0:T(8,128)(2,1)}, u32[]{:S(2)}, u32[]{:S(2)}) async-start(bf16[128,8,2048]{2,1,0:T(8,128)(2,1)} %convert_bitcast_fusion.1), calls=%async_computation.2 | async-start | bytes 8388608 | tf_op jit(solution)/shard_map/all_to_all | solution.py:237
  352.8 6.3 %copy-start.1 = (bf16[192,32,256]{2,1,0:T(8,128)(2,1)S(1)}, bf16[192,32,256]{2,1,0:T(8,128)(2,1)}, u32[]{:S(2)}) copy-start(bf16[192,32,256]{2,1,0:T(8,128)(2,1)} %param.13) | copy-start | bytes 9437188
  (4 other events, 7.2 us)
Sparse Core Ops, SparseCore 0:
  9.6 55.3 all-gather.1

commit v6 on v4

--- a/solution.py
+++ b/solution.py
@@ -223,6 +223,8 @@
     owner_slot = (flat_routes // experts_here) * capacity + rank_in_expert
     parity = flat_routes % experts_here
     routed = jnp.zeros((tok_rows, width), jnp.float32)
+    slot_ids = jnp.arange(tensor_size * capacity, dtype=jnp.int32)
+    flat_gates = route_gates.reshape(-1)
     for k in range(experts_here):
         fanned = jnp.broadcast_to(outgoing_rows[None, :, k], (group_count,) + outgoing_rows[:, k].shape)
         fanned = fanned.reshape((group_count * tensor_size, capacity, width))
@@ -236,12 +238,15 @@
         returned = lax.all_to_all(
             partial_value, ("dp", "tensor"), split_axis=0, concat_axis=0, tiled=True
         )
-        slot_out = jnp.sum(
-            returned.reshape(group_count, tensor_size * capacity, width).astype(jnp.float32), axis=0
-        )
-        weight = jnp.where(parity == k, route_gates.reshape(-1), 0.0)
-        picked = slot_out[owner_slot] * weight[:, None]
-        routed = routed + jnp.sum(picked.reshape(tok_rows, TOP, width), axis=1)
+        hit = (owner_slot[:, None] == slot_ids[None, :]) & (parity == k)[:, None]
+        coeff = jnp.where(hit, flat_gates[:, None], 0.0).reshape(tok_rows, TOP, -1).sum(axis=1)
+        coeff = jnp.tile(coeff, (1, group_count))
+        routed = routed + jnp.dot(
+            coeff,
+            returned.reshape(-1, width).astype(jnp.float32),
+            precision=lax.Precision.HIGHEST,
+            preferred_element_type=jnp.float32,
+        )
     return hidden + routed
 
 

time: 362 us -> 351 us (0.970)
  local copies, waits for them, and re-layouts: 40.7 us -> 24.2 us
  other arithmetic: 24.7 us -> 12.3 us
  matrix products: 33.9 us -> 44.8 us
  waiting for transfers between devices: 136 us -> 144 us
    gather x4 -> x0, local copies, waits for them, and re-layouts: 15.7 us -> none  [shards(): picked = slot_out[owner_slot] * weight[:, None]]
    reduce_sum x4 -> x1, other arithmetic: 11.8 us -> 0.27 us  [shards(): jnp.where(hit, flat_gates[:, None], 0.0).reshape(tok_rows, TOP, -1)]
    dot_general x0 -> x2, matrix products: none -> 11 us  [shards(): jnp.dot(coeff, returned.reshape(-1, width).astype(jnp.float32), precision...]
    all_to_all x2, waiting for transfers between devices: 78.9 us -> 84.4 us  [shards(): lax.all_to_all(partial_value, ('dp', 'tensor'), split_axis=0, concat_axis...]
  transfers between devices with their start and end apart: 15 -> 15, of which waited for: 9 -> 9; matrix products, arithmetic and copies ran while one was open for 19% -> 18% of each run, Pallas kernels for 4% -> 4%
where the time goes in v6:
time: 351 us; the launch traced here: 350 us
  waiting for transfers between devices  144 us (41%)
  blocking collectives  57.6 us (16%)
  matrix products  44.8 us (13%)
  starting transfers between devices  39.8 us (11%)
  local copies, waits for them, and re-layouts  24.2 us (7%)
  between operations  13.9 us (4%)
  Pallas kernels  13.7 us (4%)
  other arithmetic  12.3 us (4%)
    all_to_all x2, waiting for transfers between devices, shards(): lax.all_to_all(partial_value, ('dp', 'tensor'), split_axis=0, concat_axis...  84.4 us
    all_to_all x1, blocking collectives, shards(): lax.all_to_all(fanned, ('dp', 'tensor'), split_axis=0, concat_axis=0, til...  57.6 us
    all_to_all x1, waiting for transfers between devices, shards(): lax.all_to_all(fanned, ('dp', 'tensor'), split_axis=0, concat_axis=0, til...  38.1 us
    dot_general x2, matrix products, shards(): jnp.dot(active, expert_down[k], preferred_element_type=jnp.float32)  18.8 us
    pallas_call x1, Pallas kernels, attention_kernel(): pl.pallas_call(body, grid_spec=grid_spec, out_shape=[jax.ShapeDtypeStruct...  13.7 us
    all_to_all x2, starting transfers between devices, shards(): lax.all_to_all(partial_value, ('dp', 'tensor'), split_axis=0, concat_axis...  13 us
    dot_general x2, matrix products, shards(): jnp.dot(coeff, returned.reshape(-1, width).astype(jnp.float32), precision...  11 us
    dot_general x2, matrix products, shards(): jnp.dot(flat_rows, expert_gate[k], preferred_element_type=jnp.float32)  9.97 us
  transfers between devices with their start and end apart: 15, of which 9 were waited for; matrix products, arithmetic and copies ran while one was open for 18% of the time, Pallas kernels for 4%

profile of v6, /device:TPU:0, one launch (start us, length us, event | category | flops | bytes accessed | tf_op | source)
XLA Modules:
  0.0 349.9 jit_solution(4692185896954902720)
XLA Ops:
  9.6 2.7 gather_fusion.1
  16.0 2.9 collective-permute-start.1
  24.8 3.3 collective-permute-done.1
  31.0 2.8 gather_fusion.3
  35.7 13.7 %shard_map.127 = (f32[4,512,128]{2,1,0:T(8,128)}, f32[4,512,1]{2,1,0:T(8,128)}, f32[4,512,1]{2,1,0:T(8,128)}) custom-call(s32[6]{0:T(128)} %pad_add_fusion.scal_ref, bf16[4,512,128]{2,1,0:T(8,128)(2,1)} %pad_maximum_fusion.1.q_ref, bf16[4,2048,256]{2,1,0:T(8,128)(2,1)} %bitcast.139, bf16[4,256,384]{2,1,0:T(8,128)(2,1)} %copy-done.3), custom_call_target="tpu_custom_call" | custom-call | tf_op jit(solution)/shard_map/pallas_call | solution.py:76
  63.0 4.3 %collective-permute-done.9 = bf16[512,64]{1,0:T(8,128)(2,1)S(1)} collective-permute-done((bf16[512,64]{1,0:T(8,128)(2,1)S(1)}, bf16[512,64]{1,0:T(8,128)(2,1)S(1)}, u32[]{:S(2)}, u32[]{:S(2)}) %collective-permute-start.9) | collective-permute-done | bytes 65568 | tf_op jit(solution)/shard_map/ppermute | solution.py:190
  72.8 8.6 %all-to-all-start = ((bf16[32,2,2048]{2,1,0:T(2,128)(2,1)}), bf16[32,2,2048]{2,1,0:T(2,128)(2,1)S(1)}, u32[]{:S(2)}, u32[]{:S(2)}) async-start(bf16[32,2,2048]{2,1,0:T(2,128)(2,1)} %reshape.406), calls=%async_computation | async-start | bytes 524288 | tf_op jit(solution)/shard_map/all_to_all | solution.py:195
  81.5 8.7 %all-to-all-done = bf16[32,2,2048]{2,1,0:T(2,128)(2,1)S(1)} async-done(((bf16[32,2,2048]{2,1,0:T(2,128)(2,1)}), bf16[32,2,2048]{2,1,0:T(2,128)(2,1)S(1)}, u32[]{:S(2)}, u32[]{:S(2)}) %all-to-all-start) | async-done | bytes 262176 | tf_op jit(solution)/shard_map/all_to_all | solution.py:195
  91.4 5.1 %multiply_reduce_fusion = (f32[64]{0:T(128)S(1)}, f32[64,2048]{1,0:T(8,128)S(1)}) fusion(bf16[64,2048]{1,0:T(8,128)(2,1)S(1)} %reshape.331, bf16[2048,2048]{1,0:T(8,128)(2,1)} %all-gather.2.cloned.1.call-done, bf16[64,2048]{1,0:T(8,128)(2,1)S(1)} %copy-done.7), kind=kOutput, calls=%fused_computation.53 | convolution fusion | flops 537395136 | bytes 9437440 | tf_op jit(solution)/shard_map/dot_general | solution.py:198
  96.6 2.5 gather_fusion.5
  100.0 57.6 %all_to_all.25 = bf16[128,8,2048]{2,1,0:T(8,128)(2,1)} all-to-all(bf16[128,8,2048]{2,1,0:T(8,128)(2,1)S(1)} %bitcast.141), channel_id=1, replica_groups=mesh['dp'=4,'tensor'=32] {'dp','tensor'}, dimensions={0} | all-to-all | bytes 8388608 | tf_op jit(solution)/shard_map/all_to_all | solution.py:231
  157.6 2.5 broadcast_in_dim.120
  160.1 7.0 %all-to-all-start.1 = ((bf16[128,8,2048]{2,1,0:T(8,128)(2,1)}), bf16[128,8,2048]{2,1,0:T(8,128)(2,1)}, u32[]{:S(2)}, u32[]{:S(2)}) async-start(bf16[128,8,2048]{2,1,0:T(8,128)(2,1)} %bitcast.140), calls=%async_computation.1 | async-start | bytes 8388608 | tf_op jit(solution)/shard_map/all_to_all | solution.py:231
  167.1 5.0 %fusion.4 = f32[1024,352]{0,1:T(8,128)} fusion(bf16[128,8,2048]{2,1,0:T(8,128)(2,1)} %all_to_all.25, bf16[2,2048,352]{1,2,0:T(8,128)(2,1)S(1)} %copy-done.14), kind=kOutput, calls=%fused_computation.11 | convolution fusion | flops 1476395008 | bytes 7077888 | tf_op jit(solution)/shard_map/dot_general | solution.py:233
  172.0 9.4 %convert_bitcast_fusion = bf16[128,8,2048]{2,1,0:T(8,128)(2,1)} fusion(bf16[2,352,2048]{2,1,0:T(8,128)(2,1)} %param.25, bf16[2,2048,352]{1,2,0:T(8,128)(2,1)} %param.24, bf16[128,8,2048]{2,1,0:T(8,128)(2,1)} %all_to_all.25, f32[1024,352]{0,1:T(8,128)} %fusion.4), kind=kOutput, calls=%fused_computation.19 | convolution fusion | flops 2957049856 | bytes 12713984 | tf_op jit(solution)/shard_map/dot_general | solution.py:236
  181.5 38.1 %all-to-all-done.1 = bf16[128,8,2048]{2,1,0:T(8,128)(2,1)} async-done(((bf16[128,8,2048]{2,1,0:T(8,128)(2,1)}), bf16[128,8,2048]{2,1,0:T(8,128)(2,1)}, u32[]{:S(2)}, u32[]{:S(2)}) %all-to-all-start.1) | async-done | bytes 4194336 | tf_op jit(solution)/shard_map/all_to_all | solution.py:231
  219.6 6.0 %all-to-all-start.4 = ((bf16[128,8,2048]{2,1,0:T(8,128)(2,1)}), bf16[128,8,2048]{2,1,0:T(8,128)(2,1)}, u32[]{:S(2)}, u32[]{:S(2)}) async-start(bf16[128,8,2048]{2,1,0:T(8,128)(2,1)} %convert_bitcast_fusion), calls=%async_computation.4 | async-start | bytes 8388608 | tf_op jit(solution)/shard_map/all_to_all | solution.py:238
  225.6 5.0 %fusion.10 = f32[1024,352]{0,1:T(8,128)} fusion(bf16[128,8,2048]{2,1,0:T(8,128)(2,1)} %all-to-all-done.1, bf16[2,2048,352]{1,2,0:T(8,128)(2,1)S(1)} %copy-done.14), kind=kOutput, calls=%fused_computation.17 | convolution fusion | flops 1476395008 | bytes 7077888 | tf_op jit(solution)/shard_map/dot_general | solution.py:233
  230.6 9.4 %convert_bitcast_fusion.1 = bf16[128,8,2048]{2,1,0:T(8,128)(2,1)} fusion(bf16[2,352,2048]{2,1,0:T(8,128)(2,1)} %param.25, bf16[2,2048,352]{1,2,0:T(8,128)(2,1)} %param.24, bf16[128,8,2048]{2,1,0:T(8,128)(2,1)} %all-to-all-done.1, f32[1024,352]{0,1:T(8,128)} %fusion.10), kind=kOutput, calls=%fused_computation.20 | convolution fusion | flops 2957049856 | bytes 12713984 | tf_op jit(solution)/shard_map/dot_general | solution.py:236
  240.0 37.9 %all-to-all-done.4 = bf16[128,8,2048]{2,1,0:T(8,128)(2,1)} async-done(((bf16[128,8,2048]{2,1,0:T(8,128)(2,1)}), bf16[128,8,2048]{2,1,0:T(8,128)(2,1)}, u32[]{:S(2)}, u32[]{:S(2)}) %all-to-all-start.4) | async-done | bytes 4194336 | tf_op jit(solution)/shard_map/all_to_all | solution.py:238
  277.9 7.0 %all-to-all-start.2 = ((bf16[128,8,2048]{2,1,0:T(8,128)(2,1)}), bf16[128,8,2048]{2,1,0:T(8,128)(2,1)}, u32[]{:S(2)}, u32[]{:S(2)}) async-start(bf16[128,8,2048]{2,1,0:T(8,128)(2,1)} %convert_bitcast_fusion.1), calls=%async_computation.2 | async-start | bytes 8388608 | tf_op jit(solution)/shard_map/all_to_all | solution.py:238
  285.6 5.3 %fusion = f32[64,2048]{1,0:T(8,128)} fusion(f32[64,1024]{1,0:T(8,128)S(1)} %bitcast.146, bf16[128,8,2048]{2,1,0:T(8,128)(2,1)} %all-to-all-done.4), kind=kOutput, calls=%fused_computation.7 | convolution fusion | flops 1610612736 | bytes 4980736 | tf_op jit(solution)/shard_map/dot_general | solution.py:244
  290.9 46.4 %all-to-all-done.2 = bf16[128,8,2048]{2,1,0:T(8,128)(2,1)} async-done(((bf16[128,8,2048]{2,1,0:T(8,128)(2,1)}), bf16[128,8,2048]{2,1,0:T(8,128)(2,1)}, u32[]{:S(2)}, u32[]{:S(2)}) %all-to-all-start.2) | async-done | bytes 4194336 | tf_op jit(solution)/shard_map/all_to_all | solution.py:238
  337.4 5.7 %fusion.15 = f32[64,2048]{1,0:T(8,128)} fusion(f32[64,2048]{1,0:T(8,128)} %copy-done.4, f32[64,2048]{1,0:T(8,128)} %fusion, f32[64,1024]{1,0:T(8,128)S(1)} %bitcast.145, bf16[128,8,2048]{2,1,0:T(8,128)(2,1)} %all-to-all-done.2), kind=kOutput, calls=%fused_computation.22 | convolution fusion | flops 1610874880 | bytes 6029312 | tf_op jit(solution)/shard_map/dot_general | solution.py:244
  (118 shorter events, 39.3 us)
Async XLA Ops:
  6.5 24.5 %copy-start = (bf16[192,32,256]{2,1,0:T(8,128)(2,1)S(1)}, bf16[192,32,256]{2,1,0:T(8,128)(2,1)}, u32[]{:S(2)}) copy-start(bf16[192,32,256]{2,1,0:T(8,128)(2,1)} %param.13) | copy-start | bytes 9437188
  6.5 14.1 %copy-start.13 = (s32[16]{0:T(128)S(1)}, s32[16]{0:T(128)}, u32[]{:S(2)}) copy-start(s32[16]{0:T(128)} %param.15) | copy-start | bytes 196
  6.5 13.7 %copy-start.9 = (s32[64,6]{0,1:T(8,128)S(1)}, s32[64,6]{0,1:T(8,128)}, u32[]{:S(2)}) copy-start(s32[64,6]{0,1:T(8,128)} %param.21) | copy-start | bytes 4612
  6.5 14.9 %copy-start.8 = (s32[4,64]{1,0:T(4,128)S(1)}, s32[4,64]{1,0:T(4,128)}, u32[]{:S(2)}) copy-start(s32[4,64]{1,0:T(4,128)} %param.14) | copy-start | bytes 3076
  6.5 17.3 %copy-start.2 = (s32[16]{0:T(128)S(1)}, s32[16]{0:T(128)}, u32[]{:S(2)}) copy-start(s32[16]{0:T(128)} %param.16) | copy-start | bytes 196
  6.5 84.8 %all-gather.2.cloned.1.call-start = ((), (), s32[]{:S(2)}) async-start(), calls=%async_computation.5 | async-start | bytes 8650752 | tf_op jit(solution)/shard_map/all_gather | solution.py:197
  14.3 10.5 %collective-permute-start.2 = (bf16[256,384]{1,0:T(8,128)(2,1)}, bf16[256,384]{1,0:T(8,128)(2,1)}, u32[]{:S(2)}, u32[]{:S(2)}) collective-permute-start(bf16[256,384]{1,0:T(8,128)(2,1)} %get-tuple-element.25), channel_id=1, source_target_pairs={{0,32},{32,64},{64,96},{96,0},{1,33},{33,65},{65,97},{97,1},{2,34}... | collective-permute-start | bytes 589832 | tf_op jit(solution)/shard_map/ppermute | solution.py:152
  16.0 12.0 %collective-permute-start.1 = (bf16[256,384]{1,0:T(8,128)(2,1)}, bf16[256,384]{1,0:T(8,128)(2,1)}, u32[]{:S(2)}, u32[]{:S(2)}) collective-permute-start(bf16[256,384]{1,0:T(8,128)(2,1)} %get-tuple-element.23), channel_id=1, source_target_pairs={{0,64},{32,96},{64,0},{96,32},{1,65},{33,97},{65,1},{97,33},{2,66}... | collective-permute-start | bytes 589832 | tf_op jit(solution)/shard_map/ppermute | solution.py:152
  18.9 9.1 %collective-permute-start = (bf16[256,384]{1,0:T(8,128)(2,1)}, bf16[256,384]{1,0:T(8,128)(2,1)}, u32[]{:S(2)}, u32[]{:S(2)}) collective-permute-start(bf16[256,384]{1,0:T(8,128)(2,1)} %get-tuple-element.24), channel_id=1, source_target_pairs={{0,96},{32,0},{64,32},{96,64},{1,97},{33,1},{65,33},{97,65},{2,98}... | collective-permute-start | bytes 589832 | tf_op jit(solution)/shard_map/ppermute | solution.py:152
  30.3 3.6 %collective-permute-start.3 = (bf16[4,256,128]{2,1,0:T(8,128)(2,1)S(1)}, bf16[4,256,128]{2,1,0:T(8,128)(2,1)}, u32[]{:S(2)}, u32[]{:S(2)}) collective-permute-start(bf16[4,256,128]{2,1,0:T(8,128)(2,1)S(1)} %slice.92), channel_id=1, source_target_pairs={{0,1},{1,0},{2,3},{3,2},{4,5},{5,4},{6,7},{7,6},{8,9},{9,8},{10,11... | collective-permute-start | bytes 786440 | tf_op jit(solution)/shard_map/ppermute | solution.py:18
  52.2 4.2 %collective-permute-start.5 = (f32[4,512,64]{1,2,0:T(8,128)}, f32[4,512,64]{1,2,0:T(8,128)}, u32[]{:S(2)}, u32[]{:S(2)}) collective-permute-start(f32[4,512,64]{1,2,0:T(8,128)} %copy.51), channel_id=1, source_target_pairs={{0,1},{1,0},{2,3},{3,2},{4,5},{5,4},{6,7},{7,6},{8,9},{9,8},{10,11... | collective-permute-start | bytes 1572872 | tf_op jit(solution)/shard_map/ppermute | solution.py:18
  54.6 1.3 collective-permute-start.6
  55.0 8.0 %copy-start.12 = (s32[4]{0:T(128)S(1)}, s32[4]{0:T(128)}, u32[]{:S(2)}) copy-start(s32[4]{0:T(128)} %get-tuple-element.13) | copy-start | bytes 52
  55.0 1.4 collective-permute-start.4
  59.2 8.1 %collective-permute-start.9 = (bf16[512,64]{1,0:T(8,128)(2,1)S(1)}, bf16[512,64]{1,0:T(8,128)(2,1)S(1)}, u32[]{:S(2)}, u32[]{:S(2)}) collective-permute-start(bf16[512,64]{1,0:T(8,128)(2,1)S(1)} %get-tuple-element.27), channel_id=1, source_target_pairs={{0,96},{32,0},{64,32},{96,64},{1,97},{33,1},{65,33},{97,65},{2,98}... | collective-permute-start | bytes 196616 | tf_op jit(solution)/shard_map/ppermute | solution.py:190
  61.2 7.9 %collective-permute-start.8 = (bf16[512,64]{1,0:T(8,128)(2,1)S(1)}, bf16[512,64]{1,0:T(8,128)(2,1)S(1)}, u32[]{:S(2)}, u32[]{:S(2)}) collective-permute-start(bf16[512,64]{1,0:T(8,128)(2,1)S(1)} %get-tuple-element.28), channel_id=1, source_target_pairs={{0,64},{32,96},{64,0},{96,32},{1,65},{33,97},{65,1},{97,33},{2,66}... | collective-permute-start | bytes 196616 | tf_op jit(solution)/shard_map/ppermute | solution.py:190
  62.3 8.7 %collective-permute-start.7 = (bf16[512,64]{1,0:T(8,128)(2,1)S(1)}, bf16[512,64]{1,0:T(8,128)(2,1)S(1)}, u32[]{:S(2)}, u32[]{:S(2)}) collective-permute-start(bf16[512,64]{1,0:T(8,128)(2,1)S(1)} %get-tuple-element.29), channel_id=1, source_target_pairs={{0,32},{32,64},{64,96},{96,0},{1,33},{33,65},{65,97},{97,1},{2,34}... | collective-permute-start | bytes 196616 | tf_op jit(solution)/shard_map/ppermute | solution.py:190
  70.9 20.4 %copy-start.7 = (bf16[64,2048]{1,0:T(8,128)(2,1)S(1)}, bf16[64,2048]{1,0:T(8,128)(2,1)}, u32[]{:S(2)}) copy-start(bf16[64,2048]{1,0:T(8,128)(2,1)} %param.18) | copy-start | bytes 786436
  72.8 17.3 %all-to-all-start = ((bf16[32,2,2048]{2,1,0:T(2,128)(2,1)}), bf16[32,2,2048]{2,1,0:T(2,128)(2,1)S(1)}, u32[]{:S(2)}, u32[]{:S(2)}) async-start(bf16[32,2,2048]{2,1,0:T(2,128)(2,1)} %reshape.406), calls=%async_computation | async-start | bytes 524288 | tf_op jit(solution)/shard_map/all_to_all | solution.py:195
  160.1 7.0 %copy-start.14 = (bf16[2,2048,352]{1,2,0:T(8,128)(2,1)S(1)}, bf16[2,2048,352]{1,2,0:T(8,128)(2,1)}, u32[]{:S(2)}) copy-start(bf16[2,2048,352]{1,2,0:T(8,128)(2,1)} %param.23) | copy-start | bytes 8650756
  160.1 59.5 %all-to-all-start.1 = ((bf16[128,8,2048]{2,1,0:T(8,128)(2,1)}), bf16[128,8,2048]{2,1,0:T(8,128)(2,1)}, u32[]{:S(2)}, u32[]{:S(2)}) async-start(bf16[128,8,2048]{2,1,0:T(8,128)(2,1)} %bitcast.140), calls=%async_computation.1 | async-start | bytes 8388608 | tf_op jit(solution)/shard_map/all_to_all | solution.py:231
  219.6 58.3 %all-to-all-start.4 = ((bf16[128,8,2048]{2,1,0:T(8,128)(2,1)}), bf16[128,8,2048]{2,1,0:T(8,128)(2,1)}, u32[]{:S(2)}, u32[]{:S(2)}) async-start(bf16[128,8,2048]{2,1,0:T(8,128)(2,1)} %convert_bitcast_fusion), calls=%async_computation.4 | async-start | bytes 8388608 | tf_op jit(solution)/shard_map/all_to_all | solution.py:238
  240.0 45.2 %copy-start.11 = (f32[64,6]{0,1:T(8,128)S(1)}, f32[64,6]{0,1:T(8,128)}, u32[]{:S(2)}) copy-start(f32[64,6]{0,1:T(8,128)} %param.22) | copy-start | bytes 4612
  277.9 59.5 %all-to-all-start.2 = ((bf16[128,8,2048]{2,1,0:T(8,128)(2,1)}), bf16[128,8,2048]{2,1,0:T(8,128)(2,1)}, u32[]{:S(2)}, u32[]{:S(2)}) async-start(bf16[128,8,2048]{2,1,0:T(8,128)(2,1)} %convert_bitcast_fusion.1), calls=%async_computation.2 | async-start | bytes 8388608 | tf_op jit(solution)/shard_map/all_to_all | solution.py:238
  (6 other events, 26.4 us)
Sparse Core Ops, SparseCore 0:
  9.6 55.4 all-gather.1

commit v7 on v6

--- a/solution.py
+++ b/solution.py
@@ -18,7 +18,7 @@
     return lax.ppermute(array, axis, [(i, i ^ 1 << stride) for i in range(lax.axis_size(axis))])
 
 
-def attn_body(scal_ref, q_ref, c_ref, f_ref, w_ref, m_ref, d_ref, *, block_q, page_rows, head):
+def attn_body(scal_ref, q_ref, c_ref, f_ref, lo_ref, hi_ref, m_ref, d_ref, *, block_q, page_rows, head):
     item = pl.program_id(0)
     qb = pl.program_id(1)
     length = scal_ref[item]
@@ -43,9 +43,11 @@
     den = jnp.sum(cw, axis=1, keepdims=True) + jnp.sum(sw, axis=1, keepdims=True)
     acc = jnp.dot(cw.astype(jnp.bfloat16), cached[:, head:], preferred_element_type=jnp.float32)
     acc = acc + jnp.dot(sw.astype(jnp.bfloat16), fresh[:, 2 * head:], preferred_element_type=jnp.float32)
-    w_ref[...] = acc
-    m_ref[...] = mx
-    d_ref[...] = den
+    half = head // 2
+    lo_ref[...] = acc[:, :half]
+    hi_ref[...] = acc[:, half:]
+    m_ref[...] = jnp.transpose(jnp.broadcast_to(mx, (block_q, 128)))[0:1, :]
+    d_ref[...] = jnp.transpose(jnp.broadcast_to(den, (block_q, 128)))[0:1, :]
 
 
 def attention_kernel(queries, cached, fresh, lengths, cache_offset, span_offset, interpret=False):
@@ -68,22 +70,24 @@
             pl.BlockSpec((None, fresh_rows, 3 * head), lambda i, b, s: (i, 0, 0)),
         ],
         out_specs=[
-            pl.BlockSpec((None, block_q, head), lambda i, b, s: (i, b, 0)),
-            pl.BlockSpec((None, block_q, 1), lambda i, b, s: (i, b, 0)),
-            pl.BlockSpec((None, block_q, 1), lambda i, b, s: (i, b, 0)),
+            pl.BlockSpec((None, block_q, head // 2), lambda i, b, s: (i, b, 0)),
+            pl.BlockSpec((None, block_q, head // 2), lambda i, b, s: (i, b, 0)),
+            pl.BlockSpec((None, 1, block_q), lambda i, b, s: (i, 0, b)),
+            pl.BlockSpec((None, 1, block_q), lambda i, b, s: (i, 0, b)),
         ],
     )
-    weighted, mx, den = pl.pallas_call(
+    lower, upper, mx, den = pl.pallas_call(
         body,
         grid_spec=grid_spec,
         out_shape=[
-            jax.ShapeDtypeStruct((items, span, head), jnp.float32),
-            jax.ShapeDtypeStruct((items, span, 1), jnp.float32),
-            jax.ShapeDtypeStruct((items, span, 1), jnp.float32),
+            jax.ShapeDtypeStruct((items, span, head // 2), jnp.float32),
+            jax.ShapeDtypeStruct((items, span, head // 2), jnp.float32),
+            jax.ShapeDtypeStruct((items, 1, span), jnp.float32),
+            jax.ShapeDtypeStruct((items, 1, span), jnp.float32),
         ],
         interpret=interpret,
     )(scal, queries, cached, fresh)
-    return weighted, mx[..., 0], den[..., 0]
+    return lower, upper, mx[:, 0], den[:, 0]
 
 
 def run_experts(slot_rows, expert_gate, expert_up, expert_down):
@@ -173,10 +177,10 @@
         side_index * rows_per_head,
         side_index * fresh_per,
     )
-    weighted, maximum, denominator = head_results
+    lower, upper, maximum, denominator = head_results
     half_dim = HD // 2
-    given_part = lax.dynamic_slice_in_dim(weighted, (1 - side_index) * half_dim, half_dim, 2)
-    kept_part = lax.dynamic_slice_in_dim(weighted, side_index * half_dim, half_dim, 2)
+    given_part = jnp.where(side_index == 0, upper, lower)
+    kept_part = jnp.where(side_index == 0, lower, upper)
     received_part, other_max, other_den = swapped((given_part, maximum, denominator), "tensor", 0)
     joint_max = jnp.maximum(maximum, other_max)
     own_scale = jnp.exp(maximum - joint_max)

time: 351 us -> 349 us (level)
  no operation moved by 1% of the time
where the time goes in v7:
time: 349 us; the launch traced here: 348 us
  waiting for transfers between devices  144 us (41%)
  blocking collectives  57.6 us (17%)
  matrix products  44.8 us (13%)
  starting transfers between devices  39.5 us (11%)
  local copies, waits for them, and re-layouts  22.6 us (6%)
  Pallas kernels  14 us (4%)
  between operations  13.9 us (4%)
  other arithmetic  11.5 us (3%)
    all_to_all x2, waiting for transfers between devices, shards(): lax.all_to_all(partial_value, ('dp', 'tensor'), split_axis=0, concat_axis...  84.4 us
    all_to_all x1, blocking collectives, shards(): lax.all_to_all(fanned, ('dp', 'tensor'), split_axis=0, concat_axis=0, til...  57.6 us
    all_to_all x1, waiting for transfers between devices, shards(): lax.all_to_all(fanned, ('dp', 'tensor'), split_axis=0, concat_axis=0, til...  38.1 us
    dot_general x2, matrix products, shards(): jnp.dot(active, expert_down[k], preferred_element_type=jnp.float32)  18.7 us
    pallas_call x1, Pallas kernels, attention_kernel(): pl.pallas_call(body, grid_spec=grid_spec, out_shape=[jax.ShapeDtypeStruct...  14 us
    all_to_all x2, starting transfers between devices, shards(): lax.all_to_all(partial_value, ('dp', 'tensor'), split_axis=0, concat_axis...  13 us
    dot_general x2, matrix products, shards(): jnp.dot(coeff, returned.reshape(-1, width).astype(jnp.float32), precision...  11 us
    dot_general x2, matrix products, shards(): jnp.dot(flat_rows, expert_gate[k], preferred_element_type=jnp.float32)  9.96 us
  transfers between devices with their start and end apart: 15, of which 9 were waited for; matrix products, arithmetic and copies ran while one was open for 18% of the time, Pallas kernels for 4%

profile of v7, /device:TPU:0, one launch (start us, length us, event | category | flops | bytes accessed | tf_op | source)
XLA Modules:
  0.0 348.1 jit_solution(2442570625782351069)
XLA Ops:
  9.5 2.8 gather_fusion.1
  15.9 2.9 collective-permute-start.1
  24.8 3.2 collective-permute-done.1
  30.9 2.8 gather_fusion.3
  35.6 14.0 %shard_map.127 = (f32[4,512,64]{2,1,0:T(8,128)}, f32[4,512,64]{2,1,0:T(8,128)}, f32[4,1,512]{2,1,0:T(1,128)}, f32[4,1,512]{2,1,0:T(1,128)}) custom-call(s32[6]{0:T(128)} %pad_add_fusion.scal_ref, bf16[4,512,128]{2,1,0:T(8,128)(2,1)} %pad_maximum_fusion.1.q_ref, bf16[4,2048,256]{2,1,0:T(8,128)(2,1)} %bitcast.153, bf16[4,256,384]{2,1,0:T(8,128)(2,1)} %copy-done.3), custom_call_target="tpu_custom_call" | custom-call | tf_op jit(solution)/shard_map/pallas_call | solution.py:79
  61.6 4.2 %collective-permute-done.9 = bf16[512,64]{1,0:T(8,128)(2,1)S(1)} collective-permute-done((bf16[512,64]{1,0:T(8,128)(2,1)S(1)}, bf16[512,64]{1,0:T(8,128)(2,1)S(1)}, u32[]{:S(2)}, u32[]{:S(2)}) %collective-permute-start.9) | collective-permute-done | bytes 65568 | tf_op jit(solution)/shard_map/ppermute | solution.py:194
  71.3 8.4 %all-to-all-start = ((bf16[32,2,2048]{2,1,0:T(2,128)(2,1)}), bf16[32,2,2048]{2,1,0:T(2,128)(2,1)S(1)}, u32[]{:S(2)}, u32[]{:S(2)}) async-start(bf16[32,2,2048]{2,1,0:T(2,128)(2,1)} %reshape.404), calls=%async_computation | async-start | bytes 524288 | tf_op jit(solution)/shard_map/all_to_all | solution.py:199
  79.7 8.7 %all-to-all-done = bf16[32,2,2048]{2,1,0:T(2,128)(2,1)S(1)} async-done(((bf16[32,2,2048]{2,1,0:T(2,128)(2,1)}), bf16[32,2,2048]{2,1,0:T(2,128)(2,1)S(1)}, u32[]{:S(2)}, u32[]{:S(2)}) %all-to-all-start) | async-done | bytes 262176 | tf_op jit(solution)/shard_map/all_to_all | solution.py:199
  89.6 5.1 %multiply_reduce_fusion = (f32[64]{0:T(128)S(1)}, f32[64,2048]{1,0:T(8,128)S(1)}) fusion(bf16[64,2048]{1,0:T(8,128)(2,1)S(1)} %reshape.331, bf16[2048,2048]{1,0:T(8,128)(2,1)} %all-gather.2.cloned.1.call-done, bf16[64,2048]{1,0:T(8,128)(2,1)S(1)} %copy-done.7), kind=kOutput, calls=%fused_computation.53 | convolution fusion | flops 537395136 | bytes 9437440 | tf_op jit(solution)/shard_map/dot_general | solution.py:202
  94.8 2.5 gather_fusion.5
  98.2 57.6 %all_to_all.25 = bf16[128,8,2048]{2,1,0:T(8,128)(2,1)} all-to-all(bf16[128,8,2048]{2,1,0:T(8,128)(2,1)S(1)} %bitcast.155), channel_id=1, replica_groups=mesh['dp'=4,'tensor'=32] {'dp','tensor'}, dimensions={0} | all-to-all | bytes 8388608 | tf_op jit(solution)/shard_map/all_to_all | solution.py:235
  155.8 2.5 broadcast_in_dim.120
  158.3 6.9 %all-to-all-start.1 = ((bf16[128,8,2048]{2,1,0:T(8,128)(2,1)}), bf16[128,8,2048]{2,1,0:T(8,128)(2,1)}, u32[]{:S(2)}, u32[]{:S(2)}) async-start(bf16[128,8,2048]{2,1,0:T(8,128)(2,1)} %bitcast.154), calls=%async_computation.1 | async-start | bytes 8388608 | tf_op jit(solution)/shard_map/all_to_all | solution.py:235
  165.3 5.0 %fusion.4 = f32[1024,352]{0,1:T(8,128)} fusion(bf16[128,8,2048]{2,1,0:T(8,128)(2,1)} %all_to_all.25, bf16[2,2048,352]{1,2,0:T(8,128)(2,1)S(1)} %copy-done.16), kind=kOutput, calls=%fused_computation.11 | convolution fusion | flops 1476395008 | bytes 7077888 | tf_op jit(solution)/shard_map/dot_general | solution.py:237
  170.2 9.4 %convert_bitcast_fusion = bf16[128,8,2048]{2,1,0:T(8,128)(2,1)} fusion(bf16[2,352,2048]{2,1,0:T(8,128)(2,1)} %param.25, bf16[2,2048,352]{1,2,0:T(8,128)(2,1)} %param.24, bf16[128,8,2048]{2,1,0:T(8,128)(2,1)} %all_to_all.25, f32[1024,352]{0,1:T(8,128)} %fusion.4), kind=kOutput, calls=%fused_computation.19 | convolution fusion | flops 2957049856 | bytes 12713984 | tf_op jit(solution)/shard_map/dot_general | solution.py:240
  179.6 38.1 %all-to-all-done.1 = bf16[128,8,2048]{2,1,0:T(8,128)(2,1)} async-done(((bf16[128,8,2048]{2,1,0:T(8,128)(2,1)}), bf16[128,8,2048]{2,1,0:T(8,128)(2,1)}, u32[]{:S(2)}, u32[]{:S(2)}) %all-to-all-start.1) | async-done | bytes 4194336 | tf_op jit(solution)/shard_map/all_to_all | solution.py:235
  217.8 6.0 %all-to-all-start.4 = ((bf16[128,8,2048]{2,1,0:T(8,128)(2,1)}), bf16[128,8,2048]{2,1,0:T(8,128)(2,1)}, u32[]{:S(2)}, u32[]{:S(2)}) async-start(bf16[128,8,2048]{2,1,0:T(8,128)(2,1)} %convert_bitcast_fusion), calls=%async_computation.4 | async-start | bytes 8388608 | tf_op jit(solution)/shard_map/all_to_all | solution.py:242
  223.8 5.0 %fusion.10 = f32[1024,352]{0,1:T(8,128)} fusion(bf16[128,8,2048]{2,1,0:T(8,128)(2,1)} %all-to-all-done.1, bf16[2,2048,352]{1,2,0:T(8,128)(2,1)S(1)} %copy-done.16), kind=kOutput, calls=%fused_computation.17 | convolution fusion | flops 1476395008 | bytes 7077888 | tf_op jit(solution)/shard_map/dot_general | solution.py:237
  228.8 9.4 %convert_bitcast_fusion.1 = bf16[128,8,2048]{2,1,0:T(8,128)(2,1)} fusion(bf16[2,352,2048]{2,1,0:T(8,128)(2,1)} %param.25, bf16[2,2048,352]{1,2,0:T(8,128)(2,1)} %param.24, bf16[128,8,2048]{2,1,0:T(8,128)(2,1)} %all-to-all-done.1, f32[1024,352]{0,1:T(8,128)} %fusion.10), kind=kOutput, calls=%fused_computation.20 | convolution fusion | flops 2957049856 | bytes 12713984 | tf_op jit(solution)/shard_map/dot_general | solution.py:240
  238.1 37.9 %all-to-all-done.4 = bf16[128,8,2048]{2,1,0:T(8,128)(2,1)} async-done(((bf16[128,8,2048]{2,1,0:T(8,128)(2,1)}), bf16[128,8,2048]{2,1,0:T(8,128)(2,1)}, u32[]{:S(2)}, u32[]{:S(2)}) %all-to-all-start.4) | async-done | bytes 4194336 | tf_op jit(solution)/shard_map/all_to_all | solution.py:242
  276.1 7.0 %all-to-all-start.2 = ((bf16[128,8,2048]{2,1,0:T(8,128)(2,1)}), bf16[128,8,2048]{2,1,0:T(8,128)(2,1)}, u32[]{:S(2)}, u32[]{:S(2)}) async-start(bf16[128,8,2048]{2,1,0:T(8,128)(2,1)} %convert_bitcast_fusion.1), calls=%async_computation.2 | async-start | bytes 8388608 | tf_op jit(solution)/shard_map/all_to_all | solution.py:242
  283.8 5.3 %fusion = f32[64,2048]{1,0:T(8,128)} fusion(f32[64,1024]{1,0:T(8,128)S(1)} %bitcast.160, bf16[128,8,2048]{2,1,0:T(8,128)(2,1)} %all-to-all-done.4), kind=kOutput, calls=%fused_computation.7 | convolution fusion | flops 1610612736 | bytes 4980736 | tf_op jit(solution)/shard_map/dot_general | solution.py:248
  289.1 46.5 %all-to-all-done.2 = bf16[128,8,2048]{2,1,0:T(8,128)(2,1)} async-done(((bf16[128,8,2048]{2,1,0:T(8,128)(2,1)}), bf16[128,8,2048]{2,1,0:T(8,128)(2,1)}, u32[]{:S(2)}, u32[]{:S(2)}) %all-to-all-start.2) | async-done | bytes 4194336 | tf_op jit(solution)/shard_map/all_to_all | solution.py:242
  335.6 5.7 %fusion.15 = f32[64,2048]{1,0:T(8,128)} fusion(f32[64,2048]{1,0:T(8,128)} %copy-done.4, f32[64,2048]{1,0:T(8,128)} %fusion, f32[64,1024]{1,0:T(8,128)S(1)} %bitcast.159, bf16[128,8,2048]{2,1,0:T(8,128)(2,1)} %all-to-all-done.2), kind=kOutput, calls=%fused_computation.22 | convolution fusion | flops 1610874880 | bytes 6029312 | tf_op jit(solution)/shard_map/dot_general | solution.py:248
  (122 shorter events, 37.5 us)
Async XLA Ops:
  6.5 24.4 %copy-start = (bf16[192,32,256]{2,1,0:T(8,128)(2,1)S(1)}, bf16[192,32,256]{2,1,0:T(8,128)(2,1)}, u32[]{:S(2)}) copy-start(bf16[192,32,256]{2,1,0:T(8,128)(2,1)} %param.13) | copy-start | bytes 9437188
  6.5 14.0 %copy-start.15 = (s32[16]{0:T(128)S(1)}, s32[16]{0:T(128)}, u32[]{:S(2)}) copy-start(s32[16]{0:T(128)} %param.15) | copy-start | bytes 196
  6.5 13.6 %copy-start.9 = (s32[64,6]{0,1:T(8,128)S(1)}, s32[64,6]{0,1:T(8,128)}, u32[]{:S(2)}) copy-start(s32[64,6]{0,1:T(8,128)} %param.21) | copy-start | bytes 4612
  6.5 14.8 %copy-start.8 = (s32[4,64]{1,0:T(4,128)S(1)}, s32[4,64]{1,0:T(4,128)}, u32[]{:S(2)}) copy-start(s32[4,64]{1,0:T(4,128)} %param.14) | copy-start | bytes 3076
  6.5 17.3 %copy-start.2 = (s32[16]{0:T(128)S(1)}, s32[16]{0:T(128)}, u32[]{:S(2)}) copy-start(s32[16]{0:T(128)} %param.16) | copy-start | bytes 196
  6.5 83.0 %all-gather.2.cloned.1.call-start = ((), (), s32[]{:S(2)}) async-start(), calls=%async_computation.5 | async-start | bytes 8650752 | tf_op jit(solution)/shard_map/all_gather | solution.py:201
  14.2 10.5 %collective-permute-start.2 = (bf16[256,384]{1,0:T(8,128)(2,1)}, bf16[256,384]{1,0:T(8,128)(2,1)}, u32[]{:S(2)}, u32[]{:S(2)}) collective-permute-start(bf16[256,384]{1,0:T(8,128)(2,1)} %get-tuple-element.27), channel_id=1, source_target_pairs={{0,32},{32,64},{64,96},{96,0},{1,33},{33,65},{65,97},{97,1},{2,34}... | collective-permute-start | bytes 589832 | tf_op jit(solution)/shard_map/ppermute | solution.py:156
  15.9 12.0 %collective-permute-start.1 = (bf16[256,384]{1,0:T(8,128)(2,1)}, bf16[256,384]{1,0:T(8,128)(2,1)}, u32[]{:S(2)}, u32[]{:S(2)}) collective-permute-start(bf16[256,384]{1,0:T(8,128)(2,1)} %get-tuple-element.25), channel_id=1, source_target_pairs={{0,64},{32,96},{64,0},{96,32},{1,65},{33,97},{65,1},{97,33},{2,66}... | collective-permute-start | bytes 589832 | tf_op jit(solution)/shard_map/ppermute | solution.py:156
  18.8 9.1 %collective-permute-start = (bf16[256,384]{1,0:T(8,128)(2,1)}, bf16[256,384]{1,0:T(8,128)(2,1)}, u32[]{:S(2)}, u32[]{:S(2)}) collective-permute-start(bf16[256,384]{1,0:T(8,128)(2,1)} %get-tuple-element.26), channel_id=1, source_target_pairs={{0,96},{32,0},{64,32},{96,64},{1,97},{33,1},{65,33},{97,65},{2,98}... | collective-permute-start | bytes 589832 | tf_op jit(solution)/shard_map/ppermute | solution.py:156
  30.2 3.5 %collective-permute-start.3 = (bf16[4,256,128]{2,1,0:T(8,128)(2,1)S(1)}, bf16[4,256,128]{2,1,0:T(8,128)(2,1)}, u32[]{:S(2)}, u32[]{:S(2)}) collective-permute-start(bf16[4,256,128]{2,1,0:T(8,128)(2,1)S(1)} %slice.92), channel_id=1, source_target_pairs={{0,1},{1,0},{2,3},{3,2},{4,5},{5,4},{6,7},{7,6},{8,9},{9,8},{10,11... | collective-permute-start | bytes 786440 | tf_op jit(solution)/shard_map/ppermute | solution.py:18
  49.6 6.9 %copy-start.5 = (f32[4,512,64]{2,1,0:T(8,128)S(1)}, f32[4,512,64]{2,1,0:T(8,128)}, u32[]{:S(2)}) copy-start(f32[4,512,64]{2,1,0:T(8,128)} %get-tuple-element.9) | copy-start | bytes 1572868
  52.4 2.8 collective-permute-start.5
  53.0 2.1 collective-permute-start.6
  53.2 2.0 collective-permute-start.4
  57.6 8.1 %collective-permute-start.9 = (bf16[512,64]{1,0:T(8,128)(2,1)S(1)}, bf16[512,64]{1,0:T(8,128)(2,1)S(1)}, u32[]{:S(2)}, u32[]{:S(2)}) collective-permute-start(bf16[512,64]{1,0:T(8,128)(2,1)S(1)} %get-tuple-element.29), channel_id=1, source_target_pairs={{0,96},{32,0},{64,32},{96,64},{1,97},{33,1},{65,33},{97,65},{2,98}... | collective-permute-start | bytes 196616 | tf_op jit(solution)/shard_map/ppermute | solution.py:194
  59.7 7.9 %collective-permute-start.8 = (bf16[512,64]{1,0:T(8,128)(2,1)S(1)}, bf16[512,64]{1,0:T(8,128)(2,1)S(1)}, u32[]{:S(2)}, u32[]{:S(2)}) collective-permute-start(bf16[512,64]{1,0:T(8,128)(2,1)S(1)} %get-tuple-element.30), channel_id=1, source_target_pairs={{0,64},{32,96},{64,0},{96,32},{1,65},{33,97},{65,1},{97,33},{2,66}... | collective-permute-start | bytes 196616 | tf_op jit(solution)/shard_map/ppermute | solution.py:194
  60.8 8.6 %collective-permute-start.7 = (bf16[512,64]{1,0:T(8,128)(2,1)S(1)}, bf16[512,64]{1,0:T(8,128)(2,1)S(1)}, u32[]{:S(2)}, u32[]{:S(2)}) collective-permute-start(bf16[512,64]{1,0:T(8,128)(2,1)S(1)} %get-tuple-element.31), channel_id=1, source_target_pairs={{0,32},{32,64},{64,96},{96,0},{1,33},{33,65},{65,97},{97,1},{2,34}... | collective-permute-start | bytes 196616 | tf_op jit(solution)/shard_map/ppermute | solution.py:194
  69.4 20.2 %copy-start.7 = (bf16[64,2048]{1,0:T(8,128)(2,1)S(1)}, bf16[64,2048]{1,0:T(8,128)(2,1)}, u32[]{:S(2)}) copy-start(bf16[64,2048]{1,0:T(8,128)(2,1)} %param.18) | copy-start | bytes 786436
  71.3 17.1 %all-to-all-start = ((bf16[32,2,2048]{2,1,0:T(2,128)(2,1)}), bf16[32,2,2048]{2,1,0:T(2,128)(2,1)S(1)}, u32[]{:S(2)}, u32[]{:S(2)}) async-start(bf16[32,2,2048]{2,1,0:T(2,128)(2,1)} %reshape.404), calls=%async_computation | async-start | bytes 524288 | tf_op jit(solution)/shard_map/all_to_all | solution.py:199
  158.3 6.9 %copy-start.16 = (bf16[2,2048,352]{1,2,0:T(8,128)(2,1)S(1)}, bf16[2,2048,352]{1,2,0:T(8,128)(2,1)}, u32[]{:S(2)}) copy-start(bf16[2,2048,352]{1,2,0:T(8,128)(2,1)} %param.23) | copy-start | bytes 8650756
  158.3 59.4 %all-to-all-start.1 = ((bf16[128,8,2048]{2,1,0:T(8,128)(2,1)}), bf16[128,8,2048]{2,1,0:T(8,128)(2,1)}, u32[]{:S(2)}, u32[]{:S(2)}) async-start(bf16[128,8,2048]{2,1,0:T(8,128)(2,1)} %bitcast.154), calls=%async_computation.1 | async-start | bytes 8388608 | tf_op jit(solution)/shard_map/all_to_all | solution.py:235
  217.8 58.3 %all-to-all-start.4 = ((bf16[128,8,2048]{2,1,0:T(8,128)(2,1)}), bf16[128,8,2048]{2,1,0:T(8,128)(2,1)}, u32[]{:S(2)}, u32[]{:S(2)}) async-start(bf16[128,8,2048]{2,1,0:T(8,128)(2,1)} %convert_bitcast_fusion), calls=%async_computation.4 | async-start | bytes 8388608 | tf_op jit(solution)/shard_map/all_to_all | solution.py:242
  238.1 45.2 %copy-start.13 = (f32[64,6]{0,1:T(8,128)S(1)}, f32[64,6]{0,1:T(8,128)}, u32[]{:S(2)}) copy-start(f32[64,6]{0,1:T(8,128)} %param.22) | copy-start | bytes 4612
  276.1 59.5 %all-to-all-start.2 = ((bf16[128,8,2048]{2,1,0:T(8,128)(2,1)}), bf16[128,8,2048]{2,1,0:T(8,128)(2,1)}, u32[]{:S(2)}, u32[]{:S(2)}) async-start(bf16[128,8,2048]{2,1,0:T(8,128)(2,1)} %convert_bitcast_fusion.1), calls=%async_computation.2 | async-start | bytes 8388608 | tf_op jit(solution)/shard_map/all_to_all | solution.py:242
  (8 other events, 34.7 us)
Sparse Core Ops, SparseCore 0:
  9.6 55.4 all-gather.1

commit v8 on v7

--- a/solution.py
+++ b/solution.py
@@ -239,12 +239,10 @@
         active = (jax.nn.silu(gate_part) * up_part).astype(jnp.bfloat16)
         partial_value = jnp.dot(active, expert_down[k], preferred_element_type=jnp.float32)
         partial_value = partial_value.astype(jnp.bfloat16).reshape(arrived_rows.shape)
-        returned = lax.all_to_all(
-            partial_value, ("dp", "tensor"), split_axis=0, concat_axis=0, tiled=True
-        )
+        reduced = lax.psum_scatter(partial_value, "dp", scatter_dimension=0, tiled=True)
+        returned = lax.all_to_all(reduced, "tensor", split_axis=0, concat_axis=0, tiled=True)
         hit = (owner_slot[:, None] == slot_ids[None, :]) & (parity == k)[:, None]
         coeff = jnp.where(hit, flat_gates[:, None], 0.0).reshape(tok_rows, TOP, -1).sum(axis=1)
-        coeff = jnp.tile(coeff, (1, group_count))
         routed = routed + jnp.dot(
             coeff,
             returned.reshape(-1, width).astype(jnp.float32),

time: 349 us -> 341 us (0.977)
  blocking collectives: 57.6 us -> 122 us
  waiting for transfers between devices: 144 us -> 85.6 us
  matrix products: 44.8 us -> 33.8 us
  starting transfers between devices: 39.5 us -> 33.7 us
    all_to_all x3 -> x2, waiting for transfers between devices: 123 us -> 13.5 us  [shards(): lax.all_to_all(reduced, 'tensor', split_axis=0, concat_axis=0, tiled=True)]
    all_to_all x1 -> x2, blocking collectives: 57.6 us -> 122 us  [shards(): lax.all_to_all(fanned, ('dp', 'tensor'), split_axis=0, concat_axis=0, til...]
    reduce_scatter x0 -> x2, waiting for transfers between devices: none -> 51.1 us  [shards(): lax.psum_scatter(partial_value, 'dp', scatter_dimension=0, tiled=True)]
    dot_general x2, matrix products: 9.96 us -> 4.52 us  [shards(): jnp.dot(flat_rows, expert_gate[k], preferred_element_type=jnp.float32)]
    dot_general x2, matrix products: 11 us -> 5.67 us  [shards(): jnp.dot(coeff, returned.reshape(-1, width).astype(jnp.float32), precision...]
    all_to_all x3 -> x2, starting transfers between devices: 19.9 us -> 15 us  [shards(): lax.all_to_all(reduced, 'tensor', split_axis=0, concat_axis=0, tiled=True)]
    unnamed x41 -> x45, local copies, waits for them, and re-layouts: 2.61 us -> 6.49 us
  transfers between devices with their start and end apart: 15 -> 16, of which waited for: 9 -> 8; matrix products, arithmetic and copies ran while one was open for 18% -> 13% of each run, Pallas kernels for 4% -> 4%
where the time goes in v8:
time: 341 us; the launch traced here: 339 us
  blocking collectives  122 us (36%)
  waiting for transfers between devices  85.6 us (25%)
  matrix products  33.8 us (10%)
  starting transfers between devices  33.7 us (10%)
  local copies, waits for them, and re-layouts  24.5 us (7%)
  Pallas kernels  14 us (4%)
  between operations  13.6 us (4%)
  other arithmetic  11.7 us (3%)
    all_to_all x2, blocking collectives, shards(): lax.all_to_all(fanned, ('dp', 'tensor'), split_axis=0, concat_axis=0, til...  122 us
    reduce_scatter x2, waiting for transfers between devices, shards(): lax.psum_scatter(partial_value, 'dp', scatter_dimension=0, tiled=True)  51.1 us
    dot_general x2, matrix products, shards(): jnp.dot(active, expert_down[k], preferred_element_type=jnp.float32)  18.5 us
    all_to_all x2, starting transfers between devices, shards(): lax.all_to_all(reduced, 'tensor', split_axis=0, concat_axis=0, tiled=True)  15 us
    pallas_call x1, Pallas kernels, attention_kernel(): pl.pallas_call(body, grid_spec=grid_spec, out_shape=[jax.ShapeDtypeStruct...  14 us
    all_to_all x2, waiting for transfers between devices, shards(): lax.all_to_all(reduced, 'tensor', split_axis=0, concat_axis=0, tiled=True)  13.5 us
    all_to_all x1, waiting for transfers between devices, shards(): lax.all_to_all(head_out, 'tensor', split_axis=0, concat_axis=0, tiled=True)  8.65 us
    all_to_all x1, starting transfers between devices, shards(): lax.all_to_all(head_out, 'tensor', split_axis=0, concat_axis=0, tiled=True)  8.02 us
  transfers between devices with their start and end apart: 16, of which 8 were waited for; matrix products, arithmetic and copies ran while one was open for 13% of the time, Pallas kernels for 4%

profile of v8, /device:TPU:0, one launch (start us, length us, event | category | flops | bytes accessed | tf_op | source)
XLA Modules:
  0.0 339.2 jit_solution(1183274111852754237)
XLA Ops:
  9.5 2.8 gather_fusion.1
  12.3 2.0 fusion.76
  17.5 2.1 collective-permute-start.1
  24.3 3.8 %collective-permute-done.1 = bf16[256,384]{1,0:T(8,128)(2,1)} collective-permute-done((bf16[256,384]{1,0:T(8,128)(2,1)}, bf16[256,384]{1,0:T(8,128)(2,1)}, u32[]{:S(2)}, u32[]{:S(2)}) %collective-permute-start.1) | collective-permute-done | bytes 196640 | tf_op jit(solution)/shard_map/ppermute | solution.py:156
  31.0 2.8 gather_fusion.3
  35.7 14.0 %shard_map.127 = (f32[4,512,64]{2,1,0:T(8,128)}, f32[4,512,64]{2,1,0:T(8,128)}, f32[4,1,512]{2,1,0:T(1,128)}, f32[4,1,512]{2,1,0:T(1,128)}) custom-call(s32[6]{0:T(128)} %pad_add_fusion.scal_ref, bf16[4,512,128]{2,1,0:T(8,128)(2,1)} %pad_maximum_fusion.1.q_ref, bf16[4,2048,256]{2,1,0:T(8,128)(2,1)} %bitcast.145, bf16[4,256,384]{2,1,0:T(8,128)(2,1)} %copy-done.3), custom_call_target="tpu_custom_call" | custom-call | tf_op jit(solution)/shard_map/pallas_call | solution.py:79
  58.8 2.1 collective-permute-start.8
  61.5 6.0 %collective-permute-done.7 = bf16[512,64]{1,0:T(8,128)(2,1)S(1)} collective-permute-done((bf16[512,64]{1,0:T(8,128)(2,1)S(1)}, bf16[512,64]{1,0:T(8,128)(2,1)S(1)}, u32[]{:S(2)}, u32[]{:S(2)}) %collective-permute-start.7) | collective-permute-done | bytes 65568 | tf_op jit(solution)/shard_map/ppermute | solution.py:194
  70.1 8.0 %all-to-all-start = ((bf16[32,2,2048]{2,1,0:T(2,128)(2,1)}), bf16[32,2,2048]{2,1,0:T(2,128)(2,1)S(1)}, u32[]{:S(2)}, u32[]{:S(2)}) async-start(bf16[32,2,2048]{2,1,0:T(2,128)(2,1)} %reshape.396), calls=%async_computation | async-start | bytes 524288 | tf_op jit(solution)/shard_map/all_to_all | solution.py:199
  78.4 8.7 %all-to-all-done = bf16[32,2,2048]{2,1,0:T(2,128)(2,1)S(1)} async-done(((bf16[32,2,2048]{2,1,0:T(2,128)(2,1)}), bf16[32,2,2048]{2,1,0:T(2,128)(2,1)S(1)}, u32[]{:S(2)}, u32[]{:S(2)}) %all-to-all-start) | async-done | bytes 262176 | tf_op jit(solution)/shard_map/all_to_all | solution.py:199
  88.2 5.1 %multiply_reduce_fusion = (f32[64]{0:T(128)S(1)}, f32[64,2048]{1,0:T(8,128)S(1)}) fusion(bf16[64,2048]{1,0:T(8,128)(2,1)S(1)} %reshape.323, bf16[2048,2048]{1,0:T(8,128)(2,1)} %all-gather.2.cloned.1.call-done, bf16[64,2048]{1,0:T(8,128)(2,1)S(1)} %copy-done.9), kind=kOutput, calls=%fused_computation.52 | convolution fusion | flops 537395136 | bytes 9437440 | tf_op jit(solution)/shard_map/dot_general | solution.py:202
  93.5 2.5 gather_fusion.5
  96.8 58.8 %all_to_all.25 = bf16[128,8,2048]{2,1,0:T(8,128)(2,1)S(1)} all-to-all(bf16[128,8,2048]{2,1,0:T(8,128)(2,1)S(1)} %bitcast.146), channel_id=1, replica_groups=mesh['dp'=4,'tensor'=32] {'dp','tensor'}, dimensions={0} | all-to-all | bytes 8388608 | tf_op jit(solution)/shard_map/all_to_all | solution.py:235
  159.3 9.0 %convert_bitcast_fusion.1 = bf16[128,8,2048]{2,1,0:T(8,128)(2,1)} fusion(bf16[2,352,2048]{2,1,0:T(8,128)(2,1)} %param.25, bf16[2,2048,352]{1,2,0:T(8,128)(2,1)} %param.24, bf16[128,8,2048]{2,1,0:T(8,128)(2,1)} %copy-done.5, f32[1024,352]{0,1:T(8,128)S(1)} %fusion.6), kind=kOutput, calls=%fused_computation.16 | convolution fusion | flops 2957049856 | bytes 12713984 | tf_op jit(solution)/shard_map/dot_general | solution.py:240
  168.9 63.5 %all_to_all.26 = bf16[128,8,2048]{2,1,0:T(8,128)(2,1)S(1)} all-to-all(bf16[128,8,2048]{2,1,0:T(8,128)(2,1)S(1)} %bitcast.147), channel_id=1, replica_groups=mesh['dp'=4,'tensor'=32] {'dp','tensor'}, dimensions={0} | all-to-all | bytes 8388608 | tf_op jit(solution)/shard_map/all_to_all | solution.py:235
  234.4 2.8 fusion.2
  237.3 9.5 %convert_bitcast_fusion = bf16[128,8,2048]{2,1,0:T(8,128)(2,1)} fusion(bf16[2,352,2048]{2,1,0:T(8,128)(2,1)} %param.25, bf16[2,2048,352]{1,2,0:T(8,128)(2,1)} %param.24, bf16[128,8,2048]{2,1,0:T(8,128)(2,1)} %copy-done.6, f32[1024,352]{0,1:T(8,128)} %fusion.2), kind=kOutput, calls=%fused_computation.15 | convolution fusion | flops 2957049856 | bytes 12713984 | tf_op jit(solution)/shard_map/dot_general | solution.py:240
  246.8 9.7 %reduce-scatter.3.cloned.1.call-done = bf16[32,8,2048]{2,1,0:T(8,128)(2,1)} async-done(((bf16[128,8,2048]{2,1,0:T(8,128)(2,1)}), bf16[32,8,2048]{2,1,0:T(8,128)(2,1)}) %reduce-scatter.3.cloned.1.call-update) | async-done | bytes 1048592 | tf_op jit(solution)/shard_map/reduce_scatter | solution.py:242
  256.5 7.7 %all-to-all-start.2 = ((bf16[32,8,2048]{2,1,0:T(8,128)(2,1)}), bf16[32,8,2048]{2,1,0:T(8,128)(2,1)}, u32[]{:S(2)}, u32[]{:S(2)}) async-start(bf16[32,8,2048]{2,1,0:T(8,128)(2,1)} %reduce-scatter.3.cloned.1.call-done), calls=%async_computation.3 | async-start | bytes 2097152 | tf_op jit(solution)/shard_map/all_to_all | solution.py:243
  264.2 41.4 %reduce-scatter.5.cloned.1.call-done = bf16[32,8,2048]{2,1,0:T(8,128)(2,1)} async-done(((bf16[128,8,2048]{2,1,0:T(8,128)(2,1)}), bf16[32,8,2048]{2,1,0:T(8,128)(2,1)}) %reduce-scatter.5.cloned.1.call-update) | async-done | bytes 1048592 | tf_op jit(solution)/shard_map/reduce_scatter | solution.py:242
  305.6 7.3 %all-to-all-start.4 = ((bf16[32,8,2048]{2,1,0:T(8,128)(2,1)}), bf16[32,8,2048]{2,1,0:T(8,128)(2,1)}, u32[]{:S(2)}, u32[]{:S(2)}) async-start(bf16[32,8,2048]{2,1,0:T(8,128)(2,1)} %reduce-scatter.5.cloned.1.call-done), calls=%async_computation.6 | async-start | bytes 2097152 | tf_op jit(solution)/shard_map/all_to_all | solution.py:243
  313.4 2.7 fusion.38
  316.2 13.5 %all-to-all-done.4 = bf16[32,8,2048]{2,1,0:T(8,128)(2,1)} async-done(((bf16[32,8,2048]{2,1,0:T(8,128)(2,1)}), bf16[32,8,2048]{2,1,0:T(8,128)(2,1)}, u32[]{:S(2)}, u32[]{:S(2)}) %all-to-all-start.4) | async-done | bytes 1048608 | tf_op jit(solution)/shard_map/all_to_all | solution.py:243
  329.7 3.0 fusion.8
  (129 shorter events, 36.8 us)
Async XLA Ops:
  6.5 24.5 %copy-start = (bf16[192,32,256]{2,1,0:T(8,128)(2,1)S(1)}, bf16[192,32,256]{2,1,0:T(8,128)(2,1)}, u32[]{:S(2)}) copy-start(bf16[192,32,256]{2,1,0:T(8,128)(2,1)} %param.13) | copy-start | bytes 9437188
  6.5 14.3 %copy-start.10 = (s32[4,64]{1,0:T(4,128)S(1)}, s32[4,64]{1,0:T(4,128)}, u32[]{:S(2)}) copy-start(s32[4,64]{1,0:T(4,128)} %param.14) | copy-start | bytes 3076
  6.5 16.8 %copy-start.2 = (s32[16]{0:T(128)S(1)}, s32[16]{0:T(128)}, u32[]{:S(2)}) copy-start(s32[16]{0:T(128)} %param.16) | copy-start | bytes 196
  6.5 81.7 %all-gather.2.cloned.1.call-start = ((), (), s32[]{:S(2)}) async-start(), calls=%async_computation.7 | async-start | bytes 8650752 | tf_op jit(solution)/shard_map/all_gather | solution.py:201
  14.3 10.0 %collective-permute-start.2 = (bf16[256,384]{1,0:T(8,128)(2,1)}, bf16[256,384]{1,0:T(8,128)(2,1)}, u32[]{:S(2)}, u32[]{:S(2)}) collective-permute-start(bf16[256,384]{1,0:T(8,128)(2,1)} %get-tuple-element.27), channel_id=1, source_target_pairs={{0,32},{32,64},{64,96},{96,0},{1,33},{33,65},{65,97},{97,1},{2,34}... | collective-permute-start | bytes 589832 | tf_op jit(solution)/shard_map/ppermute | solution.py:156
  16.0 8.3 %collective-permute-start = (bf16[256,384]{1,0:T(8,128)(2,1)}, bf16[256,384]{1,0:T(8,128)(2,1)}, u32[]{:S(2)}, u32[]{:S(2)}) collective-permute-start(bf16[256,384]{1,0:T(8,128)(2,1)} %get-tuple-element.26), channel_id=1, source_target_pairs={{0,96},{32,0},{64,32},{96,64},{1,97},{33,1},{65,33},{97,65},{2,98}... | collective-permute-start | bytes 589832 | tf_op jit(solution)/shard_map/ppermute | solution.py:156
  17.5 10.5 %collective-permute-start.1 = (bf16[256,384]{1,0:T(8,128)(2,1)}, bf16[256,384]{1,0:T(8,128)(2,1)}, u32[]{:S(2)}, u32[]{:S(2)}) collective-permute-start(bf16[256,384]{1,0:T(8,128)(2,1)} %get-tuple-element.25), channel_id=1, source_target_pairs={{0,64},{32,96},{64,0},{96,32},{1,65},{33,97},{65,1},{97,33},{2,66}... | collective-permute-start | bytes 589832 | tf_op jit(solution)/shard_map/ppermute | solution.py:156
  30.3 3.6 %collective-permute-start.3 = (bf16[4,256,128]{2,1,0:T(8,128)(2,1)S(1)}, bf16[4,256,128]{2,1,0:T(8,128)(2,1)}, u32[]{:S(2)}, u32[]{:S(2)}) collective-permute-start(bf16[4,256,128]{2,1,0:T(8,128)(2,1)S(1)} %slice.92), channel_id=1, source_target_pairs={{0,1},{1,0},{2,3},{3,2},{4,5},{5,4},{6,7},{7,6},{8,9},{9,8},{10,11... | collective-permute-start | bytes 786440 | tf_op jit(solution)/shard_map/ppermute | solution.py:18
  52.5 2.9 collective-permute-start.5
  53.3 2.1 collective-permute-start.4
  53.4 2.0 collective-permute-start.6
  57.9 9.7 %collective-permute-start.7 = (bf16[512,64]{1,0:T(8,128)(2,1)S(1)}, bf16[512,64]{1,0:T(8,128)(2,1)S(1)}, u32[]{:S(2)}, u32[]{:S(2)}) collective-permute-start(bf16[512,64]{1,0:T(8,128)(2,1)S(1)} %get-tuple-element.31), channel_id=1, source_target_pairs={{0,32},{32,64},{64,96},{96,0},{1,33},{33,65},{65,97},{97,1},{2,34}... | collective-permute-start | bytes 196616 | tf_op jit(solution)/shard_map/ppermute | solution.py:194
  58.8 8.8 %collective-permute-start.8 = (bf16[512,64]{1,0:T(8,128)(2,1)S(1)}, bf16[512,64]{1,0:T(8,128)(2,1)S(1)}, u32[]{:S(2)}, u32[]{:S(2)}) collective-permute-start(bf16[512,64]{1,0:T(8,128)(2,1)S(1)} %get-tuple-element.30), channel_id=1, source_target_pairs={{0,64},{32,96},{64,0},{96,32},{1,65},{33,97},{65,1},{97,33},{2,66}... | collective-permute-start | bytes 196616 | tf_op jit(solution)/shard_map/ppermute | solution.py:194
  60.9 7.3 %collective-permute-start.9 = (bf16[512,64]{1,0:T(8,128)(2,1)S(1)}, bf16[512,64]{1,0:T(8,128)(2,1)S(1)}, u32[]{:S(2)}, u32[]{:S(2)}) collective-permute-start(bf16[512,64]{1,0:T(8,128)(2,1)S(1)} %get-tuple-element.29), channel_id=1, source_target_pairs={{0,96},{32,0},{64,32},{96,64},{1,97},{33,1},{65,33},{97,65},{2,98}... | collective-permute-start | bytes 196616 | tf_op jit(solution)/shard_map/ppermute | solution.py:194
  68.2 20.1 %copy-start.9 = (bf16[64,2048]{1,0:T(8,128)(2,1)S(1)}, bf16[64,2048]{1,0:T(8,128)(2,1)}, u32[]{:S(2)}) copy-start(bf16[64,2048]{1,0:T(8,128)(2,1)} %param.18) | copy-start | bytes 786436
  70.1 16.9 %all-to-all-start = ((bf16[32,2,2048]{2,1,0:T(2,128)(2,1)}), bf16[32,2,2048]{2,1,0:T(2,128)(2,1)S(1)}, u32[]{:S(2)}, u32[]{:S(2)}) async-start(bf16[32,2,2048]{2,1,0:T(2,128)(2,1)} %reshape.396), calls=%async_computation | async-start | bytes 524288 | tf_op jit(solution)/shard_map/all_to_all | solution.py:199
  78.1 178.3 %reduce-scatter.3.cloned.1.call-start = ((), (), s32[]{:S(2)}) async-start(), calls=%async_computation.8 | async-start | bytes 5242880 | tf_op jit(solution)/shard_map/reduce_scatter | solution.py:242
  96.8 60.8 %copy-start.18 = (bf16[2,2048,352]{1,2,0:T(8,128)(2,1)S(1)}, bf16[2,2048,352]{1,2,0:T(8,128)(2,1)}, u32[]{:S(2)}) copy-start(bf16[2,2048,352]{1,2,0:T(8,128)(2,1)} %param.23) | copy-start | bytes 8650756
  168.4 137.2 %reduce-scatter.5.cloned.1.call-start = ((), (), s32[]{:S(2)}) async-start(), calls=%async_computation.9 | async-start | bytes 5242880 | tf_op jit(solution)/shard_map/reduce_scatter | solution.py:242
  168.9 65.5 %copy-start.19 = (bf16[2,2048,352]{1,2,0:T(8,128)(2,1)S(1)}, bf16[2,2048,352]{1,2,0:T(8,128)(2,1)}, u32[]{:S(2)}) copy-start(bf16[2,2048,352]{1,2,0:T(8,128)(2,1)} %param.23) | copy-start | bytes 8650756
  246.8 66.4 %copy-start.15 = (f32[64,6]{0,1:T(8,128)S(1)}, f32[64,6]{0,1:T(8,128)}, u32[]{:S(2)}) copy-start(f32[64,6]{0,1:T(8,128)} %param.22) | copy-start | bytes 4612
  256.5 49.1 %all-to-all-start.2 = ((bf16[32,8,2048]{2,1,0:T(8,128)(2,1)}), bf16[32,8,2048]{2,1,0:T(8,128)(2,1)}, u32[]{:S(2)}, u32[]{:S(2)}) async-start(bf16[32,8,2048]{2,1,0:T(8,128)(2,1)} %reduce-scatter.3.cloned.1.call-done), calls=%async_computation.3 | async-start | bytes 2097152 | tf_op jit(solution)/shard_map/all_to_all | solution.py:243
  264.2 68.5 %copy-start.1 = (bf16[192,32,256]{2,1,0:T(8,128)(2,1)S(1)}, bf16[192,32,256]{2,1,0:T(8,128)(2,1)}, u32[]{:S(2)}) copy-start(bf16[192,32,256]{2,1,0:T(8,128)(2,1)} %param.13) | copy-start | bytes 9437188
  305.6 24.1 %all-to-all-start.4 = ((bf16[32,8,2048]{2,1,0:T(8,128)(2,1)}), bf16[32,8,2048]{2,1,0:T(8,128)(2,1)}, u32[]{:S(2)}, u32[]{:S(2)}) async-start(bf16[32,8,2048]{2,1,0:T(8,128)(2,1)} %reduce-scatter.5.cloned.1.call-done), calls=%async_computation.6 | async-start | bytes 2097152 | tf_op jit(solution)/shard_map/all_to_all | solution.py:243
  (12 other events, 66.8 us)
Sparse Core Ops, SparseCore 0:
  9.6 55.3 all-gather.1
  168.5 87.9 reduce-scatter.2
  258.9 46.6 reduce-scatter.4

commit v9 on v8

--- a/solution.py
+++ b/solution.py
@@ -230,9 +230,10 @@
     slot_ids = jnp.arange(tensor_size * capacity, dtype=jnp.int32)
     flat_gates = route_gates.reshape(-1)
     for k in range(experts_here):
-        fanned = jnp.broadcast_to(outgoing_rows[None, :, k], (group_count,) + outgoing_rows[:, k].shape)
-        fanned = fanned.reshape((group_count * tensor_size, capacity, width))
-        arrived_rows = lax.all_to_all(fanned, ("dp", "tensor"), split_axis=0, concat_axis=0, tiled=True)
+        same_group = lax.all_to_all(
+            outgoing_rows[:, k], "tensor", split_axis=0, concat_axis=0, tiled=True
+        )
+        arrived_rows = lax.all_gather(same_group, "dp", axis=0, tiled=True)
         flat_rows = arrived_rows.reshape(-1, width)
         gate_part = jnp.dot(flat_rows, expert_gate[k], preferred_element_type=jnp.float32)
         up_part = jnp.dot(flat_rows, expert_up[k], preferred_element_type=jnp.float32)

time: 341 us -> 347 us (1.018)
  waiting for transfers between devices: 85.6 us -> 172 us
  blocking collectives: 122 us -> 41.2 us
  matrix products: 33.8 us -> 39.6 us
  local copies, waits for them, and re-layouts: 24.5 us -> 19.5 us
    all_to_all x2, blocking collectives: 122 us -> 41.2 us  [shards(): lax.all_to_all(outgoing_rows[:, k], 'tensor', split_axis=0, concat_axis=0...]
    all_gather x0 -> x2, waiting for transfers between devices: none -> 60.7 us  [shards(): arrived_rows = lax.all_gather(same_group, 'dp', axis=0, tiled=True)]
    reduce_scatter x2, waiting for transfers between devices: 51.1 us -> 76.5 us  [shards(): lax.psum_scatter(partial_value, 'dp', scatter_dimension=0, tiled=True)]
    dot_general x2, matrix products: 4.52 us -> 10.4 us  [shards(): jnp.dot(flat_rows, expert_gate[k], preferred_element_type=jnp.float32)]
    unnamed x45 -> x41, local copies, waits for them, and re-layouts: 6.49 us -> 2.54 us
  transfers between devices with their start and end apart: 16 -> 18, of which waited for: 8 -> 10; matrix products, arithmetic and copies ran while one was open for 13% -> 17% of each run, Pallas kernels for 4% -> 4%
where the time goes in v9:
time: 347 us; the launch traced here: 345 us
  waiting for transfers between devices  172 us (50%)
  blocking collectives  41.2 us (12%)
  matrix products  39.6 us (11%)
  starting transfers between devices  33.8 us (10%)
  local copies, waits for them, and re-layouts  19.5 us (6%)
  Pallas kernels  14 us (4%)
  between operations  13.6 us (4%)
  other arithmetic  11.7 us (3%)
    reduce_scatter x2, waiting for transfers between devices, shards(): lax.psum_scatter(partial_value, 'dp', scatter_dimension=0, tiled=True)  76.5 us
    all_gather x2, waiting for transfers between devices, shards(): arrived_rows = lax.all_gather(same_group, 'dp', axis=0, tiled=True)  60.7 us
    all_to_all x2, blocking collectives, shards(): lax.all_to_all(outgoing_rows[:, k], 'tensor', split_axis=0, concat_axis=0...  41.2 us
    dot_general x2, matrix products, shards(): jnp.dot(active, expert_down[k], preferred_element_type=jnp.float32)  18.4 us
    all_to_all x2, starting transfers between devices, shards(): lax.all_to_all(reduced, 'tensor', split_axis=0, concat_axis=0, tiled=True)  14.7 us
    pallas_call x1, Pallas kernels, attention_kernel(): pl.pallas_call(body, grid_spec=grid_spec, out_shape=[jax.ShapeDtypeStruct...  14 us
    all_to_all x2, waiting for transfers between devices, shards(): lax.all_to_all(reduced, 'tensor', split_axis=0, concat_axis=0, tiled=True)  13.5 us
    dot_general x2, matrix products, shards(): jnp.dot(flat_rows, expert_gate[k], preferred_element_type=jnp.float32)  10.4 us
  transfers between devices with their start and end apart: 18, of which 10 were waited for; matrix products, arithmetic and copies ran while one was open for 17% of the time, Pallas kernels for 4%

profile of v9, /device:TPU:0, one launch (start us, length us, event | category | flops | bytes accessed | tf_op | source)
XLA Modules:
  0.0 345.1 jit_solution(11983670838248359924)
XLA Ops:
  9.6 2.8 gather_fusion.1
  24.3 3.8 %collective-permute-done.1 = bf16[256,384]{1,0:T(8,128)(2,1)} collective-permute-done((bf16[256,384]{1,0:T(8,128)(2,1)}, bf16[256,384]{1,0:T(8,128)(2,1)}, u32[]{:S(2)}, u32[]{:S(2)}) %collective-permute-start.1) | collective-permute-done | bytes 196640 | tf_op jit(solution)/shard_map/ppermute | solution.py:156
  31.0 2.8 gather_fusion.3
  35.8 14.0 %shard_map.127 = (f32[4,512,64]{2,1,0:T(8,128)}, f32[4,512,64]{2,1,0:T(8,128)}, f32[4,1,512]{2,1,0:T(1,128)}, f32[4,1,512]{2,1,0:T(1,128)}) custom-call(s32[6]{0:T(128)} %pad_add_fusion.scal_ref, bf16[4,512,128]{2,1,0:T(8,128)(2,1)} %pad_maximum_fusion.1.q_ref, bf16[4,2048,256]{2,1,0:T(8,128)(2,1)} %bitcast.143, bf16[4,256,384]{2,1,0:T(8,128)(2,1)} %copy-done.3), custom_call_target="tpu_custom_call" | custom-call | tf_op jit(solution)/shard_map/pallas_call | solution.py:79
  61.6 6.0 %collective-permute-done.7 = bf16[512,64]{1,0:T(8,128)(2,1)S(1)} collective-permute-done((bf16[512,64]{1,0:T(8,128)(2,1)S(1)}, bf16[512,64]{1,0:T(8,128)(2,1)S(1)}, u32[]{:S(2)}, u32[]{:S(2)}) %collective-permute-start.7) | collective-permute-done | bytes 65568 | tf_op jit(solution)/shard_map/ppermute | solution.py:194
  70.1 8.1 %all-to-all-start = ((bf16[32,2,2048]{2,1,0:T(2,128)(2,1)}), bf16[32,2,2048]{2,1,0:T(2,128)(2,1)S(1)}, u32[]{:S(2)}, u32[]{:S(2)}) async-start(bf16[32,2,2048]{2,1,0:T(2,128)(2,1)} %reshape.386), calls=%async_computation | async-start | bytes 524288 | tf_op jit(solution)/shard_map/all_to_all | solution.py:199
  78.5 8.7 %all-to-all-done = bf16[32,2,2048]{2,1,0:T(2,128)(2,1)S(1)} async-done(((bf16[32,2,2048]{2,1,0:T(2,128)(2,1)}), bf16[32,2,2048]{2,1,0:T(2,128)(2,1)S(1)}, u32[]{:S(2)}, u32[]{:S(2)}) %all-to-all-start) | async-done | bytes 262176 | tf_op jit(solution)/shard_map/all_to_all | solution.py:199
  88.3 5.1 %multiply_reduce_fusion = (f32[64]{0:T(128)S(1)}, f32[64,2048]{1,0:T(8,128)S(1)}) fusion(bf16[64,2048]{1,0:T(8,128)(2,1)S(1)} %reshape.315, bf16[2048,2048]{1,0:T(8,128)(2,1)} %all-gather.4.cloned.1.call-done, bf16[64,2048]{1,0:T(8,128)(2,1)S(1)} %copy-done.7), kind=kOutput, calls=%fused_computation.52 | convolution fusion | flops 537395136 | bytes 9437440 | tf_op jit(solution)/shard_map/dot_general | solution.py:202
  93.6 2.5 gather_fusion.5
  96.4 20.4 %all_to_all.25 = bf16[32,8,2048]{2,1,0:T(8,128)(2,1)} all-to-all(bf16[32,8,2048]{2,1,0:T(8,128)(2,1)S(1)} %get-tuple-element.21), channel_id=1, replica_groups=mesh['dp'=4,'tensor'=32] {'tensor'}, dimensions={0} | all-to-all | bytes 2097152 | tf_op jit(solution)/shard_map/all_to_all | solution.py:233
  116.9 20.7 %all_to_all.26 = bf16[32,8,2048]{2,1,0:T(8,128)(2,1)} all-to-all(bf16[32,8,2048]{2,1,0:T(8,128)(2,1)S(1)} %get-tuple-element.20), channel_id=1, replica_groups=mesh['dp'=4,'tensor'=32] {'tensor'}, dimensions={0} | all-to-all | bytes 2097152 | tf_op jit(solution)/shard_map/all_to_all | solution.py:233
  137.7 25.2 %all-gather.6.cloned.1.call-done = bf16[128,8,2048]{2,1,0:T(8,128)(2,1)} async-done(((bf16[32,8,2048]{2,1,0:T(8,128)(2,1)}), bf16[128,8,2048]{2,1,0:T(8,128)(2,1)}) %all-gather.6.cloned.1.call-update) | async-done | bytes 4194320 | tf_op jit(solution)/shard_map/all_gather | solution.py:236
  162.9 5.4 %fusion.6 = f32[1024,352]{0,1:T(8,128)} fusion(bf16[128,8,2048]{2,1,0:T(8,128)(2,1)} %all-gather.6.cloned.1.call-done, bf16[2,2048,352]{1,2,0:T(8,128)(2,1)} %param.23), kind=kOutput, calls=%fused_computation.13 | convolution fusion | flops 1476395008 | bytes 7077888 | tf_op jit(solution)/shard_map/dot_general | solution.py:238
  168.4 9.0 %convert_bitcast_fusion.1 = bf16[128,8,2048]{2,1,0:T(8,128)(2,1)} fusion(bf16[2,352,2048]{2,1,0:T(8,128)(2,1)S(1)} %copy-done.17, bf16[2,2048,352]{1,2,0:T(8,128)(2,1)} %param.24, bf16[128,8,2048]{2,1,0:T(8,128)(2,1)} %all-gather.6.cloned.1.call-done, f32[1024,352]{0,1:T(8,128)} %fusion.6), kind=kOutput, calls=%fused_computation.16 | convolution fusion | flops 2957049856 | bytes 12713984 | tf_op jit(solution)/shard_map/dot_general | solution.py:241
  177.7 35.5 %all-gather.8.cloned.1.call-done = bf16[128,8,2048]{2,1,0:T(8,128)(2,1)} async-done(((bf16[32,8,2048]{2,1,0:T(8,128)(2,1)}), bf16[128,8,2048]{2,1,0:T(8,128)(2,1)}) %all-gather.8.cloned.1.call-update) | async-done | bytes 4194320 | tf_op jit(solution)/shard_map/all_gather | solution.py:236
  213.2 5.0 %fusion.2 = f32[1024,352]{0,1:T(8,128)} fusion(bf16[128,8,2048]{2,1,0:T(8,128)(2,1)} %all-gather.8.cloned.1.call-done, bf16[2,2048,352]{1,2,0:T(8,128)(2,1)S(1)} %copy-done.16), kind=kOutput, calls=%fused_computation.9 | convolution fusion | flops 1476395008 | bytes 7077888 | tf_op jit(solution)/shard_map/dot_general | solution.py:238
  218.2 9.4 %convert_bitcast_fusion = bf16[128,8,2048]{2,1,0:T(8,128)(2,1)} fusion(bf16[2,352,2048]{2,1,0:T(8,128)(2,1)} %param.25, bf16[2,2048,352]{1,2,0:T(8,128)(2,1)} %param.24, bf16[128,8,2048]{2,1,0:T(8,128)(2,1)} %all-gather.8.cloned.1.call-done, f32[1024,352]{0,1:T(8,128)} %fusion.2), kind=kOutput, calls=%fused_computation.15 | convolution fusion | flops 2957049856 | bytes 12713984 | tf_op jit(solution)/shard_map/dot_general | solution.py:241
  227.6 35.0 %reduce-scatter.3.cloned.1.call-done = bf16[32,8,2048]{2,1,0:T(8,128)(2,1)} async-done(((bf16[128,8,2048]{2,1,0:T(8,128)(2,1)}), bf16[32,8,2048]{2,1,0:T(8,128)(2,1)}) %reduce-scatter.3.cloned.1.call-update) | async-done | bytes 1048592 | tf_op jit(solution)/shard_map/reduce_scatter | solution.py:243
  262.6 7.4 %all-to-all-start.2 = ((bf16[32,8,2048]{2,1,0:T(8,128)(2,1)}), bf16[32,8,2048]{2,1,0:T(8,128)(2,1)}, u32[]{:S(2)}, u32[]{:S(2)}) async-start(bf16[32,8,2048]{2,1,0:T(8,128)(2,1)} %reduce-scatter.3.cloned.1.call-done), calls=%async_computation.3 | async-start | bytes 2097152 | tf_op jit(solution)/shard_map/all_to_all | solution.py:244
  270.0 41.5 %reduce-scatter.5.cloned.1.call-done = bf16[32,8,2048]{2,1,0:T(8,128)(2,1)} async-done(((bf16[128,8,2048]{2,1,0:T(8,128)(2,1)}), bf16[32,8,2048]{2,1,0:T(8,128)(2,1)}) %reduce-scatter.5.cloned.1.call-update) | async-done | bytes 1048592 | tf_op jit(solution)/shard_map/reduce_scatter | solution.py:243
  311.5 7.4 %all-to-all-start.4 = ((bf16[32,8,2048]{2,1,0:T(8,128)(2,1)}), bf16[32,8,2048]{2,1,0:T(8,128)(2,1)}, u32[]{:S(2)}, u32[]{:S(2)}) async-start(bf16[32,8,2048]{2,1,0:T(8,128)(2,1)} %reduce-scatter.5.cloned.1.call-done), calls=%async_computation.6 | async-start | bytes 2097152 | tf_op jit(solution)/shard_map/all_to_all | solution.py:244
  319.4 2.7 fusion.38
  322.1 13.5 %all-to-all-done.4 = bf16[32,8,2048]{2,1,0:T(8,128)(2,1)} async-done(((bf16[32,8,2048]{2,1,0:T(8,128)(2,1)}), bf16[32,8,2048]{2,1,0:T(8,128)(2,1)}, u32[]{:S(2)}, u32[]{:S(2)}) %all-to-all-start.4) | async-done | bytes 1048608 | tf_op jit(solution)/shard_map/all_to_all | solution.py:244
  335.6 3.0 fusion.8
  (130 shorter events, 36.7 us)
Async XLA Ops:
  6.5 24.5 %copy-start = (bf16[192,32,256]{2,1,0:T(8,128)(2,1)S(1)}, bf16[192,32,256]{2,1,0:T(8,128)(2,1)}, u32[]{:S(2)}) copy-start(bf16[192,32,256]{2,1,0:T(8,128)(2,1)} %param.13) | copy-start | bytes 9437188
  6.5 81.8 %all-gather.4.cloned.1.call-start = ((), (), s32[]{:S(2)}) async-start(), calls=%async_computation.7 | async-start | bytes 8650752 | tf_op jit(solution)/shard_map/all_gather | solution.py:201
  14.4 9.9 %collective-permute-start.2 = (bf16[256,384]{1,0:T(8,128)(2,1)}, bf16[256,384]{1,0:T(8,128)(2,1)}, u32[]{:S(2)}, u32[]{:S(2)}) collective-permute-start(bf16[256,384]{1,0:T(8,128)(2,1)} %get-tuple-element.27), channel_id=1, source_target_pairs={{0,32},{32,64},{64,96},{96,0},{1,33},{33,65},{65,97},{97,1},{2,34}... | collective-permute-start | bytes 589832 | tf_op jit(solution)/shard_map/ppermute | solution.py:156
  16.1 8.3 %collective-permute-start = (bf16[256,384]{1,0:T(8,128)(2,1)}, bf16[256,384]{1,0:T(8,128)(2,1)}, u32[]{:S(2)}, u32[]{:S(2)}) collective-permute-start(bf16[256,384]{1,0:T(8,128)(2,1)} %get-tuple-element.26), channel_id=1, source_target_pairs={{0,96},{32,0},{64,32},{96,64},{1,97},{33,1},{65,33},{97,65},{2,98}... | collective-permute-start | bytes 589832 | tf_op jit(solution)/shard_map/ppermute | solution.py:156
  17.6 10.5 %collective-permute-start.1 = (bf16[256,384]{1,0:T(8,128)(2,1)}, bf16[256,384]{1,0:T(8,128)(2,1)}, u32[]{:S(2)}, u32[]{:S(2)}) collective-permute-start(bf16[256,384]{1,0:T(8,128)(2,1)} %get-tuple-element.25), channel_id=1, source_target_pairs={{0,64},{32,96},{64,0},{96,32},{1,65},{33,97},{65,1},{97,33},{2,66}... | collective-permute-start | bytes 589832 | tf_op jit(solution)/shard_map/ppermute | solution.py:156
  30.3 3.5 %collective-permute-start.3 = (bf16[4,256,128]{2,1,0:T(8,128)(2,1)S(1)}, bf16[4,256,128]{2,1,0:T(8,128)(2,1)}, u32[]{:S(2)}, u32[]{:S(2)}) collective-permute-start(bf16[4,256,128]{2,1,0:T(8,128)(2,1)S(1)} %slice.92), channel_id=1, source_target_pairs={{0,1},{1,0},{2,3},{3,2},{4,5},{5,4},{6,7},{7,6},{8,9},{9,8},{10,11... | collective-permute-start | bytes 786440 | tf_op jit(solution)/shard_map/ppermute | solution.py:18
  52.5 2.9 collective-permute-start.5
  53.3 2.0 collective-permute-start.4
  53.4 1.9 collective-permute-start.6
  57.9 9.7 %collective-permute-start.7 = (bf16[512,64]{1,0:T(8,128)(2,1)S(1)}, bf16[512,64]{1,0:T(8,128)(2,1)S(1)}, u32[]{:S(2)}, u32[]{:S(2)}) collective-permute-start(bf16[512,64]{1,0:T(8,128)(2,1)S(1)} %get-tuple-element.31), channel_id=1, source_target_pairs={{0,32},{32,64},{64,96},{96,0},{1,33},{33,65},{65,97},{97,1},{2,34}... | collective-permute-start | bytes 196616 | tf_op jit(solution)/shard_map/ppermute | solution.py:194
  58.8 8.8 %collective-permute-start.8 = (bf16[512,64]{1,0:T(8,128)(2,1)S(1)}, bf16[512,64]{1,0:T(8,128)(2,1)S(1)}, u32[]{:S(2)}, u32[]{:S(2)}) collective-permute-start(bf16[512,64]{1,0:T(8,128)(2,1)S(1)} %get-tuple-element.30), channel_id=1, source_target_pairs={{0,64},{32,96},{64,0},{96,32},{1,65},{33,97},{65,1},{97,33},{2,66}... | collective-permute-start | bytes 196616 | tf_op jit(solution)/shard_map/ppermute | solution.py:194
  60.9 7.3 %collective-permute-start.9 = (bf16[512,64]{1,0:T(8,128)(2,1)S(1)}, bf16[512,64]{1,0:T(8,128)(2,1)S(1)}, u32[]{:S(2)}, u32[]{:S(2)}) collective-permute-start(bf16[512,64]{1,0:T(8,128)(2,1)S(1)} %get-tuple-element.29), channel_id=1, source_target_pairs={{0,96},{32,0},{64,32},{96,64},{1,97},{33,1},{65,33},{97,65},{2,98}... | collective-permute-start | bytes 196616 | tf_op jit(solution)/shard_map/ppermute | solution.py:194
  68.2 20.1 %copy-start.7 = (bf16[64,2048]{1,0:T(8,128)(2,1)S(1)}, bf16[64,2048]{1,0:T(8,128)(2,1)}, u32[]{:S(2)}) copy-start(bf16[64,2048]{1,0:T(8,128)(2,1)} %param.18) | copy-start | bytes 786436
  70.1 17.0 %all-to-all-start = ((bf16[32,2,2048]{2,1,0:T(2,128)(2,1)}), bf16[32,2,2048]{2,1,0:T(2,128)(2,1)S(1)}, u32[]{:S(2)}, u32[]{:S(2)}) async-start(bf16[32,2,2048]{2,1,0:T(2,128)(2,1)} %reshape.386), calls=%async_computation | async-start | bytes 524288 | tf_op jit(solution)/shard_map/all_to_all | solution.py:199
  78.2 84.7 %all-gather.6.cloned.1.call-start = ((), (), s32[]{:S(2)}) async-start(), calls=%async_computation.8 | async-start | bytes 5242880 | tf_op jit(solution)/shard_map/all_gather | solution.py:236
  116.9 96.3 %all-gather.8.cloned.1.call-start = ((), (), s32[]{:S(2)}) async-start(), calls=%async_computation.10 | async-start | bytes 5242880 | tf_op jit(solution)/shard_map/all_gather | solution.py:236
  137.7 30.7 %copy-start.17 = (bf16[2,352,2048]{2,1,0:T(8,128)(2,1)S(1)}, bf16[2,352,2048]{2,1,0:T(8,128)(2,1)}, u32[]{:S(2)}) copy-start(bf16[2,352,2048]{2,1,0:T(8,128)(2,1)} %param.25) | copy-start | bytes 8650756
  137.7 125.0 %reduce-scatter.3.cloned.1.call-start = ((), (), s32[]{:S(2)}) async-start(), calls=%async_computation.9 | async-start | bytes 5242880 | tf_op jit(solution)/shard_map/reduce_scatter | solution.py:243
  177.4 35.8 %copy-start.16 = (bf16[2,2048,352]{1,2,0:T(8,128)(2,1)S(1)}, bf16[2,2048,352]{1,2,0:T(8,128)(2,1)}, u32[]{:S(2)}) copy-start(bf16[2,2048,352]{1,2,0:T(8,128)(2,1)} %param.23) | copy-start | bytes 8650756
  177.4 134.1 %reduce-scatter.5.cloned.1.call-start = ((), (), s32[]{:S(2)}) async-start(), calls=%async_computation.11 | async-start | bytes 5242880 | tf_op jit(solution)/shard_map/reduce_scatter | solution.py:243
  227.6 91.5 %copy-start.13 = (f32[64,6]{0,1:T(8,128)S(1)}, f32[64,6]{0,1:T(8,128)}, u32[]{:S(2)}) copy-start(f32[64,6]{0,1:T(8,128)} %param.22) | copy-start | bytes 4612
  262.6 48.8 %all-to-all-start.2 = ((bf16[32,8,2048]{2,1,0:T(8,128)(2,1)}), bf16[32,8,2048]{2,1,0:T(8,128)(2,1)}, u32[]{:S(2)}, u32[]{:S(2)}) async-start(bf16[32,8,2048]{2,1,0:T(8,128)(2,1)} %reduce-scatter.3.cloned.1.call-done), calls=%async_computation.3 | async-start | bytes 2097152 | tf_op jit(solution)/shard_map/all_to_all | solution.py:244
  270.0 68.6 %copy-start.1 = (bf16[192,32,256]{2,1,0:T(8,128)(2,1)S(1)}, bf16[192,32,256]{2,1,0:T(8,128)(2,1)}, u32[]{:S(2)}) copy-start(bf16[192,32,256]{2,1,0:T(8,128)(2,1)} %param.13) | copy-start | bytes 9437188
  311.5 24.1 %all-to-all-start.4 = ((bf16[32,8,2048]{2,1,0:T(8,128)(2,1)}), bf16[32,8,2048]{2,1,0:T(8,128)(2,1)}, u32[]{:S(2)}, u32[]{:S(2)}) async-start(bf16[32,8,2048]{2,1,0:T(8,128)(2,1)} %reduce-scatter.5.cloned.1.call-done), calls=%async_computation.6 | async-start | bytes 2097152 | tf_op jit(solution)/shard_map/all_to_all | solution.py:244
  (12 other events, 94.0 us)
Sparse Core Ops, SparseCore 0:
  9.6 55.3 all-gather.3
  117.0 45.8 all-gather.5
  164.6 48.5 all-gather.7
  215.4 47.1 reduce-scatter.2
  264.9 46.5 reduce-scatter.4

commit v10 on v8

--- a/solution.py
+++ b/solution.py
@@ -230,9 +230,17 @@
     slot_ids = jnp.arange(tensor_size * capacity, dtype=jnp.int32)
     flat_gates = route_gates.reshape(-1)
     for k in range(experts_here):
-        fanned = jnp.broadcast_to(outgoing_rows[None, :, k], (group_count,) + outgoing_rows[:, k].shape)
-        fanned = fanned.reshape((group_count * tensor_size, capacity, width))
-        arrived_rows = lax.all_to_all(fanned, ("dp", "tensor"), split_axis=0, concat_axis=0, tiled=True)
+        if k == 0:
+            fanned = jnp.broadcast_to(outgoing_rows[None, :, k], (group_count,) + outgoing_rows[:, k].shape)
+            fanned = fanned.reshape((group_count * tensor_size, capacity, width))
+            arrived_rows = lax.all_to_all(
+                fanned, ("dp", "tensor"), split_axis=0, concat_axis=0, tiled=True
+            )
+        else:
+            same_group = lax.all_to_all(
+                outgoing_rows[:, k], "tensor", split_axis=0, concat_axis=0, tiled=True
+            )
+            arrived_rows = lax.all_gather(same_group, "dp", axis=0, tiled=True)
         flat_rows = arrived_rows.reshape(-1, width)
         gate_part = jnp.dot(flat_rows, expert_gate[k], preferred_element_type=jnp.float32)
         up_part = jnp.dot(flat_rows, expert_up[k], preferred_element_type=jnp.float32)

time: 341 us -> 339 us (level)
  waiting for transfers between devices: 85.6 us -> 104 us
  blocking collectives: 122 us -> 109 us
  starting transfers between devices: 33.7 us -> 26.4 us
  matrix products: 33.8 us -> 37.4 us
    all_to_all x2 -> x1, blocking collectives: 122 us -> 63.7 us  [shards(): lax.all_to_all(fanned, ('dp', 'tensor'), split_axis=0, concat_axis=0, til...]
    all_to_all x0 -> x2, blocking collectives: none -> 44.8 us  [the longest x1 24.4 us: shards(): lax.all_to_all(reduced, 'tensor', split_axis=0, concat_axis=0, tiled=True)]
    all_gather x0 -> x1, waiting for transfers between devices: none -> 9.52 us  [shards(): arrived_rows = lax.all_gather(same_group, 'dp', axis=0, tiled=True)]
    reduce_scatter x2, waiting for transfers between devices: 51.1 us -> 60 us  [shards(): lax.psum_scatter(partial_value, 'dp', scatter_dimension=0, tiled=True)]
    all_to_all x2 -> x1, starting transfers between devices: 15 us -> 7.36 us  [shards(): lax.all_to_all(reduced, 'tensor', split_axis=0, concat_axis=0, tiled=True)]
    all_to_all x2 -> x1, waiting for transfers between devices: 13.5 us -> 13.5 us  [shards(): lax.all_to_all(reduced, 'tensor', split_axis=0, concat_axis=0, tiled=True)]
  transfers between devices with their start and end apart: 16 -> 16, of which waited for: 8 -> 9; matrix products, arithmetic and copies ran while one was open for 13% -> 17% of each run, Pallas kernels for 4% -> 4%
where the time goes in v10:
time: 339 us; the launch traced here: 337 us
  blocking collectives  109 us (32%)
  waiting for transfers between devices  104 us (31%)
  matrix products  37.4 us (11%)
  starting transfers between devices  26.4 us (8%)
  local copies, waits for them, and re-layouts  21.9 us (6%)
  Pallas kernels  14 us (4%)
  between operations  13.6 us (4%)
  other arithmetic  11.5 us (3%)
    all_to_all x1, blocking collectives, shards(): lax.all_to_all(fanned, ('dp', 'tensor'), split_axis=0, concat_axis=0, til...  63.7 us
    reduce_scatter x2, waiting for transfers between devices, shards(): lax.psum_scatter(partial_value, 'dp', scatter_dimension=0, tiled=True)  60 us
    all_to_all x1, blocking collectives, shards(): lax.all_to_all(reduced, 'tensor', split_axis=0, concat_axis=0, tiled=True)  24.4 us
    all_to_all x1, blocking collectives, shards(): lax.all_to_all(outgoing_rows[:, k], 'tensor', split_axis=0, concat_axis=0...  20.4 us
    dot_general x2, matrix products, shards(): jnp.dot(active, expert_down[k], preferred_element_type=jnp.float32)  18.9 us
    pallas_call x1, Pallas kernels, attention_kernel(): pl.pallas_call(body, grid_spec=grid_spec, out_shape=[jax.ShapeDtypeStruct...  14 us
    all_to_all x1, waiting for transfers between devices, shards(): lax.all_to_all(reduced, 'tensor', split_axis=0, concat_axis=0, tiled=True)  13.5 us
    all_gather x1, waiting for transfers between devices, shards(): arrived_rows = lax.all_gather(same_group, 'dp', axis=0, tiled=True)  9.52 us
  transfers between devices with their start and end apart: 16, of which 9 were waited for; matrix products, arithmetic and copies ran while one was open for 17% of the time, Pallas kernels for 4%

profile of v10, /device:TPU:0, one launch (start us, length us, event | category | flops | bytes accessed | tf_op | source)
XLA Modules:
  0.0 337.4 jit_solution(15697814622701547774)
XLA Ops:
  9.5 2.8 gather_fusion.1
  17.5 2.1 collective-permute-start.1
  24.2 3.8 %collective-permute-done.1 = bf16[256,384]{1,0:T(8,128)(2,1)} collective-permute-done((bf16[256,384]{1,0:T(8,128)(2,1)}, bf16[256,384]{1,0:T(8,128)(2,1)}, u32[]{:S(2)}, u32[]{:S(2)}) %collective-permute-start.1) | collective-permute-done | bytes 196640 | tf_op jit(solution)/shard_map/ppermute | solution.py:156
  30.9 2.8 gather_fusion.3
  35.6 14.0 %shard_map.127 = (f32[4,512,64]{2,1,0:T(8,128)}, f32[4,512,64]{2,1,0:T(8,128)}, f32[4,1,512]{2,1,0:T(1,128)}, f32[4,1,512]{2,1,0:T(1,128)}) custom-call(s32[6]{0:T(128)} %pad_add_fusion.scal_ref, bf16[4,512,128]{2,1,0:T(8,128)(2,1)} %pad_maximum_fusion.1.q_ref, bf16[4,2048,256]{2,1,0:T(8,128)(2,1)} %bitcast.144, bf16[4,256,384]{2,1,0:T(8,128)(2,1)} %copy-done.3), custom_call_target="tpu_custom_call" | custom-call | tf_op jit(solution)/shard_map/pallas_call | solution.py:79
  61.5 5.9 %collective-permute-done.7 = bf16[512,64]{1,0:T(8,128)(2,1)S(1)} collective-permute-done((bf16[512,64]{1,0:T(8,128)(2,1)S(1)}, bf16[512,64]{1,0:T(8,128)(2,1)S(1)}, u32[]{:S(2)}, u32[]{:S(2)}) %collective-permute-start.7) | collective-permute-done | bytes 65568 | tf_op jit(solution)/shard_map/ppermute | solution.py:194
  69.8 8.0 %all-to-all-start = ((bf16[32,2,2048]{2,1,0:T(2,128)(2,1)}), bf16[32,2,2048]{2,1,0:T(2,128)(2,1)S(1)}, u32[]{:S(2)}, u32[]{:S(2)}) async-start(bf16[32,2,2048]{2,1,0:T(2,128)(2,1)} %reshape.391), calls=%async_computation | async-start | bytes 524288 | tf_op jit(solution)/shard_map/all_to_all | solution.py:199
  78.2 8.7 %all-to-all-done = bf16[32,2,2048]{2,1,0:T(2,128)(2,1)S(1)} async-done(((bf16[32,2,2048]{2,1,0:T(2,128)(2,1)}), bf16[32,2,2048]{2,1,0:T(2,128)(2,1)S(1)}, u32[]{:S(2)}, u32[]{:S(2)}) %all-to-all-start) | async-done | bytes 262176 | tf_op jit(solution)/shard_map/all_to_all | solution.py:199
  88.0 5.1 %multiply_reduce_fusion = (f32[64]{0:T(128)S(1)}, f32[64,2048]{1,0:T(8,128)S(1)}) fusion(bf16[64,2048]{1,0:T(8,128)(2,1)S(1)} %reshape.319, bf16[2048,2048]{1,0:T(8,128)(2,1)} %all-gather.3.cloned.1.call-done, bf16[64,2048]{1,0:T(8,128)(2,1)S(1)} %copy-done.8), kind=kOutput, calls=%fused_computation.52 | convolution fusion | flops 537395136 | bytes 9437440 | tf_op jit(solution)/shard_map/dot_general | solution.py:202
  93.3 2.5 gather_fusion.5
  96.1 20.4 %all_to_all.25 = bf16[32,8,2048]{2,1,0:T(8,128)(2,1)} all-to-all(bf16[32,8,2048]{2,1,0:T(8,128)(2,1)S(1)} %get-tuple-element.20), channel_id=1, replica_groups=mesh['dp'=4,'tensor'=32] {'tensor'}, dimensions={0} | all-to-all | bytes 2097152 | tf_op jit(solution)/shard_map/all_to_all | solution.py:240
  117.1 63.7 %all_to_all.26 = bf16[128,8,2048]{2,1,0:T(8,128)(2,1)S(1)} all-to-all(bf16[128,8,2048]{2,1,0:T(8,128)(2,1)S(1)} %bitcast.145), channel_id=1, replica_groups=mesh['dp'=4,'tensor'=32] {'dp','tensor'}, dimensions={0} | all-to-all | bytes 8388608 | tf_op jit(solution)/shard_map/all_to_all | solution.py:236
  182.9 2.8 fusion.6
  185.7 9.5 %convert_bitcast_fusion.1 = bf16[128,8,2048]{2,1,0:T(8,128)(2,1)} fusion(bf16[2,352,2048]{2,1,0:T(8,128)(2,1)} %param.25, bf16[2,2048,352]{1,2,0:T(8,128)(2,1)} %param.24, bf16[128,8,2048]{2,1,0:T(8,128)(2,1)} %copy-done.5, f32[1024,352]{0,1:T(8,128)} %fusion.6), kind=kOutput, calls=%fused_computation.16 | convolution fusion | flops 2957049856 | bytes 12713984 | tf_op jit(solution)/shard_map/dot_general | solution.py:248
  195.4 9.5 %all-gather.5.cloned.1.call-done = bf16[128,8,2048]{2,1,0:T(8,128)(2,1)} async-done(((bf16[32,8,2048]{2,1,0:T(8,128)(2,1)}), bf16[128,8,2048]{2,1,0:T(8,128)(2,1)}) %all-gather.5.cloned.1.call-update) | async-done | bytes 4194320 | tf_op jit(solution)/shard_map/all_gather | solution.py:243
  205.0 5.0 %fusion.2 = f32[1024,352]{0,1:T(8,128)} fusion(bf16[128,8,2048]{2,1,0:T(8,128)(2,1)} %all-gather.5.cloned.1.call-done, bf16[2,2048,352]{1,2,0:T(8,128)(2,1)S(1)} %copy-done.17), kind=kOutput, calls=%fused_computation.9 | convolution fusion | flops 1476395008 | bytes 7077888 | tf_op jit(solution)/shard_map/dot_general | solution.py:245
  210.0 9.4 %convert_bitcast_fusion = bf16[128,8,2048]{2,1,0:T(8,128)(2,1)} fusion(bf16[2,352,2048]{2,1,0:T(8,128)(2,1)} %param.25, bf16[2,2048,352]{1,2,0:T(8,128)(2,1)} %param.24, bf16[128,8,2048]{2,1,0:T(8,128)(2,1)} %all-gather.5.cloned.1.call-done, f32[1024,352]{0,1:T(8,128)} %fusion.2), kind=kOutput, calls=%fused_computation.15 | convolution fusion | flops 2957049856 | bytes 12713984 | tf_op jit(solution)/shard_map/dot_general | solution.py:248
  219.4 35.5 %reduce-scatter.3.cloned.1.call-done = bf16[32,8,2048]{2,1,0:T(8,128)(2,1)} async-done(((bf16[128,8,2048]{2,1,0:T(8,128)(2,1)}), bf16[32,8,2048]{2,1,0:T(8,128)(2,1)}) %reduce-scatter.3.cloned.1.call-update) | async-done | bytes 1048592 | tf_op jit(solution)/shard_map/reduce_scatter | solution.py:250
  254.9 24.4 %all_to_all.27 = bf16[32,8,2048]{2,1,0:T(8,128)(2,1)} all-to-all(bf16[32,8,2048]{2,1,0:T(8,128)(2,1)} %reduce-scatter.3.cloned.1.call-done), channel_id=1, replica_groups=mesh['dp'=4,'tensor'=32] {'tensor'}, dimensions={0} | all-to-all | bytes 2097152 | tf_op jit(solution)/shard_map/all_to_all | solution.py:251
  279.3 24.5 %reduce-scatter.5.cloned.1.call-done = bf16[32,8,2048]{2,1,0:T(8,128)(2,1)} async-done(((bf16[128,8,2048]{2,1,0:T(8,128)(2,1)}), bf16[32,8,2048]{2,1,0:T(8,128)(2,1)}) %reduce-scatter.5.cloned.1.call-update) | async-done | bytes 1048592 | tf_op jit(solution)/shard_map/reduce_scatter | solution.py:250
  303.8 7.4 %all-to-all-start.4 = ((bf16[32,8,2048]{2,1,0:T(8,128)(2,1)}), bf16[32,8,2048]{2,1,0:T(8,128)(2,1)}, u32[]{:S(2)}, u32[]{:S(2)}) async-start(bf16[32,8,2048]{2,1,0:T(8,128)(2,1)} %reduce-scatter.5.cloned.1.call-done), calls=%async_computation.6 | async-start | bytes 2097152 | tf_op jit(solution)/shard_map/all_to_all | solution.py:251
  311.7 2.7 fusion.38
  314.4 13.5 %all-to-all-done.4 = bf16[32,8,2048]{2,1,0:T(8,128)(2,1)} async-done(((bf16[32,8,2048]{2,1,0:T(8,128)(2,1)}), bf16[32,8,2048]{2,1,0:T(8,128)(2,1)}, u32[]{:S(2)}, u32[]{:S(2)}) %all-to-all-start.4) | async-done | bytes 1048608 | tf_op jit(solution)/shard_map/all_to_all | solution.py:251
  327.9 3.0 fusion.8
  (127 shorter events, 36.9 us)
Async XLA Ops:
  6.5 24.4 %copy-start = (bf16[192,32,256]{2,1,0:T(8,128)(2,1)S(1)}, bf16[192,32,256]{2,1,0:T(8,128)(2,1)}, u32[]{:S(2)}) copy-start(bf16[192,32,256]{2,1,0:T(8,128)(2,1)} %param.13) | copy-start | bytes 9437188
  6.5 13.4 %copy-start.16 = (s32[16]{0:T(128)S(1)}, s32[16]{0:T(128)}, u32[]{:S(2)}) copy-start(s32[16]{0:T(128)} %param.15) | copy-start | bytes 196
  6.5 14.2 %copy-start.9 = (s32[4,64]{1,0:T(4,128)S(1)}, s32[4,64]{1,0:T(4,128)}, u32[]{:S(2)}) copy-start(s32[4,64]{1,0:T(4,128)} %param.14) | copy-start | bytes 3076
  6.5 16.7 %copy-start.2 = (s32[16]{0:T(128)S(1)}, s32[16]{0:T(128)}, u32[]{:S(2)}) copy-start(s32[16]{0:T(128)} %param.16) | copy-start | bytes 196
  6.5 81.5 %all-gather.3.cloned.1.call-start = ((), (), s32[]{:S(2)}) async-start(), calls=%async_computation.7 | async-start | bytes 8650752 | tf_op jit(solution)/shard_map/all_gather | solution.py:201
  14.2 9.9 %collective-permute-start.2 = (bf16[256,384]{1,0:T(8,128)(2,1)}, bf16[256,384]{1,0:T(8,128)(2,1)}, u32[]{:S(2)}, u32[]{:S(2)}) collective-permute-start(bf16[256,384]{1,0:T(8,128)(2,1)} %get-tuple-element.27), channel_id=1, source_target_pairs={{0,32},{32,64},{64,96},{96,0},{1,33},{33,65},{65,97},{97,1},{2,34}... | collective-permute-start | bytes 589832 | tf_op jit(solution)/shard_map/ppermute | solution.py:156
  15.9 8.2 %collective-permute-start = (bf16[256,384]{1,0:T(8,128)(2,1)}, bf16[256,384]{1,0:T(8,128)(2,1)}, u32[]{:S(2)}, u32[]{:S(2)}) collective-permute-start(bf16[256,384]{1,0:T(8,128)(2,1)} %get-tuple-element.26), channel_id=1, source_target_pairs={{0,96},{32,0},{64,32},{96,64},{1,97},{33,1},{65,33},{97,65},{2,98}... | collective-permute-start | bytes 589832 | tf_op jit(solution)/shard_map/ppermute | solution.py:156
  17.5 10.5 %collective-permute-start.1 = (bf16[256,384]{1,0:T(8,128)(2,1)}, bf16[256,384]{1,0:T(8,128)(2,1)}, u32[]{:S(2)}, u32[]{:S(2)}) collective-permute-start(bf16[256,384]{1,0:T(8,128)(2,1)} %get-tuple-element.25), channel_id=1, source_target_pairs={{0,64},{32,96},{64,0},{96,32},{1,65},{33,97},{65,1},{97,33},{2,66}... | collective-permute-start | bytes 589832 | tf_op jit(solution)/shard_map/ppermute | solution.py:156
  30.2 3.5 %collective-permute-start.3 = (bf16[4,256,128]{2,1,0:T(8,128)(2,1)S(1)}, bf16[4,256,128]{2,1,0:T(8,128)(2,1)}, u32[]{:S(2)}, u32[]{:S(2)}) collective-permute-start(bf16[4,256,128]{2,1,0:T(8,128)(2,1)S(1)} %slice.92), channel_id=1, source_target_pairs={{0,1},{1,0},{2,3},{3,2},{4,5},{5,4},{6,7},{7,6},{8,9},{9,8},{10,11... | collective-permute-start | bytes 786440 | tf_op jit(solution)/shard_map/ppermute | solution.py:18
  52.4 2.9 collective-permute-start.5
  53.1 2.1 collective-permute-start.4
  53.3 2.0 collective-permute-start.6
  57.7 9.6 %collective-permute-start.7 = (bf16[512,64]{1,0:T(8,128)(2,1)S(1)}, bf16[512,64]{1,0:T(8,128)(2,1)S(1)}, u32[]{:S(2)}, u32[]{:S(2)}) collective-permute-start(bf16[512,64]{1,0:T(8,128)(2,1)S(1)} %get-tuple-element.31), channel_id=1, source_target_pairs={{0,32},{32,64},{64,96},{96,0},{1,33},{33,65},{65,97},{97,1},{2,34}... | collective-permute-start | bytes 196616 | tf_op jit(solution)/shard_map/ppermute | solution.py:194
  58.7 8.7 %collective-permute-start.8 = (bf16[512,64]{1,0:T(8,128)(2,1)S(1)}, bf16[512,64]{1,0:T(8,128)(2,1)S(1)}, u32[]{:S(2)}, u32[]{:S(2)}) collective-permute-start(bf16[512,64]{1,0:T(8,128)(2,1)S(1)} %get-tuple-element.30), channel_id=1, source_target_pairs={{0,64},{32,96},{64,0},{96,32},{1,65},{33,97},{65,1},{97,33},{2,66}... | collective-permute-start | bytes 196616 | tf_op jit(solution)/shard_map/ppermute | solution.py:194
  60.7 7.2 %collective-permute-start.9 = (bf16[512,64]{1,0:T(8,128)(2,1)S(1)}, bf16[512,64]{1,0:T(8,128)(2,1)S(1)}, u32[]{:S(2)}, u32[]{:S(2)}) collective-permute-start(bf16[512,64]{1,0:T(8,128)(2,1)S(1)} %get-tuple-element.29), channel_id=1, source_target_pairs={{0,96},{32,0},{64,32},{96,64},{1,97},{33,1},{65,33},{97,65},{2,98}... | collective-permute-start | bytes 196616 | tf_op jit(solution)/shard_map/ppermute | solution.py:194
  67.9 20.1 %copy-start.8 = (bf16[64,2048]{1,0:T(8,128)(2,1)S(1)}, bf16[64,2048]{1,0:T(8,128)(2,1)}, u32[]{:S(2)}) copy-start(bf16[64,2048]{1,0:T(8,128)(2,1)} %param.18) | copy-start | bytes 786436
  69.8 17.0 %all-to-all-start = ((bf16[32,2,2048]{2,1,0:T(2,128)(2,1)}), bf16[32,2,2048]{2,1,0:T(2,128)(2,1)S(1)}, u32[]{:S(2)}, u32[]{:S(2)}) async-start(bf16[32,2,2048]{2,1,0:T(2,128)(2,1)} %reshape.391), calls=%async_computation | async-start | bytes 524288 | tf_op jit(solution)/shard_map/all_to_all | solution.py:199
  77.9 127.1 %all-gather.5.cloned.1.call-start = ((), (), s32[]{:S(2)}) async-start(), calls=%async_computation.9 | async-start | bytes 5242880 | tf_op jit(solution)/shard_map/all_gather | solution.py:243
  116.6 138.4 %reduce-scatter.3.cloned.1.call-start = ((), (), s32[]{:S(2)}) async-start(), calls=%async_computation.8 | async-start | bytes 5242880 | tf_op jit(solution)/shard_map/reduce_scatter | solution.py:250
  117.1 65.7 %copy-start.17 = (bf16[2,2048,352]{1,2,0:T(8,128)(2,1)S(1)}, bf16[2,2048,352]{1,2,0:T(8,128)(2,1)}, u32[]{:S(2)}) copy-start(bf16[2,2048,352]{1,2,0:T(8,128)(2,1)} %param.23) | copy-start | bytes 8650756
  195.2 108.6 %reduce-scatter.5.cloned.1.call-start = ((), (), s32[]{:S(2)}) async-start(), calls=%async_computation.10 | async-start | bytes 5242880 | tf_op jit(solution)/shard_map/reduce_scatter | solution.py:250
  219.4 92.0 %copy-start.14 = (f32[64,6]{0,1:T(8,128)S(1)}, f32[64,6]{0,1:T(8,128)}, u32[]{:S(2)}) copy-start(f32[64,6]{0,1:T(8,128)} %param.22) | copy-start | bytes 4612
  254.9 76.0 %copy-start.1 = (bf16[192,32,256]{2,1,0:T(8,128)(2,1)S(1)}, bf16[192,32,256]{2,1,0:T(8,128)(2,1)}, u32[]{:S(2)}) copy-start(bf16[192,32,256]{2,1,0:T(8,128)(2,1)} %param.13) | copy-start | bytes 9437188
  303.8 24.1 %all-to-all-start.4 = ((bf16[32,8,2048]{2,1,0:T(8,128)(2,1)}), bf16[32,8,2048]{2,1,0:T(8,128)(2,1)}, u32[]{:S(2)}, u32[]{:S(2)}) async-start(bf16[32,8,2048]{2,1,0:T(8,128)(2,1)} %reduce-scatter.5.cloned.1.call-done), calls=%async_computation.6 | async-start | bytes 2097152 | tf_op jit(solution)/shard_map/all_to_all | solution.py:251
  (10 other events, 51.2 us)
Sparse Core Ops, SparseCore 0:
  9.6 55.3 all-gather.2
  116.7 88.2 all-gather.4
  207.4 47.4 reduce-scatter.2
  257.2 46.5 reduce-scatter.4

commit v11 on v10

--- a/solution.py
+++ b/solution.py
@@ -247,10 +247,16 @@
         active = (jax.nn.silu(gate_part) * up_part).astype(jnp.bfloat16)
         partial_value = jnp.dot(active, expert_down[k], preferred_element_type=jnp.float32)
         partial_value = partial_value.astype(jnp.bfloat16).reshape(arrived_rows.shape)
-        reduced = lax.psum_scatter(partial_value, "dp", scatter_dimension=0, tiled=True)
-        returned = lax.all_to_all(reduced, "tensor", split_axis=0, concat_axis=0, tiled=True)
         hit = (owner_slot[:, None] == slot_ids[None, :]) & (parity == k)[:, None]
         coeff = jnp.where(hit, flat_gates[:, None], 0.0).reshape(tok_rows, TOP, -1).sum(axis=1)
+        if k == 0:
+            returned = lax.all_to_all(
+                partial_value, ("dp", "tensor"), split_axis=0, concat_axis=0, tiled=True
+            )
+            coeff = jnp.tile(coeff, (1, group_count))
+        else:
+            reduced = lax.psum_scatter(partial_value, "dp", scatter_dimension=0, tiled=True)
+            returned = lax.all_to_all(reduced, "tensor", split_axis=0, concat_axis=0, tiled=True)
         routed = routed + jnp.dot(
             coeff,
             returned.reshape(-1, width).astype(jnp.float32),

time: 339 us -> 364 us (1.074)
  waiting for transfers between devices: 104 us -> 144 us
  blocking collectives: 109 us -> 88.6 us
  starting transfers between devices: 26.4 us -> 33.5 us
    all_to_all x0 -> x1, waiting for transfers between devices: none -> 50.4 us  [shards(): lax.all_to_all(partial_value, ('dp', 'tensor'), split_axis=0, concat_axis...]
    reduce_scatter x2 -> x1, waiting for transfers between devices: 60 us -> 23.7 us  [shards(): lax.psum_scatter(partial_value, 'dp', scatter_dimension=0, tiled=True)]
    all_gather x1, waiting for transfers between devices: 9.52 us -> 44.7 us  [shards(): arrived_rows = lax.all_gather(same_group, 'dp', axis=0, tiled=True)]
    all_to_all x1 -> x0, blocking collectives: 24.4 us -> none  [shards(): lax.all_to_all(reduced, 'tensor', split_axis=0, concat_axis=0, tiled=True)]
    all_to_all x1, waiting for transfers between devices: 13.5 us -> 3.26 us  [shards(): lax.all_to_all(reduced, 'tensor', split_axis=0, concat_axis=0, tiled=True)]
    all_to_all x0 -> x1, starting transfers between devices: none -> 5.82 us  [shards(): lax.all_to_all(partial_value, ('dp', 'tensor'), split_axis=0, concat_axis...]
    all_to_all x1, blocking collectives: 63.7 us -> 68.1 us  [shards(): lax.all_to_all(fanned, ('dp', 'tensor'), split_axis=0, concat_axis=0, til...]
  transfers between devices with their start and end apart: 16 -> 16, of which waited for: 9 -> 10; matrix products, arithmetic and copies ran while one was open for 17% -> 12% of each run, Pallas kernels for 4% -> 4%
where the time goes in v11:
time: 364 us
  waiting for transfers between devices  144 us (40%)
  blocking collectives  88.6 us (24%)
  matrix products  38.9 us (11%)
  starting transfers between devices  33.5 us (9%)
  local copies, waits for them, and re-layouts  20 us (5%)
  Pallas kernels  14 us (4%)
  between operations  13.6 us (4%)
  other arithmetic  11.5 us (3%)
    all_to_all x1, blocking collectives, shards(): lax.all_to_all(fanned, ('dp', 'tensor'), split_axis=0, concat_axis=0, til...  68.1 us
    all_to_all x1, waiting for transfers between devices, shards(): lax.all_to_all(partial_value, ('dp', 'tensor'), split_axis=0, concat_axis...  50.4 us
    all_gather x1, waiting for transfers between devices, shards(): arrived_rows = lax.all_gather(same_group, 'dp', axis=0, tiled=True)  44.7 us
    reduce_scatter x1, waiting for transfers between devices, shards(): lax.psum_scatter(partial_value, 'dp', scatter_dimension=0, tiled=True)  23.7 us
    all_to_all x1, blocking collectives, shards(): lax.all_to_all(outgoing_rows[:, k], 'tensor', split_axis=0, concat_axis=0...  20.4 us
    dot_general x2, matrix products, shards(): jnp.dot(active, expert_down[k], preferred_element_type=jnp.float32)  18 us
    pallas_call x1, Pallas kernels, attention_kernel(): pl.pallas_call(body, grid_spec=grid_spec, out_shape=[jax.ShapeDtypeStruct...  14 us
    all_to_all x1, waiting for transfers between devices, shards(): lax.all_to_all(head_out, 'tensor', split_axis=0, concat_axis=0, tiled=True)  8.65 us
  transfers between devices with their start and end apart: 16, of which 10 were waited for; matrix products, arithmetic and copies ran while one was open for 12% of the time, Pallas kernels for 4%

profile of v11, /device:TPU:0, one launch (start us, length us, event | category | flops | bytes accessed | tf_op | source)
XLA Modules:
  0.0 363.7 jit_solution(1295817773311875410)
XLA Ops:
  9.5 2.8 gather_fusion.1
  15.9 2.9 collective-permute-start.1
  24.8 3.2 collective-permute-done.1
  30.9 2.8 gather_fusion.3
  35.6 14.0 %shard_map.127 = (f32[4,512,64]{2,1,0:T(8,128)}, f32[4,512,64]{2,1,0:T(8,128)}, f32[4,1,512]{2,1,0:T(1,128)}, f32[4,1,512]{2,1,0:T(1,128)}) custom-call(s32[6]{0:T(128)} %pad_add_fusion.scal_ref, bf16[4,512,128]{2,1,0:T(8,128)(2,1)} %pad_maximum_fusion.1.q_ref, bf16[4,2048,256]{2,1,0:T(8,128)(2,1)} %bitcast.150, bf16[4,256,384]{2,1,0:T(8,128)(2,1)} %copy-done.3), custom_call_target="tpu_custom_call" | custom-call | tf_op jit(solution)/shard_map/pallas_call | solution.py:79
  57.6 2.0 collective-permute-start.9
  61.6 4.2 %collective-permute-done.9 = bf16[512,64]{1,0:T(8,128)(2,1)S(1)} collective-permute-done((bf16[512,64]{1,0:T(8,128)(2,1)S(1)}, bf16[512,64]{1,0:T(8,128)(2,1)S(1)}, u32[]{:S(2)}, u32[]{:S(2)}) %collective-permute-start.9) | collective-permute-done | bytes 65568 | tf_op jit(solution)/shard_map/ppermute | solution.py:194
  71.3 8.2 %all-to-all-start = ((bf16[32,2,2048]{2,1,0:T(2,128)(2,1)}), bf16[32,2,2048]{2,1,0:T(2,128)(2,1)S(1)}, u32[]{:S(2)}, u32[]{:S(2)}) async-start(bf16[32,2,2048]{2,1,0:T(2,128)(2,1)} %reshape.395), calls=%async_computation | async-start | bytes 524288 | tf_op jit(solution)/shard_map/all_to_all | solution.py:199
  79.8 8.7 %all-to-all-done = bf16[32,2,2048]{2,1,0:T(2,128)(2,1)S(1)} async-done(((bf16[32,2,2048]{2,1,0:T(2,128)(2,1)}), bf16[32,2,2048]{2,1,0:T(2,128)(2,1)S(1)}, u32[]{:S(2)}, u32[]{:S(2)}) %all-to-all-start) | async-done | bytes 262176 | tf_op jit(solution)/shard_map/all_to_all | solution.py:199
  89.6 5.1 %multiply_reduce_fusion = (f32[64]{0:T(128)S(1)}, f32[64,2048]{1,0:T(8,128)S(1)}) fusion(bf16[64,2048]{1,0:T(8,128)(2,1)S(1)} %reshape.323, bf16[2048,2048]{1,0:T(8,128)(2,1)} %all-gather.3.cloned.1.call-done, bf16[64,2048]{1,0:T(8,128)(2,1)S(1)} %copy-done.7), kind=kOutput, calls=%fused_computation.53 | convolution fusion | flops 537395136 | bytes 9437440 | tf_op jit(solution)/shard_map/dot_general | solution.py:202
  94.9 2.5 gather_fusion.5
  97.7 20.4 %all_to_all.25 = bf16[32,8,2048]{2,1,0:T(8,128)(2,1)} all-to-all(bf16[32,8,2048]{2,1,0:T(8,128)(2,1)S(1)} %get-tuple-element.21), channel_id=1, replica_groups=mesh['dp'=4,'tensor'=32] {'tensor'}, dimensions={0} | all-to-all | bytes 2097152 | tf_op jit(solution)/shard_map/all_to_all | solution.py:240
  118.2 44.7 %all-gather.5.cloned.1.call-done = bf16[128,8,2048]{2,1,0:T(8,128)(2,1)} async-done(((bf16[32,8,2048]{2,1,0:T(8,128)(2,1)}), bf16[128,8,2048]{2,1,0:T(8,128)(2,1)}) %all-gather.5.cloned.1.call-update) | async-done | bytes 4194320 | tf_op jit(solution)/shard_map/all_gather | solution.py:243
  162.9 4.3 %fusion.2 = f32[1024,352]{0,1:T(8,128)S(1)} fusion(bf16[128,8,2048]{2,1,0:T(8,128)(2,1)} %all-gather.5.cloned.1.call-done, bf16[2,2048,352]{1,2,0:T(8,128)(2,1)} %param.23), kind=kOutput, calls=%fused_computation.9 | convolution fusion | flops 1476395008 | bytes 7077888 | tf_op jit(solution)/shard_map/dot_general | solution.py:245
  167.2 9.0 %convert_bitcast_fusion = bf16[128,8,2048]{2,1,0:T(8,128)(2,1)} fusion(bf16[2,352,2048]{2,1,0:T(8,128)(2,1)} %param.25, bf16[2,2048,352]{1,2,0:T(8,128)(2,1)} %param.24, bf16[128,8,2048]{2,1,0:T(8,128)(2,1)} %all-gather.5.cloned.1.call-done, f32[1024,352]{0,1:T(8,128)S(1)} %fusion.2), kind=kOutput, calls=%fused_computation.17 | convolution fusion | flops 2957049856 | bytes 12713984 | tf_op jit(solution)/shard_map/dot_general | solution.py:248
  176.7 68.1 %all_to_all.26 = bf16[128,8,2048]{2,1,0:T(8,128)(2,1)} all-to-all(bf16[128,8,2048]{2,1,0:T(8,128)(2,1)S(1)} %bitcast.151), channel_id=1, replica_groups=mesh['dp'=4,'tensor'=32] {'dp','tensor'}, dimensions={0} | all-to-all | bytes 8388608 | tf_op jit(solution)/shard_map/all_to_all | solution.py:236
  244.8 23.7 %reduce-scatter.2.cloned.1.call-done = bf16[32,8,2048]{2,1,0:T(8,128)(2,1)} async-done(((bf16[128,8,2048]{2,1,0:T(8,128)(2,1)}), bf16[32,8,2048]{2,1,0:T(8,128)(2,1)}) %reduce-scatter.2.cloned.1.call-update) | async-done | bytes 1048592 | tf_op jit(solution)/shard_map/reduce_scatter | solution.py:258
  268.5 8.0 %all-to-all-start.4 = ((bf16[32,8,2048]{2,1,0:T(8,128)(2,1)}), bf16[32,8,2048]{2,1,0:T(8,128)(2,1)S(1)}, u32[]{:S(2)}, u32[]{:S(2)}) async-start(bf16[32,8,2048]{2,1,0:T(8,128)(2,1)} %reduce-scatter.2.cloned.1.call-done), calls=%async_computation.5 | async-start | bytes 2097152 | tf_op jit(solution)/shard_map/all_to_all | solution.py:259
  276.5 4.3 %fusion.8 = f32[1024,352]{0,1:T(8,128)S(1)} fusion(bf16[128,8,2048]{2,1,0:T(8,128)(2,1)} %all_to_all.26, bf16[2,2048,352]{1,2,0:T(8,128)(2,1)} %param.23), kind=kOutput, calls=%fused_computation.15 | convolution fusion | flops 1476395008 | bytes 7077888 | tf_op jit(solution)/shard_map/dot_general | solution.py:245
  280.9 9.0 %convert_bitcast_fusion.1 = bf16[128,8,2048]{2,1,0:T(8,128)(2,1)} fusion(bf16[2,352,2048]{2,1,0:T(8,128)(2,1)} %param.25, bf16[2,2048,352]{1,2,0:T(8,128)(2,1)} %param.24, bf16[128,8,2048]{2,1,0:T(8,128)(2,1)} %all_to_all.26, f32[1024,352]{0,1:T(8,128)S(1)} %fusion.8), kind=kOutput, calls=%fused_computation.18 | convolution fusion | flops 2957049856 | bytes 12713984 | tf_op jit(solution)/shard_map/dot_general | solution.py:248
  289.8 3.3 all-to-all-done.4
  293.1 5.8 %all-to-all-start.2 = ((bf16[128,8,2048]{2,1,0:T(8,128)(2,1)}), bf16[128,8,2048]{2,1,0:T(8,128)(2,1)}, u32[]{:S(2)}, u32[]{:S(2)}) async-start(bf16[128,8,2048]{2,1,0:T(8,128)(2,1)} %convert_bitcast_fusion.1), calls=%async_computation.2 | async-start | bytes 8388608 | tf_op jit(solution)/shard_map/all_to_all | solution.py:253
  301.1 50.4 %all-to-all-done.2 = bf16[128,8,2048]{2,1,0:T(8,128)(2,1)} async-done(((bf16[128,8,2048]{2,1,0:T(8,128)(2,1)}), bf16[128,8,2048]{2,1,0:T(8,128)(2,1)}, u32[]{:S(2)}, u32[]{:S(2)}) %all-to-all-start.2) | async-done | bytes 4194336 | tf_op jit(solution)/shard_map/all_to_all | solution.py:253
  351.4 5.7 %fusion.13 = f32[64,2048]{1,0:T(8,128)} fusion(f32[64,2048]{1,0:T(8,128)} %copy-done.4, f32[64,2048]{1,0:T(8,128)} %fusion.44, f32[64,1024]{1,0:T(8,128)S(1)} %bitcast.155, bf16[128,8,2048]{2,1,0:T(8,128)(2,1)} %all-to-all-done.2), kind=kOutput, calls=%fused_computation.20 | convolution fusion | flops 1610874880 | bytes 6029312 | tf_op jit(solution)/shard_map/dot_general | solution.py:260
  (123 shorter events, 37.2 us)
Async XLA Ops:
  6.5 24.4 %copy-start = (bf16[192,32,256]{2,1,0:T(8,128)(2,1)S(1)}, bf16[192,32,256]{2,1,0:T(8,128)(2,1)}, u32[]{:S(2)}) copy-start(bf16[192,32,256]{2,1,0:T(8,128)(2,1)} %param.13) | copy-start | bytes 9437188
  6.5 14.0 %copy-start.15 = (s32[16]{0:T(128)S(1)}, s32[16]{0:T(128)}, u32[]{:S(2)}) copy-start(s32[16]{0:T(128)} %param.15) | copy-start | bytes 196
  6.5 13.6 %copy-start.9 = (s32[64,6]{0,1:T(8,128)S(1)}, s32[64,6]{0,1:T(8,128)}, u32[]{:S(2)}) copy-start(s32[64,6]{0,1:T(8,128)} %param.21) | copy-start | bytes 4612
  6.5 14.8 %copy-start.8 = (s32[4,64]{1,0:T(4,128)S(1)}, s32[4,64]{1,0:T(4,128)}, u32[]{:S(2)}) copy-start(s32[4,64]{1,0:T(4,128)} %param.14) | copy-start | bytes 3076
  6.5 17.3 %copy-start.2 = (s32[16]{0:T(128)S(1)}, s32[16]{0:T(128)}, u32[]{:S(2)}) copy-start(s32[16]{0:T(128)} %param.16) | copy-start | bytes 196
  6.5 83.1 %all-gather.3.cloned.1.call-start = ((), (), s32[]{:S(2)}) async-start(), calls=%async_computation.6 | async-start | bytes 8650752 | tf_op jit(solution)/shard_map/all_gather | solution.py:201
  14.2 10.5 %collective-permute-start.2 = (bf16[256,384]{1,0:T(8,128)(2,1)}, bf16[256,384]{1,0:T(8,128)(2,1)}, u32[]{:S(2)}, u32[]{:S(2)}) collective-permute-start(bf16[256,384]{1,0:T(8,128)(2,1)} %get-tuple-element.27), channel_id=1, source_target_pairs={{0,32},{32,64},{64,96},{96,0},{1,33},{33,65},{65,97},{97,1},{2,34}... | collective-permute-start | bytes 589832 | tf_op jit(solution)/shard_map/ppermute | solution.py:156
  15.9 12.0 %collective-permute-start.1 = (bf16[256,384]{1,0:T(8,128)(2,1)}, bf16[256,384]{1,0:T(8,128)(2,1)}, u32[]{:S(2)}, u32[]{:S(2)}) collective-permute-start(bf16[256,384]{1,0:T(8,128)(2,1)} %get-tuple-element.25), channel_id=1, source_target_pairs={{0,64},{32,96},{64,0},{96,32},{1,65},{33,97},{65,1},{97,33},{2,66}... | collective-permute-start | bytes 589832 | tf_op jit(solution)/shard_map/ppermute | solution.py:156
  18.8 9.1 %collective-permute-start = (bf16[256,384]{1,0:T(8,128)(2,1)}, bf16[256,384]{1,0:T(8,128)(2,1)}, u32[]{:S(2)}, u32[]{:S(2)}) collective-permute-start(bf16[256,384]{1,0:T(8,128)(2,1)} %get-tuple-element.26), channel_id=1, source_target_pairs={{0,96},{32,0},{64,32},{96,64},{1,97},{33,1},{65,33},{97,65},{2,98}... | collective-permute-start | bytes 589832 | tf_op jit(solution)/shard_map/ppermute | solution.py:156
  30.2 3.5 collective-permute-start.3
  49.6 6.9 %copy-start.5 = (f32[4,512,64]{2,1,0:T(8,128)S(1)}, f32[4,512,64]{2,1,0:T(8,128)}, u32[]{:S(2)}) copy-start(f32[4,512,64]{2,1,0:T(8,128)} %get-tuple-element.9) | copy-start | bytes 1572868
  52.4 2.8 collective-permute-start.5
  53.0 2.1 collective-permute-start.6
  53.2 2.0 collective-permute-start.4
  57.6 8.1 %collective-permute-start.9 = (bf16[512,64]{1,0:T(8,128)(2,1)S(1)}, bf16[512,64]{1,0:T(8,128)(2,1)S(1)}, u32[]{:S(2)}, u32[]{:S(2)}) collective-permute-start(bf16[512,64]{1,0:T(8,128)(2,1)S(1)} %get-tuple-element.29), channel_id=1, source_target_pairs={{0,96},{32,0},{64,32},{96,64},{1,97},{33,1},{65,33},{97,65},{2,98}... | collective-permute-start | bytes 196616 | tf_op jit(solution)/shard_map/ppermute | solution.py:194
  59.7 7.9 %collective-permute-start.8 = (bf16[512,64]{1,0:T(8,128)(2,1)S(1)}, bf16[512,64]{1,0:T(8,128)(2,1)S(1)}, u32[]{:S(2)}, u32[]{:S(2)}) collective-permute-start(bf16[512,64]{1,0:T(8,128)(2,1)S(1)} %get-tuple-element.30), channel_id=1, source_target_pairs={{0,64},{32,96},{64,0},{96,32},{1,65},{33,97},{65,1},{97,33},{2,66}... | collective-permute-start | bytes 196616 | tf_op jit(solution)/shard_map/ppermute | solution.py:194
  60.8 8.6 %collective-permute-start.7 = (bf16[512,64]{1,0:T(8,128)(2,1)S(1)}, bf16[512,64]{1,0:T(8,128)(2,1)S(1)}, u32[]{:S(2)}, u32[]{:S(2)}) collective-permute-start(bf16[512,64]{1,0:T(8,128)(2,1)S(1)} %get-tuple-element.31), channel_id=1, source_target_pairs={{0,32},{32,64},{64,96},{96,0},{1,33},{33,65},{65,97},{97,1},{2,34}... | collective-permute-start | bytes 196616 | tf_op jit(solution)/shard_map/ppermute | solution.py:194
  69.4 20.2 %copy-start.7 = (bf16[64,2048]{1,0:T(8,128)(2,1)S(1)}, bf16[64,2048]{1,0:T(8,128)(2,1)}, u32[]{:S(2)}) copy-start(bf16[64,2048]{1,0:T(8,128)(2,1)} %param.18) | copy-start | bytes 786436
  71.3 17.1 %all-to-all-start = ((bf16[32,2,2048]{2,1,0:T(2,128)(2,1)}), bf16[32,2,2048]{2,1,0:T(2,128)(2,1)S(1)}, u32[]{:S(2)}, u32[]{:S(2)}) async-start(bf16[32,2,2048]{2,1,0:T(2,128)(2,1)} %reshape.395), calls=%async_computation | async-start | bytes 524288 | tf_op jit(solution)/shard_map/all_to_all | solution.py:199
  79.5 83.4 %all-gather.5.cloned.1.call-start = ((), (), s32[]{:S(2)}) async-start(), calls=%async_computation.7 | async-start | bytes 5242880 | tf_op jit(solution)/shard_map/all_gather | solution.py:243
  118.2 150.4 %reduce-scatter.2.cloned.1.call-start = ((), (), s32[]{:S(2)}) async-start(), calls=%async_computation.8 | async-start | bytes 5242880 | tf_op jit(solution)/shard_map/reduce_scatter | solution.py:258
  268.5 24.6 %all-to-all-start.4 = ((bf16[32,8,2048]{2,1,0:T(8,128)(2,1)}), bf16[32,8,2048]{2,1,0:T(8,128)(2,1)S(1)}, u32[]{:S(2)}, u32[]{:S(2)}) async-start(bf16[32,8,2048]{2,1,0:T(8,128)(2,1)} %reduce-scatter.2.cloned.1.call-done), calls=%async_computation.5 | async-start | bytes 2097152 | tf_op jit(solution)/shard_map/all_to_all | solution.py:259
  289.8 9.3 %copy-start.13 = (f32[64,6]{0,1:T(8,128)S(1)}, f32[64,6]{0,1:T(8,128)}, u32[]{:S(2)}) copy-start(f32[64,6]{0,1:T(8,128)} %param.22) | copy-start | bytes 4612
  293.1 58.3 %all-to-all-start.2 = ((bf16[128,8,2048]{2,1,0:T(8,128)(2,1)}), bf16[128,8,2048]{2,1,0:T(8,128)(2,1)}, u32[]{:S(2)}, u32[]{:S(2)}) async-start(bf16[128,8,2048]{2,1,0:T(8,128)(2,1)} %convert_bitcast_fusion.1), calls=%async_computation.2 | async-start | bytes 8388608 | tf_op jit(solution)/shard_map/all_to_all | solution.py:253
  (8 other events, 34.7 us)
Sparse Core Ops, SparseCore 0:
  9.6 55.4 all-gather.2
  118.3 44.5 all-gather.4
  176.3 92.1 reduce-scatter.1

commit v12 on v10

--- a/solution.py
+++ b/solution.py
@@ -230,7 +230,7 @@
     slot_ids = jnp.arange(tensor_size * capacity, dtype=jnp.int32)
     flat_gates = route_gates.reshape(-1)
     for k in range(experts_here):
-        if k == 0:
+        if k == 1:
             fanned = jnp.broadcast_to(outgoing_rows[None, :, k], (group_count,) + outgoing_rows[:, k].shape)
             fanned = fanned.reshape((group_count * tensor_size, capacity, width))
             arrived_rows = lax.all_to_all(

time: 339 us -> 353 us (1.041)
  waiting for transfers between devices: 104 us -> 131 us
  blocking collectives: 109 us -> 88.4 us
  starting transfers between devices: 26.4 us -> 34 us
    all_gather x1, waiting for transfers between devices: 9.52 us -> 46 us  [shards(): arrived_rows = lax.all_gather(same_group, 'dp', axis=0, tiled=True)]
    all_to_all x1 -> x0, blocking collectives: 24.4 us -> none  [shards(): lax.all_to_all(reduced, 'tensor', split_axis=0, concat_axis=0, tiled=True)]
    reduce_scatter x2, waiting for transfers between devices: 60 us -> 50.9 us  [shards(): lax.psum_scatter(partial_value, 'dp', scatter_dimension=0, tiled=True)]
    all_to_all x1 -> x2, starting transfers between devices: 7.36 us -> 15 us  [shards(): lax.all_to_all(reduced, 'tensor', split_axis=0, concat_axis=0, tiled=True)]
    all_to_all x1, blocking collectives: 63.7 us -> 68 us  [shards(): lax.all_to_all(fanned, ('dp', 'tensor'), split_axis=0, concat_axis=0, til...]
    all_to_all x1 -> x2, waiting for transfers between devices: 13.5 us -> 13.5 us  [shards(): lax.all_to_all(reduced, 'tensor', split_axis=0, concat_axis=0, tiled=True)]
  transfers between devices with their start and end apart: 16 -> 17, of which waited for: 9 -> 9; matrix products, arithmetic and copies ran while one was open for 17% -> 12% of each run, Pallas kernels for 4% -> 4%
where the time goes in v12:
time: 353 us; the launch traced here: 351 us
  waiting for transfers between devices  131 us (37%)
  blocking collectives  88.4 us (25%)
  matrix products  36.4 us (10%)
  starting transfers between devices  34 us (10%)
  local copies, waits for them, and re-layouts  21.9 us (6%)
  Pallas kernels  14 us (4%)
  between operations  13.7 us (4%)
  other arithmetic  11.8 us (3%)
    all_to_all x1, blocking collectives, shards(): lax.all_to_all(fanned, ('dp', 'tensor'), split_axis=0, concat_axis=0, til...  68 us
    reduce_scatter x2, waiting for transfers between devices, shards(): lax.psum_scatter(partial_value, 'dp', scatter_dimension=0, tiled=True)  50.9 us
    all_gather x1, waiting for transfers between devices, shards(): arrived_rows = lax.all_gather(same_group, 'dp', axis=0, tiled=True)  46 us
    all_to_all x1, blocking collectives, shards(): lax.all_to_all(outgoing_rows[:, k], 'tensor', split_axis=0, concat_axis=0...  20.4 us
    dot_general x2, matrix products, shards(): jnp.dot(active, expert_down[k], preferred_element_type=jnp.float32)  18.5 us
    all_to_all x2, starting transfers between devices, shards(): lax.all_to_all(reduced, 'tensor', split_axis=0, concat_axis=0, tiled=True)  15 us
    pallas_call x1, Pallas kernels, attention_kernel(): pl.pallas_call(body, grid_spec=grid_spec, out_shape=[jax.ShapeDtypeStruct...  14 us
    all_to_all x2, waiting for transfers between devices, shards(): lax.all_to_all(reduced, 'tensor', split_axis=0, concat_axis=0, tiled=True)  13.5 us
  transfers between devices with their start and end apart: 17, of which 9 were waited for; matrix products, arithmetic and copies ran while one was open for 12% of the time, Pallas kernels for 4%

profile of v12, /device:TPU:0, one launch (start us, length us, event | category | flops | bytes accessed | tf_op | source)
XLA Modules:
  0.0 351.4 jit_solution(5015662398598243154)
XLA Ops:
  9.6 2.8 gather_fusion.1
  24.5 3.6 %collective-permute-done.1 = bf16[256,384]{1,0:T(8,128)(2,1)} collective-permute-done((bf16[256,384]{1,0:T(8,128)(2,1)}, bf16[256,384]{1,0:T(8,128)(2,1)}, u32[]{:S(2)}, u32[]{:S(2)}) %collective-permute-start.1) | collective-permute-done | bytes 196640 | tf_op jit(solution)/shard_map/ppermute | solution.py:156
  31.1 2.8 gather_fusion.3
  35.8 14.0 %shard_map.127 = (f32[4,512,64]{2,1,0:T(8,128)}, f32[4,512,64]{2,1,0:T(8,128)}, f32[4,1,512]{2,1,0:T(1,128)}, f32[4,1,512]{2,1,0:T(1,128)}) custom-call(s32[6]{0:T(128)} %pad_add_fusion.scal_ref, bf16[4,512,128]{2,1,0:T(8,128)(2,1)} %pad_maximum_fusion.1.q_ref, bf16[4,2048,256]{2,1,0:T(8,128)(2,1)} %bitcast.144, bf16[4,256,384]{2,1,0:T(8,128)(2,1)} %copy-done.3), custom_call_target="tpu_custom_call" | custom-call | tf_op jit(solution)/shard_map/pallas_call | solution.py:79
  58.8 2.1 collective-permute-start.8
  61.5 6.1 %collective-permute-done.7 = bf16[512,64]{1,0:T(8,128)(2,1)S(1)} collective-permute-done((bf16[512,64]{1,0:T(8,128)(2,1)S(1)}, bf16[512,64]{1,0:T(8,128)(2,1)S(1)}, u32[]{:S(2)}, u32[]{:S(2)}) %collective-permute-start.7) | collective-permute-done | bytes 65568 | tf_op jit(solution)/shard_map/ppermute | solution.py:194
  70.1 8.1 %all-to-all-start = ((bf16[32,2,2048]{2,1,0:T(2,128)(2,1)}), bf16[32,2,2048]{2,1,0:T(2,128)(2,1)S(1)}, u32[]{:S(2)}, u32[]{:S(2)}) async-start(bf16[32,2,2048]{2,1,0:T(2,128)(2,1)} %reshape.391), calls=%async_computation | async-start | bytes 524288 | tf_op jit(solution)/shard_map/all_to_all | solution.py:199
  78.5 8.7 %all-to-all-done = bf16[32,2,2048]{2,1,0:T(2,128)(2,1)S(1)} async-done(((bf16[32,2,2048]{2,1,0:T(2,128)(2,1)}), bf16[32,2,2048]{2,1,0:T(2,128)(2,1)S(1)}, u32[]{:S(2)}, u32[]{:S(2)}) %all-to-all-start) | async-done | bytes 262176 | tf_op jit(solution)/shard_map/all_to_all | solution.py:199
  88.4 5.1 %multiply_reduce_fusion = (f32[64]{0:T(128)S(1)}, f32[64,2048]{1,0:T(8,128)S(1)}) fusion(bf16[64,2048]{1,0:T(8,128)(2,1)S(1)} %reshape.319, bf16[2048,2048]{1,0:T(8,128)(2,1)} %all-gather.3.cloned.1.call-done, bf16[64,2048]{1,0:T(8,128)(2,1)S(1)} %copy-done.8), kind=kOutput, calls=%fused_computation.52 | convolution fusion | flops 537395136 | bytes 9437440 | tf_op jit(solution)/shard_map/dot_general | solution.py:202
  93.6 2.5 gather_fusion.5
  96.5 20.4 %all_to_all.25 = bf16[32,8,2048]{2,1,0:T(8,128)(2,1)} all-to-all(bf16[32,8,2048]{2,1,0:T(8,128)(2,1)S(1)} %get-tuple-element.21), channel_id=1, replica_groups=mesh['dp'=4,'tensor'=32] {'tensor'}, dimensions={0} | all-to-all | bytes 2097152 | tf_op jit(solution)/shard_map/all_to_all | solution.py:240
  117.0 46.0 %all-gather.5.cloned.1.call-done = bf16[128,8,2048]{2,1,0:T(8,128)(2,1)} async-done(((bf16[32,8,2048]{2,1,0:T(8,128)(2,1)}), bf16[128,8,2048]{2,1,0:T(8,128)(2,1)}) %all-gather.5.cloned.1.call-update) | async-done | bytes 4194320 | tf_op jit(solution)/shard_map/all_gather | solution.py:243
  163.0 4.3 %fusion.6 = f32[1024,352]{0,1:T(8,128)S(1)} fusion(bf16[128,8,2048]{2,1,0:T(8,128)(2,1)} %all-gather.5.cloned.1.call-done, bf16[2,2048,352]{1,2,0:T(8,128)(2,1)} %param.23), kind=kOutput, calls=%fused_computation.13 | convolution fusion | flops 1476395008 | bytes 7077888 | tf_op jit(solution)/shard_map/dot_general | solution.py:245
  167.3 9.0 %convert_bitcast_fusion.1 = bf16[128,8,2048]{2,1,0:T(8,128)(2,1)} fusion(bf16[2,352,2048]{2,1,0:T(8,128)(2,1)} %param.25, bf16[2,2048,352]{1,2,0:T(8,128)(2,1)} %param.24, bf16[128,8,2048]{2,1,0:T(8,128)(2,1)} %all-gather.5.cloned.1.call-done, f32[1024,352]{0,1:T(8,128)S(1)} %fusion.6), kind=kOutput, calls=%fused_computation.16 | convolution fusion | flops 2957049856 | bytes 12713984 | tf_op jit(solution)/shard_map/dot_general | solution.py:248
  176.9 68.0 %all_to_all.26 = bf16[128,8,2048]{2,1,0:T(8,128)(2,1)S(1)} all-to-all(bf16[128,8,2048]{2,1,0:T(8,128)(2,1)S(1)} %bitcast.145), channel_id=1, replica_groups=mesh['dp'=4,'tensor'=32] {'dp','tensor'}, dimensions={0} | all-to-all | bytes 8388608 | tf_op jit(solution)/shard_map/all_to_all | solution.py:236
  246.8 2.8 fusion.2
  249.7 9.5 %convert_bitcast_fusion = bf16[128,8,2048]{2,1,0:T(8,128)(2,1)} fusion(bf16[2,352,2048]{2,1,0:T(8,128)(2,1)} %param.25, bf16[2,2048,352]{1,2,0:T(8,128)(2,1)} %param.24, bf16[128,8,2048]{2,1,0:T(8,128)(2,1)} %copy-done.5, f32[1024,352]{0,1:T(8,128)} %fusion.2), kind=kOutput, calls=%fused_computation.15 | convolution fusion | flops 2957049856 | bytes 12713984 | tf_op jit(solution)/shard_map/dot_general | solution.py:248
  259.2 9.7 %reduce-scatter.3.cloned.1.call-done = bf16[32,8,2048]{2,1,0:T(8,128)(2,1)} async-done(((bf16[128,8,2048]{2,1,0:T(8,128)(2,1)}), bf16[32,8,2048]{2,1,0:T(8,128)(2,1)}) %reduce-scatter.3.cloned.1.call-update) | async-done | bytes 1048592 | tf_op jit(solution)/shard_map/reduce_scatter | solution.py:250
  268.9 7.7 %all-to-all-start.2 = ((bf16[32,8,2048]{2,1,0:T(8,128)(2,1)}), bf16[32,8,2048]{2,1,0:T(8,128)(2,1)}, u32[]{:S(2)}, u32[]{:S(2)}) async-start(bf16[32,8,2048]{2,1,0:T(8,128)(2,1)} %reduce-scatter.3.cloned.1.call-done), calls=%async_computation.3 | async-start | bytes 2097152 | tf_op jit(solution)/shard_map/all_to_all | solution.py:251
  276.6 41.2 %reduce-scatter.5.cloned.1.call-done = bf16[32,8,2048]{2,1,0:T(8,128)(2,1)} async-done(((bf16[128,8,2048]{2,1,0:T(8,128)(2,1)}), bf16[32,8,2048]{2,1,0:T(8,128)(2,1)}) %reduce-scatter.5.cloned.1.call-update) | async-done | bytes 1048592 | tf_op jit(solution)/shard_map/reduce_scatter | solution.py:250
  317.8 7.4 %all-to-all-start.4 = ((bf16[32,8,2048]{2,1,0:T(8,128)(2,1)}), bf16[32,8,2048]{2,1,0:T(8,128)(2,1)}, u32[]{:S(2)}, u32[]{:S(2)}) async-start(bf16[32,8,2048]{2,1,0:T(8,128)(2,1)} %reduce-scatter.5.cloned.1.call-done), calls=%async_computation.6 | async-start | bytes 2097152 | tf_op jit(solution)/shard_map/all_to_all | solution.py:251
  325.7 2.7 fusion.38
  328.4 13.5 %all-to-all-done.4 = bf16[32,8,2048]{2,1,0:T(8,128)(2,1)} async-done(((bf16[32,8,2048]{2,1,0:T(8,128)(2,1)}), bf16[32,8,2048]{2,1,0:T(8,128)(2,1)}, u32[]{:S(2)}, u32[]{:S(2)}) %all-to-all-start.4) | async-done | bytes 1048608 | tf_op jit(solution)/shard_map/all_to_all | solution.py:251
  341.9 3.0 fusion.8
  (128 shorter events, 36.9 us)
Async XLA Ops:
  6.5 24.5 %copy-start = (bf16[192,32,256]{2,1,0:T(8,128)(2,1)S(1)}, bf16[192,32,256]{2,1,0:T(8,128)(2,1)}, u32[]{:S(2)}) copy-start(bf16[192,32,256]{2,1,0:T(8,128)(2,1)} %param.13) | copy-start | bytes 9437188
  6.5 14.4 %copy-start.9 = (s32[4,64]{1,0:T(4,128)S(1)}, s32[4,64]{1,0:T(4,128)}, u32[]{:S(2)}) copy-start(s32[4,64]{1,0:T(4,128)} %param.14) | copy-start | bytes 3076
  6.5 17.0 %copy-start.2 = (s32[16]{0:T(128)S(1)}, s32[16]{0:T(128)}, u32[]{:S(2)}) copy-start(s32[16]{0:T(128)} %param.16) | copy-start | bytes 196
  6.5 81.8 %all-gather.3.cloned.1.call-start = ((), (), s32[]{:S(2)}) async-start(), calls=%async_computation.7 | async-start | bytes 8650752 | tf_op jit(solution)/shard_map/all_gather | solution.py:201
  14.4 10.1 %collective-permute-start.2 = (bf16[256,384]{1,0:T(8,128)(2,1)}, bf16[256,384]{1,0:T(8,128)(2,1)}, u32[]{:S(2)}, u32[]{:S(2)}) collective-permute-start(bf16[256,384]{1,0:T(8,128)(2,1)} %get-tuple-element.27), channel_id=1, source_target_pairs={{0,32},{32,64},{64,96},{96,0},{1,33},{33,65},{65,97},{97,1},{2,34}... | collective-permute-start | bytes 589832 | tf_op jit(solution)/shard_map/ppermute | solution.py:156
  16.1 8.4 %collective-permute-start = (bf16[256,384]{1,0:T(8,128)(2,1)}, bf16[256,384]{1,0:T(8,128)(2,1)}, u32[]{:S(2)}, u32[]{:S(2)}) collective-permute-start(bf16[256,384]{1,0:T(8,128)(2,1)} %get-tuple-element.26), channel_id=1, source_target_pairs={{0,96},{32,0},{64,32},{96,64},{1,97},{33,1},{65,33},{97,65},{2,98}... | collective-permute-start | bytes 589832 | tf_op jit(solution)/shard_map/ppermute | solution.py:156
  17.6 10.5 %collective-permute-start.1 = (bf16[256,384]{1,0:T(8,128)(2,1)}, bf16[256,384]{1,0:T(8,128)(2,1)}, u32[]{:S(2)}, u32[]{:S(2)}) collective-permute-start(bf16[256,384]{1,0:T(8,128)(2,1)} %get-tuple-element.25), channel_id=1, source_target_pairs={{0,64},{32,96},{64,0},{96,32},{1,65},{33,97},{65,1},{97,33},{2,66}... | collective-permute-start | bytes 589832 | tf_op jit(solution)/shard_map/ppermute | solution.py:156
  30.3 3.6 %collective-permute-start.3 = (bf16[4,256,128]{2,1,0:T(8,128)(2,1)S(1)}, bf16[4,256,128]{2,1,0:T(8,128)(2,1)}, u32[]{:S(2)}, u32[]{:S(2)}) collective-permute-start(bf16[4,256,128]{2,1,0:T(8,128)(2,1)S(1)} %slice.92), channel_id=1, source_target_pairs={{0,1},{1,0},{2,3},{3,2},{4,5},{5,4},{6,7},{7,6},{8,9},{9,8},{10,11... | collective-permute-start | bytes 786440 | tf_op jit(solution)/shard_map/ppermute | solution.py:18
  52.5 2.8 collective-permute-start.5
  53.3 2.0 collective-permute-start.4
  53.4 1.9 collective-permute-start.6
  57.8 9.8 %collective-permute-start.7 = (bf16[512,64]{1,0:T(8,128)(2,1)S(1)}, bf16[512,64]{1,0:T(8,128)(2,1)S(1)}, u32[]{:S(2)}, u32[]{:S(2)}) collective-permute-start(bf16[512,64]{1,0:T(8,128)(2,1)S(1)} %get-tuple-element.31), channel_id=1, source_target_pairs={{0,32},{32,64},{64,96},{96,0},{1,33},{33,65},{65,97},{97,1},{2,34}... | collective-permute-start | bytes 196616 | tf_op jit(solution)/shard_map/ppermute | solution.py:194
  58.8 8.8 %collective-permute-start.8 = (bf16[512,64]{1,0:T(8,128)(2,1)S(1)}, bf16[512,64]{1,0:T(8,128)(2,1)S(1)}, u32[]{:S(2)}, u32[]{:S(2)}) collective-permute-start(bf16[512,64]{1,0:T(8,128)(2,1)S(1)} %get-tuple-element.30), channel_id=1, source_target_pairs={{0,64},{32,96},{64,0},{96,32},{1,65},{33,97},{65,1},{97,33},{2,66}... | collective-permute-start | bytes 196616 | tf_op jit(solution)/shard_map/ppermute | solution.py:194
  60.9 7.3 %collective-permute-start.9 = (bf16[512,64]{1,0:T(8,128)(2,1)S(1)}, bf16[512,64]{1,0:T(8,128)(2,1)S(1)}, u32[]{:S(2)}, u32[]{:S(2)}) collective-permute-start(bf16[512,64]{1,0:T(8,128)(2,1)S(1)} %get-tuple-element.29), channel_id=1, source_target_pairs={{0,96},{32,0},{64,32},{96,64},{1,97},{33,1},{65,33},{97,65},{2,98}... | collective-permute-start | bytes 196616 | tf_op jit(solution)/shard_map/ppermute | solution.py:194
  68.2 20.2 %copy-start.8 = (bf16[64,2048]{1,0:T(8,128)(2,1)S(1)}, bf16[64,2048]{1,0:T(8,128)(2,1)}, u32[]{:S(2)}) copy-start(bf16[64,2048]{1,0:T(8,128)(2,1)} %param.18) | copy-start | bytes 786436
  70.1 17.1 %all-to-all-start = ((bf16[32,2,2048]{2,1,0:T(2,128)(2,1)}), bf16[32,2,2048]{2,1,0:T(2,128)(2,1)S(1)}, u32[]{:S(2)}, u32[]{:S(2)}) async-start(bf16[32,2,2048]{2,1,0:T(2,128)(2,1)} %reshape.391), calls=%async_computation | async-start | bytes 524288 | tf_op jit(solution)/shard_map/all_to_all | solution.py:199
  78.3 84.7 %all-gather.5.cloned.1.call-start = ((), (), s32[]{:S(2)}) async-start(), calls=%async_computation.8 | async-start | bytes 5242880 | tf_op jit(solution)/shard_map/all_gather | solution.py:243
  116.9 151.9 %reduce-scatter.3.cloned.1.call-start = ((), (), s32[]{:S(2)}) async-start(), calls=%async_computation.9 | async-start | bytes 5242880 | tf_op jit(solution)/shard_map/reduce_scatter | solution.py:250
  176.3 141.5 %reduce-scatter.5.cloned.1.call-start = ((), (), s32[]{:S(2)}) async-start(), calls=%async_computation.10 | async-start | bytes 5242880 | tf_op jit(solution)/shard_map/reduce_scatter | solution.py:250
  176.9 69.9 %copy-start.17 = (bf16[2,2048,352]{1,2,0:T(8,128)(2,1)S(1)}, bf16[2,2048,352]{1,2,0:T(8,128)(2,1)}, u32[]{:S(2)}) copy-start(bf16[2,2048,352]{1,2,0:T(8,128)(2,1)} %param.23) | copy-start | bytes 8650756
  259.2 66.2 %copy-start.14 = (f32[64,6]{0,1:T(8,128)S(1)}, f32[64,6]{0,1:T(8,128)}, u32[]{:S(2)}) copy-start(f32[64,6]{0,1:T(8,128)} %param.22) | copy-start | bytes 4612
  268.9 48.9 %all-to-all-start.2 = ((bf16[32,8,2048]{2,1,0:T(8,128)(2,1)}), bf16[32,8,2048]{2,1,0:T(8,128)(2,1)}, u32[]{:S(2)}, u32[]{:S(2)}) async-start(bf16[32,8,2048]{2,1,0:T(8,128)(2,1)} %reduce-scatter.3.cloned.1.call-done), calls=%async_computation.3 | async-start | bytes 2097152 | tf_op jit(solution)/shard_map/all_to_all | solution.py:251
  276.6 68.3 %copy-start.1 = (bf16[192,32,256]{2,1,0:T(8,128)(2,1)S(1)}, bf16[192,32,256]{2,1,0:T(8,128)(2,1)}, u32[]{:S(2)}) copy-start(bf16[192,32,256]{2,1,0:T(8,128)(2,1)} %param.13) | copy-start | bytes 9437188
  317.8 24.1 %all-to-all-start.4 = ((bf16[32,8,2048]{2,1,0:T(8,128)(2,1)}), bf16[32,8,2048]{2,1,0:T(8,128)(2,1)}, u32[]{:S(2)}, u32[]{:S(2)}) async-start(bf16[32,8,2048]{2,1,0:T(8,128)(2,1)} %reduce-scatter.5.cloned.1.call-done), calls=%async_computation.6 | async-start | bytes 2097152 | tf_op jit(solution)/shard_map/all_to_all | solution.py:251
  (11 other events, 64.6 us)
Sparse Core Ops, SparseCore 0:
  9.6 55.3 all-gather.2
  117.0 45.8 all-gather.4
  176.4 92.3 reduce-scatter.2
  271.1 46.6 reduce-scatter.4

commit v13 on v10

--- a/solution.py
+++ b/solution.py
@@ -18,12 +18,12 @@
     return lax.ppermute(array, axis, [(i, i ^ 1 << stride) for i in range(lax.axis_size(axis))])
 
 
-def attn_body(scal_ref, q_ref, c_ref, f_ref, lo_ref, hi_ref, m_ref, d_ref, *, block_q, page_rows, head):
+def attn_body(scal_ref, q_ref, c_ref, f_ref, lo_ref, hi_ref, m_ref, d_ref, *, items, block_q, page_rows, head):
     item = pl.program_id(0)
     qb = pl.program_id(1)
     length = scal_ref[item]
-    cache_offset = scal_ref[4]
-    span_offset = scal_ref[5]
+    cache_offset = scal_ref[items]
+    span_offset = scal_ref[items + 1]
     scale = 1.0 / head**0.5
     q = q_ref[...]
     cached = c_ref[...]
@@ -60,7 +60,7 @@
     scal = jnp.concatenate(
         [lengths.astype(jnp.int32), jnp.stack([cache_offset, span_offset]).astype(jnp.int32)]
     )
-    body = functools.partial(attn_body, block_q=block_q, page_rows=page_rows, head=head)
+    body = functools.partial(attn_body, items=items, block_q=block_q, page_rows=page_rows, head=head)
     grid_spec = pltpu.PrefetchScalarGridSpec(
         num_scalar_prefetch=1,
         grid=(items, span // block_q),
@@ -163,20 +163,24 @@
     fresh_per = new_tokens.shape[1] // heads_here
     span_len = fresh_per * split_ways
     rows_per_head = dense_cache.shape[2] // heads_here
-    own_queries = new_tokens[:, :, :HD]
-    other_queries = swapped(own_queries, "tensor", 0)
-    lower_half = jnp.where(side_index == 0, own_queries, other_queries)
-    upper_half = jnp.where(side_index == 0, other_queries, own_queries)
-    queries = jnp.concatenate([lower_half, upper_half], axis=1)[:, None]
-
-    head_results = attention_kernel(
-        queries[:, 0],
-        dense_cache,
-        new_tokens,
-        lengths,
-        side_index * rows_per_head,
-        side_index * fresh_per,
-    )
+    def run_items(fresh_items, cache_items, length_items):
+        own_queries = fresh_items[:, :, :HD]
+        other_queries = swapped(own_queries, "tensor", 0)
+        lower_half = jnp.where(side_index == 0, own_queries, other_queries)
+        upper_half = jnp.where(side_index == 0, other_queries, own_queries)
+        queries = jnp.concatenate([lower_half, upper_half], axis=1)
+        return attention_kernel(
+            queries,
+            cache_items,
+            fresh_items,
+            length_items,
+            side_index * rows_per_head,
+            side_index * fresh_per,
+        )
+
+    local_part = run_items(new_tokens[:1], dense_cache[:1], lengths[:1])
+    moved_part = run_items(new_tokens[1:], dense_cache[1:], lengths[1:])
+    head_results = [jnp.concatenate([x, y], axis=0) for x, y in zip(local_part, moved_part)]
     lower, upper, maximum, denominator = head_results
     half_dim = HD // 2
     given_part = jnp.where(side_index == 0, upper, lower)

time: 339 us -> 348 us (1.027)
  local copies, waits for them, and re-layouts: 21.9 us -> 33.2 us
  waiting for transfers between devices: 104 us -> 99.8 us
    slice x3 -> x6, local copies, waits for them, and re-layouts: 2.3 us -> 7.95 us  [the longest x2 3.94 us: shards(): moved_part = run_items(new_tokens[1:], dense_cache[1:], lengths[1:])]
    ppermute x3, waiting for transfers between devices: 3.81 us -> 0.01 us  [shards(): lax.ppermute(outgoing_tokens[j], 'dp', [(i, (i - j) % group_count) for i...]
    pallas_call x1 -> x2, Pallas kernels: 14 us -> 16.6 us  [attention_kernel(): pl.pallas_call(body, grid_spec=grid_spec, out_shape=[jax.ShapeDtypeStruct...]
  transfers between devices with their start and end apart: 16 -> 17, of which waited for: 9 -> 9; matrix products, arithmetic and copies ran while one was open for 17% -> 20% of each run, Pallas kernels for 4% -> 5%
where the time goes in v13:
time: 348 us; the launch traced here: 345 us
  blocking collectives  109 us (31%)
  waiting for transfers between devices  99.8 us (29%)
  matrix products  37.4 us (11%)
  local copies, waits for them, and re-layouts  33.2 us (10%)
  starting transfers between devices  26.2 us (8%)
  Pallas kernels  16.6 us (5%)
  between operations  13.6 us (4%)
  other arithmetic  9.98 us (3%)
    all_to_all x1, blocking collectives, shards(): lax.all_to_all(fanned, ('dp', 'tensor'), split_axis=0, concat_axis=0, til...  63.7 us
    reduce_scatter x2, waiting for transfers between devices, shards(): lax.psum_scatter(partial_value, 'dp', scatter_dimension=0, tiled=True)  60 us
    all_to_all x1, blocking collectives, shards(): lax.all_to_all(reduced, 'tensor', split_axis=0, concat_axis=0, tiled=True)  24.4 us
    all_to_all x1, blocking collectives, shards(): lax.all_to_all(outgoing_rows[:, k], 'tensor', split_axis=0, concat_axis=0...  20.5 us
    dot_general x2, matrix products, shards(): jnp.dot(active, expert_down[k], preferred_element_type=jnp.float32)  18.9 us
    pallas_call x2, Pallas kernels, attention_kernel(): pl.pallas_call(body, grid_spec=grid_spec, out_shape=[jax.ShapeDtypeStruct...  16.6 us
    all_to_all x1, waiting for transfers between devices, shards(): lax.all_to_all(reduced, 'tensor', split_axis=0, concat_axis=0, tiled=True)  13.5 us
    all_gather x1, waiting for transfers between devices, shards(): arrived_rows = lax.all_gather(same_group, 'dp', axis=0, tiled=True)  9.51 us
  transfers between devices with their start and end apart: 17, of which 9 were waited for; matrix products, arithmetic and copies ran while one was open for 20% of the time, Pallas kernels for 5%

profile of v13, /device:TPU:0, one launch (start us, length us, event | category | flops | bytes accessed | tf_op | source)
XLA Modules:
  0.0 345.5 jit_solution(7565773180804545500)
XLA Ops:
  9.0 2.7 gather_fusion.1
  13.8 3.1 collective-permute-start.1
  23.4 2.8 gather_fusion.3
  26.2 3.9 %slice.118 = bf16[192,32,256]{2,1,0:T(8,128)(2,1)} slice(bf16[256,32,256]{2,1,0:T(8,128)(2,1)} %gather_fusion.3), slice={[64:256], [0:32], [0:256]} | slice | bytes 6291456 | tf_op jit(solution)/shard_map/slice | solution.py:182
  35.9 5.4 %shard_map.127 = (f32[1,512,64]{2,1,0:T(8,128)}, f32[1,512,64]{2,1,0:T(8,128)}, f32[1,1,512]{2,1,0:T(1,128)}, f32[1,1,512]{2,1,0:T(1,128)}) custom-call(s32[3]{0:T(128)} %pad_add_fusion.scal_ref, bf16[1,512,128]{2,1,0:T(8,128)(2,1)} %pad_maximum_fusion.3.q_ref, bf16[1,2048,256]{2,1,0:T(8,128)(2,1)} %bitcast.143, bf16[1,256,384]{2,1,0:T(8,128)(2,1)} %get-tuple-element.36.f_ref), custom_call_target="tpu_custom_call" | custom-call | tf_op jit(solution)/shard_map/pallas_call | solution.py:79
  46.0 11.1 %shard_map.128 = (f32[3,512,64]{2,1,0:T(8,128)}, f32[3,512,64]{2,1,0:T(8,128)}, f32[3,1,512]{2,1,0:T(1,128)}, f32[3,1,512]{2,1,0:T(1,128)}) custom-call(s32[5]{0:T(128)} %pad_add_fusion.1.scal_ref, bf16[3,512,128]{2,1,0:T(8,128)(2,1)} %pad_maximum_fusion.2.q_ref, bf16[3,2048,256]{2,1,0:T(8,128)(2,1)} %bitcast.141, bf16[3,256,384]{2,1,0:T(8,128)(2,1)} %copy-done.4), custom_call_target="tpu_custom_call" | custom-call | tf_op jit(solution)/shard_map/pallas_call | solution.py:79
  72.9 3.2 collective-permute-done.9
  78.1 7.8 %all-to-all-start = ((bf16[32,2,2048]{2,1,0:T(2,128)(2,1)}), bf16[32,2,2048]{2,1,0:T(2,128)(2,1)S(1)}, u32[]{:S(2)}, u32[]{:S(2)}) async-start(bf16[32,2,2048]{2,1,0:T(2,128)(2,1)} %reshape.398), calls=%async_computation | async-start | bytes 524288 | tf_op jit(solution)/shard_map/all_to_all | solution.py:203
  86.4 8.4 %all-to-all-done = bf16[32,2,2048]{2,1,0:T(2,128)(2,1)S(1)} async-done(((bf16[32,2,2048]{2,1,0:T(2,128)(2,1)}), bf16[32,2,2048]{2,1,0:T(2,128)(2,1)S(1)}, u32[]{:S(2)}, u32[]{:S(2)}) %all-to-all-start) | async-done | bytes 262176 | tf_op jit(solution)/shard_map/all_to_all | solution.py:203
  96.1 5.1 %multiply_reduce_fusion = (f32[64]{0:T(128)S(1)}, f32[64,2048]{1,0:T(8,128)S(1)}) fusion(bf16[64,2048]{1,0:T(8,128)(2,1)S(1)} %reshape.323, bf16[2048,2048]{1,0:T(8,128)(2,1)} %all-gather.3.cloned.1.call-done, bf16[64,2048]{1,0:T(8,128)(2,1)S(1)} %copy-done.6), kind=kOutput, calls=%fused_computation.51 | convolution fusion | flops 537395136 | bytes 9437440 | tf_op jit(solution)/shard_map/dot_general | solution.py:206
  104.1 20.5 %all_to_all.25 = bf16[32,8,2048]{2,1,0:T(8,128)(2,1)} all-to-all(bf16[32,8,2048]{2,1,0:T(8,128)(2,1)S(1)} %get-tuple-element.28), channel_id=1, replica_groups=mesh['dp'=4,'tensor'=32] {'tensor'}, dimensions={0} | all-to-all | bytes 2097152 | tf_op jit(solution)/shard_map/all_to_all | solution.py:244
  125.2 63.7 %all_to_all.26 = bf16[128,8,2048]{2,1,0:T(8,128)(2,1)S(1)} all-to-all(bf16[128,8,2048]{2,1,0:T(8,128)(2,1)S(1)} %bitcast.140), channel_id=1, replica_groups=mesh['dp'=4,'tensor'=32] {'dp','tensor'}, dimensions={0} | all-to-all | bytes 8388608 | tf_op jit(solution)/shard_map/all_to_all | solution.py:240
  190.9 2.8 fusion.6
  193.7 9.5 %convert_bitcast_fusion.1 = bf16[128,8,2048]{2,1,0:T(8,128)(2,1)} fusion(bf16[2,352,2048]{2,1,0:T(8,128)(2,1)} %param.25, bf16[2,2048,352]{1,2,0:T(8,128)(2,1)} %param.24, bf16[128,8,2048]{2,1,0:T(8,128)(2,1)} %copy-done.5, f32[1024,352]{0,1:T(8,128)} %fusion.6), kind=kOutput, calls=%fused_computation.16 | convolution fusion | flops 2957049856 | bytes 12713984 | tf_op jit(solution)/shard_map/dot_general | solution.py:252
  203.5 9.5 %all-gather.5.cloned.1.call-done = bf16[128,8,2048]{2,1,0:T(8,128)(2,1)} async-done(((bf16[32,8,2048]{2,1,0:T(8,128)(2,1)}), bf16[128,8,2048]{2,1,0:T(8,128)(2,1)}) %all-gather.5.cloned.1.call-update) | async-done | bytes 4194320 | tf_op jit(solution)/shard_map/all_gather | solution.py:247
  213.0 5.0 %fusion.2 = f32[1024,352]{0,1:T(8,128)} fusion(bf16[128,8,2048]{2,1,0:T(8,128)(2,1)} %all-gather.5.cloned.1.call-done, bf16[2,2048,352]{1,2,0:T(8,128)(2,1)S(1)} %copy-done.16), kind=kOutput, calls=%fused_computation.9 | convolution fusion | flops 1476395008 | bytes 7077888 | tf_op jit(solution)/shard_map/dot_general | solution.py:249
  218.0 9.4 %convert_bitcast_fusion = bf16[128,8,2048]{2,1,0:T(8,128)(2,1)} fusion(bf16[2,352,2048]{2,1,0:T(8,128)(2,1)} %param.25, bf16[2,2048,352]{1,2,0:T(8,128)(2,1)} %param.24, bf16[128,8,2048]{2,1,0:T(8,128)(2,1)} %all-gather.5.cloned.1.call-done, f32[1024,352]{0,1:T(8,128)} %fusion.2), kind=kOutput, calls=%fused_computation.15 | convolution fusion | flops 2957049856 | bytes 12713984 | tf_op jit(solution)/shard_map/dot_general | solution.py:252
  227.4 35.5 %reduce-scatter.3.cloned.1.call-done = bf16[32,8,2048]{2,1,0:T(8,128)(2,1)} async-done(((bf16[128,8,2048]{2,1,0:T(8,128)(2,1)}), bf16[32,8,2048]{2,1,0:T(8,128)(2,1)}) %reduce-scatter.3.cloned.1.call-update) | async-done | bytes 1048592 | tf_op jit(solution)/shard_map/reduce_scatter | solution.py:254
  263.0 24.4 %all_to_all.27 = bf16[32,8,2048]{2,1,0:T(8,128)(2,1)} all-to-all(bf16[32,8,2048]{2,1,0:T(8,128)(2,1)} %reduce-scatter.3.cloned.1.call-done), channel_id=1, replica_groups=mesh['dp'=4,'tensor'=32] {'tensor'}, dimensions={0} | all-to-all | bytes 2097152 | tf_op jit(solution)/shard_map/all_to_all | solution.py:255
  287.3 24.5 %reduce-scatter.5.cloned.1.call-done = bf16[32,8,2048]{2,1,0:T(8,128)(2,1)} async-done(((bf16[128,8,2048]{2,1,0:T(8,128)(2,1)}), bf16[32,8,2048]{2,1,0:T(8,128)(2,1)}) %reduce-scatter.5.cloned.1.call-update) | async-done | bytes 1048592 | tf_op jit(solution)/shard_map/reduce_scatter | solution.py:254
  311.8 7.4 %all-to-all-start.4 = ((bf16[32,8,2048]{2,1,0:T(8,128)(2,1)}), bf16[32,8,2048]{2,1,0:T(8,128)(2,1)}, u32[]{:S(2)}, u32[]{:S(2)}) async-start(bf16[32,8,2048]{2,1,0:T(8,128)(2,1)} %reduce-scatter.5.cloned.1.call-done), calls=%async_computation.6 | async-start | bytes 2097152 | tf_op jit(solution)/shard_map/all_to_all | solution.py:255
  319.7 2.7 fusion.38
  322.4 13.5 %all-to-all-done.4 = bf16[32,8,2048]{2,1,0:T(8,128)(2,1)} async-done(((bf16[32,8,2048]{2,1,0:T(8,128)(2,1)}), bf16[32,8,2048]{2,1,0:T(8,128)(2,1)}, u32[]{:S(2)}, u32[]{:S(2)}) %all-to-all-start.4) | async-done | bytes 1048608 | tf_op jit(solution)/shard_map/all_to_all | solution.py:255
  336.0 3.0 fusion.8
  (143 shorter events, 47.0 us)
Async XLA Ops:
  6.5 16.8 %copy-start = (bf16[192,32,256]{2,1,0:T(8,128)(2,1)S(1)}, bf16[192,32,256]{2,1,0:T(8,128)(2,1)}, u32[]{:S(2)}) copy-start(bf16[192,32,256]{2,1,0:T(8,128)(2,1)} %param.13) | copy-start | bytes 9437188
  6.5 13.8 %copy-start.17 = (s32[16]{0:T(128)S(1)}, s32[16]{0:T(128)}, u32[]{:S(2)}) copy-start(s32[16]{0:T(128)} %param.15) | copy-start | bytes 196
  6.5 14.6 %copy-start.7 = (s32[4,64]{1,0:T(4,128)S(1)}, s32[4,64]{1,0:T(4,128)}, u32[]{:S(2)}) copy-start(s32[4,64]{1,0:T(4,128)} %param.14) | copy-start | bytes 3076
  6.5 89.5 %all-gather.3.cloned.1.call-start = ((), (), s32[]{:S(2)}) async-start(), calls=%async_computation.7 | async-start | bytes 8650752 | tf_op jit(solution)/shard_map/all_gather | solution.py:205
  13.8 27.6 %collective-permute-start.1 = (bf16[256,384]{1,0:T(8,128)(2,1)}, bf16[256,384]{1,0:T(8,128)(2,1)S(1)}, u32[]{:S(2)}, u32[]{:S(2)}) collective-permute-start(bf16[256,384]{1,0:T(8,128)(2,1)} %get-tuple-element.34), channel_id=1, source_target_pairs={{0,96},{32,0},{64,32},{96,64},{1,97},{33,1},{65,33},{97,65},{2,98}... | collective-permute-start | bytes 589832 | tf_op jit(solution)/shard_map/ppermute | solution.py:156
  16.9 24.4 %collective-permute-start.2 = (bf16[256,384]{1,0:T(8,128)(2,1)}, bf16[256,384]{1,0:T(8,128)(2,1)}, u32[]{:S(2)}, u32[]{:S(2)}) collective-permute-start(bf16[256,384]{1,0:T(8,128)(2,1)} %get-tuple-element.35), channel_id=1, source_target_pairs={{0,64},{32,96},{64,0},{96,32},{1,65},{33,97},{65,1},{97,33},{2,66}... | collective-permute-start | bytes 589832 | tf_op jit(solution)/shard_map/ppermute | solution.py:156
  17.5 23.8 %collective-permute-start.3 = (bf16[256,384]{1,0:T(8,128)(2,1)}, bf16[256,384]{1,0:T(8,128)(2,1)}, u32[]{:S(2)}, u32[]{:S(2)}) collective-permute-start(bf16[256,384]{1,0:T(8,128)(2,1)} %get-tuple-element.37), channel_id=1, source_target_pairs={{0,32},{32,64},{64,96},{96,0},{1,33},{33,65},{65,97},{97,1},{2,34}... | collective-permute-start | bytes 589832 | tf_op jit(solution)/shard_map/ppermute | solution.py:156
  20.0 14.4 %collective-permute-start = (bf16[1,256,128]{2,1,0:T(8,128)(2,1)}, bf16[1,256,128]{2,1,0:T(8,128)(2,1)}, u32[]{:S(2)}, u32[]{:S(2)}) collective-permute-start(bf16[1,256,128]{2,1,0:T(8,128)(2,1)} %slice.111), channel_id=1, source_target_pairs={{0,1},{1,0},{2,3},{3,2},{4,5},{5,4},{6,7},{7,6},{8,9},{9,8},{10,11... | collective-permute-start | bytes 196616 | tf_op jit(solution)/shard_map/ppermute | solution.py:18
  42.5 2.6 collective-permute-start.4
  60.9 2.7 collective-permute-start.6
  61.0 2.6 collective-permute-start.5
  61.6 2.0 collective-permute-start.7
  66.1 6.8 %collective-permute-start.8 = (bf16[512,64]{1,0:T(8,128)(2,1)S(1)}, bf16[512,64]{1,0:T(8,128)(2,1)S(1)}, u32[]{:S(2)}, u32[]{:S(2)}) collective-permute-start(bf16[512,64]{1,0:T(8,128)(2,1)S(1)} %get-tuple-element.41), channel_id=1, source_target_pairs={{0,32},{32,64},{64,96},{96,0},{1,33},{33,65},{65,97},{97,1},{2,34}... | collective-permute-start | bytes 196616 | tf_op jit(solution)/shard_map/ppermute | solution.py:198
  67.7 8.4 %collective-permute-start.9 = (bf16[512,64]{1,0:T(8,128)(2,1)S(1)}, bf16[512,64]{1,0:T(8,128)(2,1)S(1)}, u32[]{:S(2)}, u32[]{:S(2)}) collective-permute-start(bf16[512,64]{1,0:T(8,128)(2,1)S(1)} %get-tuple-element.40), channel_id=1, source_target_pairs={{0,64},{32,96},{64,0},{96,32},{1,65},{33,97},{65,1},{97,33},{2,66}... | collective-permute-start | bytes 196616 | tf_op jit(solution)/shard_map/ppermute | solution.py:198
  69.5 6.7 %collective-permute-start.10 = (bf16[512,64]{1,0:T(8,128)(2,1)S(1)}, bf16[512,64]{1,0:T(8,128)(2,1)S(1)}, u32[]{:S(2)}, u32[]{:S(2)}) collective-permute-start(bf16[512,64]{1,0:T(8,128)(2,1)S(1)} %get-tuple-element.39), channel_id=1, source_target_pairs={{0,96},{32,0},{64,32},{96,64},{1,97},{33,1},{65,33},{97,65},{2,98}... | collective-permute-start | bytes 196616 | tf_op jit(solution)/shard_map/ppermute | solution.py:198
  76.2 19.8 %copy-start.6 = (bf16[64,2048]{1,0:T(8,128)(2,1)S(1)}, bf16[64,2048]{1,0:T(8,128)(2,1)}, u32[]{:S(2)}) copy-start(bf16[64,2048]{1,0:T(8,128)(2,1)} %param.18) | copy-start | bytes 786436
  78.1 16.7 %all-to-all-start = ((bf16[32,2,2048]{2,1,0:T(2,128)(2,1)}), bf16[32,2,2048]{2,1,0:T(2,128)(2,1)S(1)}, u32[]{:S(2)}, u32[]{:S(2)}) async-start(bf16[32,2,2048]{2,1,0:T(2,128)(2,1)} %reshape.398), calls=%async_computation | async-start | bytes 524288 | tf_op jit(solution)/shard_map/all_to_all | solution.py:203
  85.9 127.1 %all-gather.5.cloned.1.call-start = ((), (), s32[]{:S(2)}) async-start(), calls=%async_computation.9 | async-start | bytes 5242880 | tf_op jit(solution)/shard_map/all_gather | solution.py:247
  124.6 138.4 %reduce-scatter.3.cloned.1.call-start = ((), (), s32[]{:S(2)}) async-start(), calls=%async_computation.8 | async-start | bytes 5242880 | tf_op jit(solution)/shard_map/reduce_scatter | solution.py:254
  125.2 65.7 %copy-start.16 = (bf16[2,2048,352]{1,2,0:T(8,128)(2,1)S(1)}, bf16[2,2048,352]{1,2,0:T(8,128)(2,1)}, u32[]{:S(2)}) copy-start(bf16[2,2048,352]{1,2,0:T(8,128)(2,1)} %param.23) | copy-start | bytes 8650756
  203.2 108.6 %reduce-scatter.5.cloned.1.call-start = ((), (), s32[]{:S(2)}) async-start(), calls=%async_computation.10 | async-start | bytes 5242880 | tf_op jit(solution)/shard_map/reduce_scatter | solution.py:254
  227.4 92.0 %copy-start.14 = (f32[64,6]{0,1:T(8,128)S(1)}, f32[64,6]{0,1:T(8,128)}, u32[]{:S(2)}) copy-start(f32[64,6]{0,1:T(8,128)} %param.22) | copy-start | bytes 4612
  263.0 76.0 %copy-start.1 = (bf16[192,32,256]{2,1,0:T(8,128)(2,1)S(1)}, bf16[192,32,256]{2,1,0:T(8,128)(2,1)}, u32[]{:S(2)}) copy-start(bf16[192,32,256]{2,1,0:T(8,128)(2,1)} %param.13) | copy-start | bytes 9437188
  311.8 24.1 %all-to-all-start.4 = ((bf16[32,8,2048]{2,1,0:T(8,128)(2,1)}), bf16[32,8,2048]{2,1,0:T(8,128)(2,1)}, u32[]{:S(2)}, u32[]{:S(2)}) async-start(bf16[32,8,2048]{2,1,0:T(8,128)(2,1)} %reduce-scatter.5.cloned.1.call-done), calls=%async_computation.6 | async-start | bytes 2097152 | tf_op jit(solution)/shard_map/all_to_all | solution.py:255
  (11 other events, 50.3 us)
Sparse Core Ops, SparseCore 0:
  9.6 55.3 all-gather.2
  124.7 88.2 all-gather.4
  215.4 47.4 reduce-scatter.2
  265.2 46.5 reduce-scatter.4
